TPU v7x, 512 devices: a whole 4x8x8 slice. The times are simulated.
512 devices in a mesh: src: 16 (over y_hi, x, core), rcv: 32 (over y_lo, z).
Axes of the slice: x: 4, y: 8 (y_hi: 2, y_lo: 4; y = y_hi * 4 + y_lo), z: 8, core: 2. Of those that a mesh axis runs over, the one named last changes fastest.
Arguments:
- observed: bfloat16 [1024, 1024, 64], P('src', 'rcv'), may hold values from -6 to 6
- estimate: bfloat16 [1024, 1024, 64], P('src', 'rcv'), may hold values from -6 to 6
- acquired: int32 [8, 8], replicated, may hold values 0 or 1
- levels: int32 [2, 64], replicated, may hold values from 1 to 3, as said below
- thresholds: float32 [64], replicated, may hold values from 0.05 to 0.6
Outputs:
- refined: float32 [1024, 1024, 64], P('src', 'rcv')
Inputs may be any that keep to these rules, and one draw needn't show every extreme that they name: `levels`: in each time sample one of the two entries equals 3 and the other is smaller.
All inputs are finite; a program needn't handle non-finite values.
Results may differ from a plain program's by a relative error of at most 0.0015.
Values may be sent and summed in bfloat16 or wider, within the bound.
No kernel may reach another device: no remote copies, remote signals or barrier semaphores. Data moves between devices by JAX's collectives and lax.ppermute only.
A program may use at most 64 MiB of HBM per device.

v0:
```python
import functools

import jax
import jax.numpy as jnp
from jax import lax
from jax.sharding import PartitionSpec as P
from jax.experimental import pallas as pl
from jax.experimental.pallas import tpu as pltpu

LEVELS = 3
SRC_HALO = 16
RCV_HALO = 24


def split_pairs(field, stride):
    length = field.shape[0]
    shaped = field.reshape((length // (2 * stride), 2, stride) + field.shape[1:])
    return (shaped, shaped[:, :, 0])


def join_pairs(shaped, new_pairs, field):
    joined = jnp.concatenate([new_pairs[:, :, None], shaped[:, :, 1:]], axis=2)
    return joined.reshape(field.shape)


def forward_core(pair_rows, first, last):
    even_part = pair_rows[:, 0]
    odd_part = pair_rows[:, 1]
    next_even = jnp.concatenate([even_part[1:], even_part[-1:]], axis=0)
    next_even = jnp.where(last, even_part, next_even)
    detail = odd_part - 0.5 * (even_part + next_even)
    prev_detail = jnp.concatenate([detail[:1], detail[:-1]], axis=0)
    prev_detail = jnp.where(first, detail, prev_detail)
    smooth = even_part + 0.25 * (prev_detail + detail)
    return jnp.stack([smooth, detail], axis=1)


def inverse_core(pair_rows, first, last):
    smooth = pair_rows[:, 0]
    detail = pair_rows[:, 1]
    prev_detail = jnp.concatenate([detail[:1], detail[:-1]], axis=0)
    prev_detail = jnp.where(first, detail, prev_detail)
    even_part = smooth - 0.25 * (prev_detail + detail)
    next_even = jnp.concatenate([even_part[1:], even_part[-1:]], axis=0)
    next_even = jnp.where(last, even_part, next_even)
    odd_part = detail + 0.5 * (even_part + next_even)
    return jnp.stack([even_part, odd_part], axis=1)


def level(field, stride, enabled, forward, width, length, is_first, is_last):
    shaped, pair_rows = split_pairs(field, stride)
    pair_ids = jnp.arange(pair_rows.shape[0], dtype=jnp.int32).reshape(
        (-1,) + (1,) * (pair_rows.ndim - 2)
    )
    first = is_first & (pair_ids == width // (2 * stride))
    last = is_last & (pair_ids == (width + length) // (2 * stride) - 1)
    core = forward_core if forward else inverse_core
    new_pairs = core(pair_rows, first, last)
    return jnp.where(enabled, join_pairs(shaped, new_pairs, field), field)


PAD = 8


def _lift_level(work, stride, enabled, forward, width, length, ends):
    rows = work.shape[0] - 2 * PAD
    pairs = rows // (2 * stride)
    step = 2 * stride
    pair_ids = lax.broadcasted_iota(jnp.int32, (pairs,) + work.shape[1:], 0)
    first = (pair_ids == width // step) & (ends[0] != 0)
    last = (pair_ids == (width + length) // step - 1) & (ends[1] != 0)
    evens = pl.ds(PAD, pairs, stride=step)
    odds = pl.ds(PAD + stride, pairs, stride=step)
    next_evens = pl.ds(PAD + step, pairs, stride=step)
    prev_odds = pl.ds(PAD - stride, pairs, stride=step)
    if forward:
        even_part = work[evens]
        odd_part = work[odds]
        next_even = jnp.where(last, even_part, work[next_evens])
        detail = odd_part - 0.5 * (even_part + next_even)
        work[odds] = jnp.where(enabled, detail, odd_part)
        prev_detail = jnp.where(first, detail, work[prev_odds])
        smooth = even_part + 0.25 * (prev_detail + detail)
        work[evens] = jnp.where(enabled, smooth, even_part)
    else:
        smooth = work[evens]
        detail = work[odds]
        prev_detail = jnp.where(first, detail, work[prev_odds])
        even_part = smooth - 0.25 * (prev_detail + detail)
        work[evens] = jnp.where(enabled, even_part, smooth)
        next_even = jnp.where(last, even_part, work[next_evens])
        odd_part = detail + 0.5 * (even_part + next_even)
        work[odds] = jnp.where(enabled, odd_part, detail)


def _stage_kernel(*refs, kind, width, length):
    if kind == "fwd":
        ends_ref, depth_ref, left_ref, right_ref, out_ref, work = refs
    elif kind == "both":
        ends_ref, depth_ref, thr_ref, in_ref, out_ref, work = refs
    else:
        ends_ref, depth_ref, in_ref, out_ref, work = refs
    rows = work.shape[0] - 2 * PAD
    ends = (ends_ref[0], ends_ref[1])
    depth = depth_ref[...]
    if kind == "fwd":
        work[PAD : PAD + rows] = 0.5 * (
            left_ref[...].astype(jnp.float32) + right_ref[...].astype(jnp.float32)
        )
    else:
        work[PAD : PAD + rows] = in_ref[...]
    if kind != "inv":
        for depth_index in range(LEVELS):
            _lift_level(work, 2**depth_index, depth > depth_index, True, width, length, ends)
    if kind == "both":
        field = work[PAD : PAD + rows]
        thr = thr_ref[...]
        work[PAD : PAD + rows] = field - jnp.clip(field, -thr, thr)
    if kind != "fwd":
        for depth_index in reversed(range(LEVELS)):
            _lift_level(work, 2**depth_index, depth > depth_index, False, width, length, ends)
    out_ref[...] = work[PAD + width : PAD + width + length]


def lift_stage(kind, operands, ends, depth, width, length):
    rows, cols, samples = operands[-1].shape
    kernel = functools.partial(_stage_kernel, kind=kind, width=width, length=length)
    smem = pl.BlockSpec(memory_space=pltpu.SMEM)
    vmem = pl.BlockSpec(memory_space=pltpu.VMEM)
    return pl.pallas_call(
        kernel,
        out_shape=jax.ShapeDtypeStruct((length, cols, samples), jnp.float32),
        in_specs=[smem] + [vmem] * (1 + len(operands)),
        out_specs=vmem,
        scratch_shapes=[pltpu.VMEM((rows + 2 * PAD, cols, samples), jnp.float32)],
    )(ends, depth, *operands)


def extend(cells, axis_name, dim, width):
    count = lax.axis_size(axis_name)
    length = cells.shape[dim]
    head = lax.slice_in_dim(cells, 0, width, axis=dim)
    tail = lax.slice_in_dim(cells, length - width, length, axis=dim)
    from_left = lax.ppermute(tail, axis_name, [(i, i + 1) for i in range(count - 1)])
    from_right = lax.ppermute(head, axis_name, [(i + 1, i) for i in range(count - 1)])
    return jnp.concatenate([from_left, cells, from_right], axis=dim)


def body(observed, estimate, acquired, levels, thresholds):
    src_count = lax.axis_size("src")
    rcv_count = lax.axis_size("rcv")
    src_index = lax.axis_index("src")
    rcv_index = lax.axis_index("rcv")
    row_count, col_count, samples = observed.shape
    extent = row_count * src_count
    blocks = acquired.shape[0]
    block_size = extent // blocks
    block_ids = jnp.arange(blocks, dtype=jnp.int32)
    row_ids = src_index * row_count + jnp.arange(row_count, dtype=jnp.int32)
    col_ids = rcv_index * col_count + jnp.arange(col_count, dtype=jnp.int32)
    pick_rows = (row_ids[:, None] // block_size == block_ids[None, :]).astype(jnp.float32)
    pick_cols = (col_ids[:, None] // block_size == block_ids[None, :]).astype(jnp.float32)
    row_mask = jnp.dot(pick_rows, acquired.astype(jnp.float32), precision=lax.Precision.HIGHEST)
    local_mask = jnp.dot(row_mask, pick_cols.T, precision=lax.Precision.HIGHEST)
    est_float = estimate.astype(jnp.float32)
    merged = (
        est_float + local_mask[:, :, None] * (observed.astype(jnp.float32) - est_float)
    ).astype(jnp.bfloat16)

    ratio = rcv_count // src_count
    pieces = merged.reshape(ratio, col_count, col_count, samples)
    own_part = rcv_index % ratio
    received = []
    for shift in range(ratio):
        perm = []
        for a in range(src_count):
            for b in range(rcv_count):
                part = (b % ratio + shift) % ratio
                perm.append((a * rcv_count + b, (b // ratio) * rcv_count + a * ratio + part))
        send = lax.dynamic_index_in_dim(pieces, (own_part + shift) % ratio, axis=0, keepdims=False)
        received.append(lax.ppermute(send, ("src", "rcv"), perm))
    received = jnp.stack(received)
    slots = []
    for slot in range(ratio):
        got = lax.dynamic_index_in_dim(received, (own_part - slot) % ratio, axis=0, keepdims=False)
        slots.append(jnp.transpose(got, (1, 0, 2)))
    mirror = jnp.concatenate(slots, axis=0)

    samples_shape = (1, 1, samples)
    src_depth = levels[0].reshape(samples_shape)
    rcv_depth = levels[1].reshape(samples_shape)
    src_ends = jnp.stack([src_index == 0, src_index == src_count - 1]).astype(jnp.int32)
    rcv_ends = jnp.stack([rcv_index == 0, rcv_index == rcv_count - 1]).astype(jnp.int32)

    merged_wide = extend(merged, "src", 0, SRC_HALO)
    mirror_wide = extend(mirror, "src", 0, SRC_HALO)
    coeff = lift_stage("fwd", (merged_wide, mirror_wide), src_ends, src_depth, SRC_HALO, row_count)

    wide = jnp.moveaxis(extend(coeff, "rcv", 1, RCV_HALO), 1, 0)
    turned = lift_stage(
        "both", (thresholds.reshape(samples_shape), wide), rcv_ends, rcv_depth, RCV_HALO, col_count
    )
    coeff = jnp.moveaxis(turned, 0, 1)

    wide = extend(coeff, "src", 0, SRC_HALO)
    return lift_stage("inv", (wide,), src_ends, src_depth, SRC_HALO, row_count)

def solution(mesh):
    return jax.shard_map(
        body,
        mesh=mesh,
        in_specs=(P("src", "rcv", None), P("src", "rcv", None), P(), P(), P()),
        out_specs=P("src", "rcv", None),
        check_vma=False,
    )
```

profile of v0, /device:TPU:23, one launch (start us, length us, event | category | flops | bytes accessed | tf_op | source)
XLA Modules:
  0.0 147.5 jit_solution(12096718065946713376)
XLA Ops:
  0.0 0.0 copy-start
  0.0 0.9 fusion.6
  0.9 0.2 fusion.8
  1.1 1.5 %fusion.1 = bf16[64,32,64]{2,1,0:T(8,128)(2,1)S(1)} fusion(bf16[64,32,64]{2,1,0:T(8,128)(2,1)} %param.6, bf16[64,32,64]{2,1,0:T(8,128)(2,1)} %param.5, f32[64,32]{1,0:T(8,128)S(1)} %fusion.8), kind=kLoop, calls=%fused_computation.5 | loop fusion | flops 786432 | bytes 794624 | tf_op jit(solution)/shard_map/convert_element_type | solution.py:168
  2.7 6.1 %collective-permute-start = (bf16[16,32,64]{2,1,0:T(8,128)(2,1)S(1)}, bf16[16,32,64]{2,1,0:T(8,128)(2,1)S(1)}, u32[]{:S(2)}, u32[]{:S(2)}) collective-permute-start(bf16[16,32,64]{2,1,0:T(8,128)(2,1)S(1)} %get-tuple-element.13), channel_id=1, source_target_pairs={{0,32},{32,64},{64,96},{96,128},{128,160},{160,192},{192,224},{224... | collective-permute-start | bytes 196616 | tf_op jit(solution)/shard_map/ppermute | solution.py:144
  8.9 1.9 %collective-permute-start.1 = (bf16[16,32,64]{2,1,0:T(8,128)(2,1)S(1)}, bf16[16,32,64]{2,1,0:T(8,128)(2,1)S(1)}, u32[]{:S(2)}, u32[]{:S(2)}) collective-permute-start(bf16[16,32,64]{2,1,0:T(8,128)(2,1)S(1)} %get-tuple-element.14), channel_id=1, source_target_pairs={{32,0},{64,32},{96,64},{128,96},{160,128},{192,160},{224,192},{256... | collective-permute-start | bytes 196616 | tf_op jit(solution)/shard_map/ppermute | solution.py:145
  10.9 0.1 copy.19
  11.0 18.0 %collective-permute-start.2 = (bf16[32,32,64]{2,0,1:T(8,128)(2,1)S(1)}, bf16[32,32,64]{2,0,1:T(8,128)(2,1)S(1)}, u32[]{:S(2)}, u32[]{:S(2)}) collective-permute-start(bf16[32,32,64]{2,0,1:T(8,128)(2,1)S(1)} %bitcast.37), channel_id=1, source_target_pairs={{0,0},{1,1},{2,32},{3,33},{4,64},{5,65},{6,96},{7,97},{8,128},{9,1... | collective-permute-start | bytes 393224 | tf_op jit(solution)/shard_map/ppermute | solution.py:181
  29.0 0.1 copy.18
  29.1 1.9 %collective-permute-start.3 = (bf16[32,32,64]{2,0,1:T(8,128)(2,1)S(1)}, bf16[32,32,64]{2,0,1:T(8,128)(2,1)S(1)}, u32[]{:S(2)}, u32[]{:S(2)}) collective-permute-start(bf16[32,32,64]{2,0,1:T(8,128)(2,1)S(1)} %bitcast.38), channel_id=1, source_target_pairs={{0,1},{1,0},{2,33},{3,32},{4,65},{5,64},{6,97},{7,96},{8,129},{9,1... | collective-permute-start | bytes 393224 | tf_op jit(solution)/shard_map/ppermute | solution.py:181
  31.1 0.0 copy-done
  31.1 0.5 slice_bitcast_fusion
  31.6 0.6 add_convert_fusion.refs_0_
  32.3 12.7 %collective-permute-done.2 = bf16[32,32,64]{2,0,1:T(8,128)(2,1)S(1)} collective-permute-done((bf16[32,32,64]{2,0,1:T(8,128)(2,1)S(1)}, bf16[32,32,64]{2,0,1:T(8,128)(2,1)S(1)}, u32[]{:S(2)}, u32[]{:S(2)}) %collective-permute-start.2) | collective-permute-done | bytes 131104 | tf_op jit(solution)/shard_map/ppermute | solution.py:181
  44.9 22.5 %collective-permute-done.3 = bf16[32,32,64]{2,0,1:T(8,128)(2,1)S(1)} collective-permute-done((bf16[32,32,64]{2,0,1:T(8,128)(2,1)S(1)}, bf16[32,32,64]{2,0,1:T(8,128)(2,1)S(1)}, u32[]{:S(2)}, u32[]{:S(2)}) %collective-permute-start.3) | collective-permute-done | bytes 131104 | tf_op jit(solution)/shard_map/ppermute | solution.py:181
  67.4 0.3 fusion.5
  67.7 9.6 %collective-permute-start.5 = (bf16[16,32,64]{2,1,0:T(8,128)(2,1)S(1)}, bf16[16,32,64]{2,1,0:T(8,128)(2,1)S(1)}, u32[]{:S(2)}, u32[]{:S(2)}) collective-permute-start(bf16[16,32,64]{2,1,0:T(8,128)(2,1)S(1)} %slice.43), channel_id=1, source_target_pairs={{32,0},{64,32},{96,64},{128,96},{160,128},{192,160},{224,192},{256... | collective-permute-start | bytes 196616 | tf_op jit(solution)/shard_map/ppermute | solution.py:145
  77.4 1.9 %collective-permute-start.4 = (bf16[16,32,64]{2,1,0:T(8,128)(2,1)S(1)}, bf16[16,32,64]{2,1,0:T(8,128)(2,1)S(1)}, u32[]{:S(2)}, u32[]{:S(2)}) collective-permute-start(bf16[16,32,64]{2,1,0:T(8,128)(2,1)S(1)} %slice.42), channel_id=1, source_target_pairs={{0,32},{32,64},{64,96},{96,128},{128,160},{160,192},{192,224},{224... | collective-permute-start | bytes 196616 | tf_op jit(solution)/shard_map/ppermute | solution.py:144
  79.3 0.0 collective-permute-done
  79.3 0.0 collective-permute-done.1
  79.3 1.1 pad_maximum_fusion.1.refs_2_
  80.4 0.0 collective-permute-done.5
  80.4 0.8 collective-permute-done.4
  81.2 1.1 pad_maximum_fusion.2.refs_3_
  82.3 3.6 %shard_map.55 = f32[64,32,64]{2,1,0:T(8,128)} custom-call(s32[2]{0:T(128)} %add_convert_fusion.refs_0_, s32[1,1,64]{2,1,0:T(1,128)} %get-tuple-element.16.refs_1_, bf16[96,32,64]{2,1,0:T(8,128)(2,1)} %pad_maximum_fusion.1.refs_2_, bf16[96,32,64]{2,1,0:T(8,128)(2,1)} %pad_maximum_fusion.2.refs_3_), custom_call_target="tpu_custom_call" | custom-call | tf_op jit(solution)/shard_map/pallas_call | solution.py:130
  86.0 1.8 %copy.9 = f32[64,32,64]{2,0,1:T(8,128)S(1)} copy(f32[64,32,64]{2,1,0:T(8,128)} %shard_map.55) | data formatting | bytes 1048576 | tf_op jit(solution)/shard_map/pallas_call | solution.py:130
  87.8 1.1 fusion.12
  88.9 6.0 %collective-permute-start.6 = (f32[64,24,64]{2,0,1:T(8,128)}, f32[64,24,64]{2,0,1:T(8,128)S(1)}, u32[]{:S(2)}, u32[]{:S(2)}) collective-permute-start(f32[64,24,64]{2,0,1:T(8,128)} %get-tuple-element.7), channel_id=1, source_target_pairs={{0,1},{1,2},{2,3},{3,4},{4,5},{5,6},{6,7},{7,8},{8,9},{9,10},{10,1... | collective-permute-start | bytes 1179656 | tf_op jit(solution)/shard_map/ppermute | solution.py:144
  94.9 1.9 %collective-permute-start.7 = (f32[64,24,64]{2,0,1:T(8,128)S(1)}, f32[64,24,64]{2,0,1:T(8,128)S(1)}, u32[]{:S(2)}, u32[]{:S(2)}) collective-permute-start(f32[64,24,64]{2,0,1:T(8,128)S(1)} %get-tuple-element.8), channel_id=1, source_target_pairs={{1,0},{2,1},{3,2},{4,3},{5,4},{6,5},{7,6},{8,7},{9,8},{10,9},{11,1... | collective-permute-start | bytes 1179656 | tf_op jit(solution)/shard_map/ppermute | solution.py:145
  96.8 0.6 add_convert_fusion.1.refs_0_
  97.4 13.7 %collective-permute-done.6 = f32[64,24,64]{2,0,1:T(8,128)S(1)} collective-permute-done((f32[64,24,64]{2,0,1:T(8,128)}, f32[64,24,64]{2,0,1:T(8,128)S(1)}, u32[]{:S(2)}, u32[]{:S(2)}) %collective-permute-start.6) | collective-permute-done | bytes 393248 | tf_op jit(solution)/shard_map/ppermute | solution.py:144
  111.1 3.8 %collective-permute-done.7 = f32[64,24,64]{2,0,1:T(8,128)S(1)} collective-permute-done((f32[64,24,64]{2,0,1:T(8,128)S(1)}, f32[64,24,64]{2,0,1:T(8,128)S(1)}, u32[]{:S(2)}, u32[]{:S(2)}) %collective-permute-start.7) | collective-permute-done | bytes 393248 | tf_op jit(solution)/shard_map/ppermute | solution.py:145
  114.9 1.7 %maximum_bitcast_fusion.refs_3_ = f32[80,64,64]{2,1,0:T(8,128)} fusion(f32[64,24,64]{2,0,1:T(8,128)S(1)} %collective-permute-done.7, f32[64,32,64]{2,0,1:T(8,128)S(1)} %copy.9, f32[64,24,64]{2,0,1:T(8,128)S(1)} %collective-permute-done.6), kind=kLoop, calls=%fused_computation | loop fusion | flops 655360 | bytes 2621440 | tf_op jit(solution)/shard_map/transpose | solution.py:199
  116.6 6.2 %shard_map.56 = f32[32,64,64]{2,1,0:T(8,128)} custom-call(s32[2]{0:T(128)} %add_convert_fusion.1.refs_0_, s32[1,1,64]{2,1,0:T(1,128)} %get-tuple-element.15.refs_1_, f32[1,1,64]{2,1,0:T(1,128)} %bitcast.39, f32[80,64,64]{2,1,0:T(8,128)} %maximum_bitcast_fusion.refs_3_), custom_call_target="tpu_custom_call" | custom-call | tf_op jit(solution)/shard_map/pallas_call | solution.py:130
  122.8 1.8 %copy.17 = f32[32,64,64]{2,0,1:T(8,128)S(1)} copy(f32[32,64,64]{2,1,0:T(8,128)} %shard_map.56) | data formatting | bytes 1048576 | tf_op jit(solution)/shard_map/pallas_call | solution.py:130
  124.6 4.5 %collective-permute-start.8 = (f32[16,32,64]{2,1,0:T(8,128)S(1)}, f32[16,32,64]{2,1,0:T(8,128)S(1)}, u32[]{:S(2)}, u32[]{:S(2)}) collective-permute-start(f32[16,32,64]{2,1,0:T(8,128)S(1)} %get-tuple-element.5), channel_id=1, source_target_pairs={{0,32},{32,64},{64,96},{96,128},{128,160},{160,192},{192,224},{224... | collective-permute-start | bytes 393224 | tf_op jit(solution)/shard_map/ppermute | solution.py:144
  129.2 1.9 %collective-permute-start.9 = (f32[16,32,64]{2,1,0:T(8,128)S(1)}, f32[16,32,64]{2,1,0:T(8,128)S(1)}, u32[]{:S(2)}, u32[]{:S(2)}) collective-permute-start(f32[16,32,64]{2,1,0:T(8,128)S(1)} %get-tuple-element.6), channel_id=1, source_target_pairs={{32,0},{64,32},{96,64},{128,96},{160,128},{192,160},{224,192},{256... | collective-permute-start | bytes 393224 | tf_op jit(solution)/shard_map/ppermute | solution.py:145
  131.1 1.4 collective-permute-done.8
  132.5 10.4 %collective-permute-done.9 = f32[16,32,64]{2,1,0:T(8,128)S(1)} collective-permute-done((f32[16,32,64]{2,1,0:T(8,128)S(1)}, f32[16,32,64]{2,1,0:T(8,128)S(1)}, u32[]{:S(2)}, u32[]{:S(2)}) %collective-permute-start.9) | collective-permute-done | bytes 131104 | tf_op jit(solution)/shard_map/ppermute | solution.py:145
  142.9 1.3 pad_maximum_fusion.refs_2_
  144.2 3.3 %shard_map.57 = f32[64,32,64]{2,1,0:T(8,128)} custom-call(s32[2]{0:T(128)} %add_convert_fusion.refs_0_, s32[1,1,64]{2,1,0:T(1,128)} %get-tuple-element.16.refs_1_, f32[96,32,64]{2,1,0:T(8,128)} %pad_maximum_fusion.refs_2_), custom_call_target="tpu_custom_call" | custom-call | tf_op jit(solution)/shard_map/pallas_call | solution.py:130
  (7 shorter events, 0.1 us)
Async XLA Ops:
  0.0 31.1 %copy-start = (s32[2,64]{1,0:T(2,128)S(1)}, s32[2,64]{1,0:T(2,128)}, u32[]{:S(2)}) copy-start(s32[2,64]{1,0:T(2,128)} %param.8) | copy-start | bytes 1540
  2.7 76.6 %collective-permute-start = (bf16[16,32,64]{2,1,0:T(8,128)(2,1)S(1)}, bf16[16,32,64]{2,1,0:T(8,128)(2,1)S(1)}, u32[]{:S(2)}, u32[]{:S(2)}) collective-permute-start(bf16[16,32,64]{2,1,0:T(8,128)(2,1)S(1)} %get-tuple-element.13), channel_id=1, source_target_pairs={{0,32},{32,64},{64,96},{96,128},{128,160},{160,192},{192,224},{224... | collective-permute-start | bytes 196616 | tf_op jit(solution)/shard_map/ppermute | solution.py:144
  8.9 70.5 %collective-permute-start.1 = (bf16[16,32,64]{2,1,0:T(8,128)(2,1)S(1)}, bf16[16,32,64]{2,1,0:T(8,128)(2,1)S(1)}, u32[]{:S(2)}, u32[]{:S(2)}) collective-permute-start(bf16[16,32,64]{2,1,0:T(8,128)(2,1)S(1)} %get-tuple-element.14), channel_id=1, source_target_pairs={{32,0},{64,32},{96,64},{128,96},{160,128},{192,160},{224,192},{256... | collective-permute-start | bytes 196616 | tf_op jit(solution)/shard_map/ppermute | solution.py:145
  11.0 33.9 %collective-permute-start.2 = (bf16[32,32,64]{2,0,1:T(8,128)(2,1)S(1)}, bf16[32,32,64]{2,0,1:T(8,128)(2,1)S(1)}, u32[]{:S(2)}, u32[]{:S(2)}) collective-permute-start(bf16[32,32,64]{2,0,1:T(8,128)(2,1)S(1)} %bitcast.37), channel_id=1, source_target_pairs={{0,0},{1,1},{2,32},{3,33},{4,64},{5,65},{6,96},{7,97},{8,128},{9,1... | collective-permute-start | bytes 393224 | tf_op jit(solution)/shard_map/ppermute | solution.py:181
  29.1 38.3 %collective-permute-start.3 = (bf16[32,32,64]{2,0,1:T(8,128)(2,1)S(1)}, bf16[32,32,64]{2,0,1:T(8,128)(2,1)S(1)}, u32[]{:S(2)}, u32[]{:S(2)}) collective-permute-start(bf16[32,32,64]{2,0,1:T(8,128)(2,1)S(1)} %bitcast.38), channel_id=1, source_target_pairs={{0,1},{1,0},{2,33},{3,32},{4,65},{5,64},{6,97},{7,96},{8,129},{9,1... | collective-permute-start | bytes 393224 | tf_op jit(solution)/shard_map/ppermute | solution.py:181
  67.7 12.7 %collective-permute-start.5 = (bf16[16,32,64]{2,1,0:T(8,128)(2,1)S(1)}, bf16[16,32,64]{2,1,0:T(8,128)(2,1)S(1)}, u32[]{:S(2)}, u32[]{:S(2)}) collective-permute-start(bf16[16,32,64]{2,1,0:T(8,128)(2,1)S(1)} %slice.43), channel_id=1, source_target_pairs={{32,0},{64,32},{96,64},{128,96},{160,128},{192,160},{224,192},{256... | collective-permute-start | bytes 196616 | tf_op jit(solution)/shard_map/ppermute | solution.py:145
  77.4 3.9 %collective-permute-start.4 = (bf16[16,32,64]{2,1,0:T(8,128)(2,1)S(1)}, bf16[16,32,64]{2,1,0:T(8,128)(2,1)S(1)}, u32[]{:S(2)}, u32[]{:S(2)}) collective-permute-start(bf16[16,32,64]{2,1,0:T(8,128)(2,1)S(1)} %slice.42), channel_id=1, source_target_pairs={{0,32},{32,64},{64,96},{96,128},{128,160},{160,192},{192,224},{224... | collective-permute-start | bytes 196616 | tf_op jit(solution)/shard_map/ppermute | solution.py:144
  88.9 22.2 %collective-permute-start.6 = (f32[64,24,64]{2,0,1:T(8,128)}, f32[64,24,64]{2,0,1:T(8,128)S(1)}, u32[]{:S(2)}, u32[]{:S(2)}) collective-permute-start(f32[64,24,64]{2,0,1:T(8,128)} %get-tuple-element.7), channel_id=1, source_target_pairs={{0,1},{1,2},{2,3},{3,4},{4,5},{5,6},{6,7},{7,8},{8,9},{9,10},{10,1... | collective-permute-start | bytes 1179656 | tf_op jit(solution)/shard_map/ppermute | solution.py:144
  94.9 20.0 %collective-permute-start.7 = (f32[64,24,64]{2,0,1:T(8,128)S(1)}, f32[64,24,64]{2,0,1:T(8,128)S(1)}, u32[]{:S(2)}, u32[]{:S(2)}) collective-permute-start(f32[64,24,64]{2,0,1:T(8,128)S(1)} %get-tuple-element.8), channel_id=1, source_target_pairs={{1,0},{2,1},{3,2},{4,3},{5,4},{6,5},{7,6},{8,7},{9,8},{10,9},{11,1... | collective-permute-start | bytes 1179656 | tf_op jit(solution)/shard_map/ppermute | solution.py:145
  124.6 7.8 %collective-permute-start.8 = (f32[16,32,64]{2,1,0:T(8,128)S(1)}, f32[16,32,64]{2,1,0:T(8,128)S(1)}, u32[]{:S(2)}, u32[]{:S(2)}) collective-permute-start(f32[16,32,64]{2,1,0:T(8,128)S(1)} %get-tuple-element.5), channel_id=1, source_target_pairs={{0,32},{32,64},{64,96},{96,128},{128,160},{160,192},{192,224},{224... | collective-permute-start | bytes 393224 | tf_op jit(solution)/shard_map/ppermute | solution.py:144
  129.2 13.7 %collective-permute-start.9 = (f32[16,32,64]{2,1,0:T(8,128)S(1)}, f32[16,32,64]{2,1,0:T(8,128)S(1)}, u32[]{:S(2)}, u32[]{:S(2)}) collective-permute-start(f32[16,32,64]{2,1,0:T(8,128)S(1)} %get-tuple-element.6), channel_id=1, source_target_pairs={{32,0},{64,32},{96,64},{128,96},{160,128},{192,160},{224,192},{256... | collective-permute-start | bytes 393224 | tf_op jit(solution)/shard_map/ppermute | solution.py:145
where the time goes:
time: 148 us
  waiting for transfers between devices  65.3 us (44%)
  starting transfers between devices  53.9 us (36%)
  Pallas kernels  13.1 us (9%)
  other arithmetic  8.29 us (6%)
  local copies, waits for them, and re-layouts  5.61 us (4%)
    ppermute x2, waiting for transfers between devices, body(): received.append(lax.ppermute(send, ('src', 'rcv'), perm))  35.2 us
    ppermute x2, starting transfers between devices, body(): received.append(lax.ppermute(send, ('src', 'rcv'), perm))  19.9 us
    ppermute x4, starting transfers between devices, extend(): lax.ppermute(tail, axis_name, [(i, i + 1) for i in range(count - 1)])  18.6 us
    ppermute x4, waiting for transfers between devices, extend(): lax.ppermute(tail, axis_name, [(i, i + 1) for i in range(count - 1)])  15.9 us
    ppermute x4, starting transfers between devices, extend(): lax.ppermute(head, axis_name, [(i + 1, i) for i in range(count - 1)])  15.4 us
    ppermute x4, waiting for transfers between devices, extend(): lax.ppermute(head, axis_name, [(i + 1, i) for i in range(count - 1)])  14.2 us
    pallas_call x3, Pallas kernels, lift_stage(): pl.pallas_call(kernel, out_shape=jax.ShapeDtypeStruct((length, cols, samp...  13.1 us
    pallas_call x2, local copies, waits for them, and re-layouts, lift_stage(): pl.pallas_call(kernel, out_shape=jax.ShapeDtypeStruct((length, cols, samp...  3.67 us
  transfers between devices with their start and end apart: 10, of which 7 were waited for; matrix products, arithmetic and copies ran while one was open for 2% of the time, Pallas kernels for 0%

commit v1 on v0

--- a/solution.py
+++ b/solution.py
@@ -93,7 +93,7 @@
         work[odds] = jnp.where(enabled, odd_part, detail)
 
 
-def _stage_kernel(*refs, kind, width, length):
+def _stage_kernel(*refs, kind, width, length, out_from, out_rows):
     if kind == "fwd":
         ends_ref, depth_ref, left_ref, right_ref, out_ref, work = refs
     elif kind == "both":
@@ -119,17 +119,19 @@
     if kind != "fwd":
         for depth_index in reversed(range(LEVELS)):
             _lift_level(work, 2**depth_index, depth > depth_index, False, width, length, ends)
-    out_ref[...] = work[PAD + width : PAD + width + length]
-
-
-def lift_stage(kind, operands, ends, depth, width, length):
+    out_ref[...] = work[PAD + out_from : PAD + out_from + out_rows]
+
+
+def lift_stage(kind, operands, ends, depth, width, length, out_from, out_rows):
     rows, cols, samples = operands[-1].shape
-    kernel = functools.partial(_stage_kernel, kind=kind, width=width, length=length)
+    kernel = functools.partial(
+        _stage_kernel, kind=kind, width=width, length=length, out_from=out_from, out_rows=out_rows
+    )
     smem = pl.BlockSpec(memory_space=pltpu.SMEM)
     vmem = pl.BlockSpec(memory_space=pltpu.VMEM)
     return pl.pallas_call(
         kernel,
-        out_shape=jax.ShapeDtypeStruct((length, cols, samples), jnp.float32),
+        out_shape=jax.ShapeDtypeStruct((out_rows, cols, samples), jnp.float32),
         in_specs=[smem] + [vmem] * (1 + len(operands)),
         out_specs=vmem,
         scratch_shapes=[pltpu.VMEM((rows + 2 * PAD, cols, samples), jnp.float32)],
@@ -167,24 +169,30 @@
         est_float + local_mask[:, :, None] * (observed.astype(jnp.float32) - est_float)
     ).astype(jnp.bfloat16)
 
-    ratio = rcv_count // src_count
-    pieces = merged.reshape(ratio, col_count, col_count, samples)
-    own_part = rcv_index % ratio
-    received = []
-    for shift in range(ratio):
-        perm = []
-        for a in range(src_count):
-            for b in range(rcv_count):
-                part = (b % ratio + shift) % ratio
-                perm.append((a * rcv_count + b, (b // ratio) * rcv_count + a * ratio + part))
-        send = lax.dynamic_index_in_dim(pieces, (own_part + shift) % ratio, axis=0, keepdims=False)
-        received.append(lax.ppermute(send, ("src", "rcv"), perm))
-    received = jnp.stack(received)
+    assert rcv_count == 2 * src_count and row_count == 2 * col_count
+    mirror_halo = col_count
+    pieces = merged.reshape(2, col_count, col_count, samples)
+    own_part = rcv_index % 2
+    everyone = ("src", "rcv")
+    received = {}
+    for c in range(2):
+        for r in range(2):
+            perm = []
+            for a in range(src_count):
+                for b in range(rcv_count):
+                    q = (b + 1) % 2 + 2 * r
+                    if (b + 1 - q) % 2 == 0 and 0 <= (b + 1 - q) // 2 < src_count:
+                        target = ((b + 1 - q) // 2) * rcv_count + 2 * a + (b + c) % 2
+                        perm.append((a * rcv_count + b, target))
+            send = jnp.where((own_part + c) % 2 == 0, pieces[0], pieces[1])
+            received[c, r] = lax.ppermute(send, everyone, perm)
     slots = []
-    for slot in range(ratio):
-        got = lax.dynamic_index_in_dim(received, (own_part - slot) % ratio, axis=0, keepdims=False)
+    for q in range(4):
+        even_c = (1 - q % 2) % 2
+        got = jnp.where(own_part == 0, received[even_c, q // 2], received[1 - even_c, q // 2])
         slots.append(jnp.transpose(got, (1, 0, 2)))
-    mirror = jnp.concatenate(slots, axis=0)
+    mirror_wide = jnp.concatenate(slots, axis=0)
+    merged_wide = extend(merged, "src", 0, mirror_halo)
 
     samples_shape = (1, 1, samples)
     src_depth = levels[0].reshape(samples_shape)
@@ -192,18 +200,18 @@
     src_ends = jnp.stack([src_index == 0, src_index == src_count - 1]).astype(jnp.int32)
     rcv_ends = jnp.stack([rcv_index == 0, rcv_index == rcv_count - 1]).astype(jnp.int32)
 
-    merged_wide = extend(merged, "src", 0, SRC_HALO)
-    mirror_wide = extend(mirror, "src", 0, SRC_HALO)
-    coeff = lift_stage("fwd", (merged_wide, mirror_wide), src_ends, src_depth, SRC_HALO, row_count)
+    coeff = lift_stage(
+        "fwd", (merged_wide, mirror_wide), src_ends, src_depth, mirror_halo, row_count,
+        mirror_halo - SRC_HALO, row_count + 2 * SRC_HALO,
+    )
 
     wide = jnp.moveaxis(extend(coeff, "rcv", 1, RCV_HALO), 1, 0)
     turned = lift_stage(
-        "both", (thresholds.reshape(samples_shape), wide), rcv_ends, rcv_depth, RCV_HALO, col_count
+        "both", (thresholds.reshape(samples_shape), wide), rcv_ends, rcv_depth, RCV_HALO, col_count,
+        RCV_HALO, col_count,
     )
     coeff = jnp.moveaxis(turned, 0, 1)
-
-    wide = extend(coeff, "src", 0, SRC_HALO)
-    return lift_stage("inv", (wide,), src_ends, src_depth, SRC_HALO, row_count)
+    return lift_stage("inv", (coeff,), src_ends, src_depth, SRC_HALO, row_count, SRC_HALO, row_count)
 
 def solution(mesh):
     return jax.shard_map(

time: 148 us -> 177 us (1.20)
  the two profiles are of different devices: /device:TPU:23 before, /device:TPU:3 now
where the time goes in v1:
time: 177 us
  waiting for transfers between devices  101 us (57%)
  starting transfers between devices  33.1 us (19%)
  local copies, waits for them, and re-layouts  17.4 us (10%)
  Pallas kernels  16.4 us (9%)
  other arithmetic  8.09 us (5%)
    ppermute x4, waiting for transfers between devices, body(): received[c, r] = lax.ppermute(send, everyone, perm)  88.7 us
    ppermute x4, starting transfers between devices, body(): received[c, r] = lax.ppermute(send, everyone, perm)  21.4 us
    pallas_call x3, Pallas kernels, lift_stage(): pl.pallas_call(kernel, out_shape=jax.ShapeDtypeStruct((out_rows, cols, sa...  16.4 us
    ppermute x2, waiting for transfers between devices, extend(): lax.ppermute(head, axis_name, [(i + 1, i) for i in range(count - 1)])  10.5 us
    ppermute x2, starting transfers between devices, extend(): lax.ppermute(tail, axis_name, [(i, i + 1) for i in range(count - 1)])  8.15 us
    pallas_call x2, local copies, waits for them, and re-layouts, lift_stage(): pl.pallas_call(kernel, out_shape=jax.ShapeDtypeStruct((out_rows, cols, sa...  4.4 us
    slice x2, local copies, waits for them, and re-layouts, extend(): tail = lax.slice_in_dim(cells, length - width, length, axis=dim)  4.09 us
    ppermute x2, starting transfers between devices, extend(): lax.ppermute(head, axis_name, [(i + 1, i) for i in range(count - 1)])  3.56 us
  transfers between devices with their start and end apart: 8, of which 5 were waited for; matrix products, arithmetic and copies ran while one was open for 4% of the time, Pallas kernels for 0%

profile of v1, /device:TPU:3, one launch (start us, length us, event | category | flops | bytes accessed | tf_op | source)
XLA Modules:
  0.0 176.8 jit_solution(17137292376665645984)
XLA Ops:
  0.0 0.9 fusion.2
  0.9 0.2 fusion.4
  1.1 0.0 copy-start.1
  1.1 1.6 fusion.1
  2.8 0.1 broadcast_select_fusion.1
  2.9 1.3 collective-permute-start.4
  4.2 11.8 %collective-permute-start.2 = (bf16[32,32,64]{2,0,1:T(8,128)(2,1)S(1)}, bf16[32,32,64]{2,0,1:T(8,128)(2,1)S(1)}, u32[]{:S(2)}, u32[]{:S(2)}) collective-permute-start(bf16[32,32,64]{2,0,1:T(8,128)(2,1)S(1)} %get-tuple-element.11), channel_id=1, source_target_pairs={{0,1},{1,32},{2,33},{3,64},{4,65},{5,96},{6,97},{7,128},{8,129},{9... | collective-permute-start | bytes 393224 | tf_op jit(solution)/shard_map/ppermute | solution.py:188
  16.0 2.3 %collective-permute-start.1 = (bf16[32,32,64]{2,0,1:T(8,128)(2,1)S(1)}, bf16[32,32,64]{2,0,1:T(8,128)(2,1)S(1)}, u32[]{:S(2)}, u32[]{:S(2)}) collective-permute-start(bf16[32,32,64]{2,0,1:T(8,128)(2,1)S(1)} %get-tuple-element.13), channel_id=1, source_target_pairs={{32,0},{64,32},{96,64},{128,96},{160,128},{192,160},{224,192},{256... | collective-permute-start | bytes 393224 | tf_op jit(solution)/shard_map/ppermute | solution.py:147
  18.3 3.3 %collective-permute-start = (bf16[32,32,64]{2,0,1:T(8,128)(2,1)S(1)}, bf16[32,32,64]{2,0,1:T(8,128)(2,1)S(1)}, u32[]{:S(2)}, u32[]{:S(2)}) collective-permute-start(bf16[32,32,64]{2,0,1:T(8,128)(2,1)S(1)} %get-tuple-element.14), channel_id=1, source_target_pairs={{0,32},{32,64},{64,96},{96,128},{128,160},{160,192},{192,224},{224... | collective-permute-start | bytes 393224 | tf_op jit(solution)/shard_map/ppermute | solution.py:146
  21.6 1.3 collective-permute-start.5
  22.9 0.0 copy-done.1
  22.9 0.5 slice_bitcast_fusion
  23.4 0.7 add_convert_fusion.refs_0_
  24.1 0.0 collective-permute-done.1
  24.1 6.9 %collective-permute-start.3 = (bf16[32,32,64]{2,0,1:T(8,128)(2,1)S(1)}, bf16[32,32,64]{2,0,1:T(8,128)(2,1)S(1)}, u32[]{:S(2)}, u32[]{:S(2)}) collective-permute-start(bf16[32,32,64]{2,0,1:T(8,128)(2,1)S(1)} %get-tuple-element.12), channel_id=1, source_target_pairs={{0,0},{1,33},{2,32},{3,65},{4,64},{5,97},{6,96},{7,129},{8,128},{9... | collective-permute-start | bytes 393224 | tf_op jit(solution)/shard_map/ppermute | solution.py:188
  31.0 0.0 collective-permute-done
  31.1 0.3 pad_maximum_fusion
  31.3 1.6 copy.15.refs_2_
  33.0 52.5 %collective-permute-done.4 = bf16[32,32,64]{2,0,1:T(8,128)(2,1)S(1)} collective-permute-done((bf16[32,32,64]{2,0,1:T(8,128)(2,1)S(1)}, bf16[32,32,64]{2,0,1:T(8,128)(2,1)S(1)}, u32[]{:S(2)}, u32[]{:S(2)}) %collective-permute-start.4) | collective-permute-done | bytes 131104 | tf_op jit(solution)/shard_map/ppermute | solution.py:188
  85.5 0.0 collective-permute-done.5
  85.5 33.3 %collective-permute-done.2 = bf16[32,32,64]{2,0,1:T(8,128)(2,1)S(1)} collective-permute-done((bf16[32,32,64]{2,0,1:T(8,128)(2,1)S(1)}, bf16[32,32,64]{2,0,1:T(8,128)(2,1)S(1)}, u32[]{:S(2)}, u32[]{:S(2)}) %collective-permute-start.2) | collective-permute-done | bytes 131104 | tf_op jit(solution)/shard_map/ppermute | solution.py:188
  118.8 2.9 %collective-permute-done.3 = bf16[32,32,64]{2,0,1:T(8,128)(2,1)S(1)} collective-permute-done((bf16[32,32,64]{2,0,1:T(8,128)(2,1)S(1)}, bf16[32,32,64]{2,0,1:T(8,128)(2,1)S(1)}, u32[]{:S(2)}, u32[]{:S(2)}) %collective-permute-start.3) | collective-permute-done | bytes 131104 | tf_op jit(solution)/shard_map/ppermute | solution.py:188
  121.7 1.2 pad_maximum_fusion.1.refs_3_
  123.0 4.5 %shard_map.55 = f32[96,32,64]{2,1,0:T(8,128)} custom-call(s32[2]{0:T(128)} %add_convert_fusion.refs_0_, s32[1,1,64]{2,1,0:T(1,128)} %get-tuple-element.16.refs_1_, bf16[128,32,64]{2,1,0:T(8,128)(2,1)} %copy.15.refs_2_, bf16[128,32,64]{2,1,0:T(8,128)(2,1)} %pad_maximum_fusion.1.refs_3_), custom_call_target="tpu_custom_call" | custom-call | tf_op jit(solution)/shard_map/pallas_call | solution.py:132
  127.4 2.8 %fusion.7 = (f32[96,24,64]{2,1,0:T(8,128)S(1)}, f32[96,24,64]{2,1,0:T(8,128)}) fusion(f32[96,32,64]{2,1,0:T(8,128)} %shard_map.55), kind=kLoop, calls=%fused_computation.33 | loop fusion | bytes 2359296 | tf_op jit(solution)/shard_map/slice | solution.py:145
  130.2 0.0 copy-start
  130.2 2.6 %copy.17 = f32[96,24,64]{0,2,1:T(8,128)} copy(f32[96,24,64]{2,1,0:T(8,128)} %get-tuple-element.6) | data formatting | bytes 1179648 | tf_op jit(solution)/shard_map/slice | solution.py:144
  132.9 1.3 collective-permute-start.7
  134.2 1.3 copy.16
  135.4 4.9 %collective-permute-start.6 = (f32[96,24,64]{0,2,1:T(8,128)}, f32[96,24,64]{0,2,1:T(8,128)}, u32[]{:S(2)}, u32[]{:S(2)}) collective-permute-start(f32[96,24,64]{0,2,1:T(8,128)} %copy.16), channel_id=1, source_target_pairs={{0,1},{1,2},{2,3},{3,4},{4,5},{5,6},{6,7},{7,8},{8,9},{9,10},{10,1... | collective-permute-start | bytes 1769480 | tf_op jit(solution)/shard_map/ppermute | solution.py:146
  140.3 0.6 add_convert_fusion.1.refs_0_
  140.9 0.0 copy-done
  140.9 0.9 copy.19
  141.9 10.5 %collective-permute-done.7 = f32[96,24,64]{0,2,1:T(8,128)} collective-permute-done((f32[96,24,64]{0,2,1:T(8,128)}, f32[96,24,64]{0,2,1:T(8,128)}, u32[]{:S(2)}, u32[]{:S(2)}) %collective-permute-start.7) | collective-permute-done | bytes 589856 | tf_op jit(solution)/shard_map/ppermute | solution.py:147
  152.4 1.5 copy.20
  153.9 1.5 collective-permute-done.6
  155.4 2.5 %copy.18 = f32[96,24,64]{2,0,1:T(8,128)} copy(f32[96,24,64]{0,2,1:T(8,128)} %collective-permute-done.6) | data formatting | bytes 1179648 | tf_op jit(solution)/shard_map/ppermute | solution.py:146
  157.9 3.5 %maximum_bitcast_fusion.refs_3_ = f32[80,96,64]{2,1,0:T(8,128)} fusion(f32[96,24,64]{2,0,1:T(8,128)S(1)} %copy.20, f32[96,32,64]{2,0,1:T(8,128)S(1)} %copy.19, f32[96,24,64]{2,0,1:T(8,128)} %copy.18), kind=kLoop, calls=%fused_computation | loop fusion | flops 983040 | bytes 3932160 | tf_op jit(solution)/shard_map/transpose | solution.py:208
  161.4 8.6 %shard_map.56 = f32[32,96,64]{2,1,0:T(8,128)} custom-call(s32[2]{0:T(128)} %add_convert_fusion.1.refs_0_, s32[1,1,64]{2,1,0:T(1,128)} %get-tuple-element.15.refs_1_, f32[1,1,64]{2,1,0:T(1,128)} %bitcast.24, f32[80,96,64]{2,1,0:T(8,128)} %maximum_bitcast_fusion.refs_3_), custom_call_target="tpu_custom_call" | custom-call | tf_op jit(solution)/shard_map/pallas_call | solution.py:132
  170.0 3.5 %copy.25 = f32[32,96,64]{2,0,1:T(8,128)} copy(f32[32,96,64]{2,1,0:T(8,128)} %shard_map.56) | data formatting | bytes 1572864 | tf_op jit(solution)/shard_map/pallas_call | solution.py:132
  173.5 3.3 %shard_map.57 = f32[64,32,64]{2,1,0:T(8,128)} custom-call(s32[2]{0:T(128)} %add_convert_fusion.refs_0_, s32[1,1,64]{2,1,0:T(1,128)} %get-tuple-element.16.refs_1_, f32[96,32,64]{2,1,0:T(8,128)} %bitcast.23), custom_call_target="tpu_custom_call" | custom-call | tf_op jit(solution)/shard_map/pallas_call | solution.py:132
  (4 shorter events, 0.1 us)
Async XLA Ops:
  1.1 21.8 %copy-start.1 = (s32[2,64]{1,0:T(2,128)S(1)}, s32[2,64]{1,0:T(2,128)}, u32[]{:S(2)}) copy-start(s32[2,64]{1,0:T(2,128)} %param.8) | copy-start | bytes 1540
  2.9 82.6 %collective-permute-start.4 = (bf16[32,32,64]{2,0,1:T(8,128)(2,1)S(1)}, bf16[32,32,64]{2,0,1:T(8,128)(2,1)S(1)}, u32[]{:S(2)}, u32[]{:S(2)}) collective-permute-start(bf16[32,32,64]{2,0,1:T(8,128)(2,1)S(1)} %get-tuple-element.11), channel_id=1, source_target_pairs={{1,0},{2,1},{3,32},{4,33},{5,64},{6,65},{7,96},{8,97},{9,128},{10,... | collective-permute-start | bytes 393224 | tf_op jit(solution)/shard_map/ppermute | solution.py:188
  4.2 114.6 %collective-permute-start.2 = (bf16[32,32,64]{2,0,1:T(8,128)(2,1)S(1)}, bf16[32,32,64]{2,0,1:T(8,128)(2,1)S(1)}, u32[]{:S(2)}, u32[]{:S(2)}) collective-permute-start(bf16[32,32,64]{2,0,1:T(8,128)(2,1)S(1)} %get-tuple-element.11), channel_id=1, source_target_pairs={{0,1},{1,32},{2,33},{3,64},{4,65},{5,96},{6,97},{7,128},{8,129},{9... | collective-permute-start | bytes 393224 | tf_op jit(solution)/shard_map/ppermute | solution.py:188
  16.0 8.1 %collective-permute-start.1 = (bf16[32,32,64]{2,0,1:T(8,128)(2,1)S(1)}, bf16[32,32,64]{2,0,1:T(8,128)(2,1)S(1)}, u32[]{:S(2)}, u32[]{:S(2)}) collective-permute-start(bf16[32,32,64]{2,0,1:T(8,128)(2,1)S(1)} %get-tuple-element.13), channel_id=1, source_target_pairs={{32,0},{64,32},{96,64},{128,96},{160,128},{192,160},{224,192},{256... | collective-permute-start | bytes 393224 | tf_op jit(solution)/shard_map/ppermute | solution.py:147
  18.3 12.8 %collective-permute-start = (bf16[32,32,64]{2,0,1:T(8,128)(2,1)S(1)}, bf16[32,32,64]{2,0,1:T(8,128)(2,1)S(1)}, u32[]{:S(2)}, u32[]{:S(2)}) collective-permute-start(bf16[32,32,64]{2,0,1:T(8,128)(2,1)S(1)} %get-tuple-element.14), channel_id=1, source_target_pairs={{0,32},{32,64},{64,96},{96,128},{128,160},{160,192},{192,224},{224... | collective-permute-start | bytes 393224 | tf_op jit(solution)/shard_map/ppermute | solution.py:146
  21.6 63.9 %collective-permute-start.5 = (bf16[32,32,64]{2,0,1:T(8,128)(2,1)S(1)}, bf16[32,32,64]{2,0,1:T(8,128)(2,1)S(1)}, u32[]{:S(2)}, u32[]{:S(2)}) collective-permute-start(bf16[32,32,64]{2,0,1:T(8,128)(2,1)S(1)} %get-tuple-element.12), channel_id=1, source_target_pairs={{1,1},{2,0},{3,33},{4,32},{5,65},{6,64},{7,97},{8,96},{9,129},{10,... | collective-permute-start | bytes 393224 | tf_op jit(solution)/shard_map/ppermute | solution.py:188
  24.1 97.6 %collective-permute-start.3 = (bf16[32,32,64]{2,0,1:T(8,128)(2,1)S(1)}, bf16[32,32,64]{2,0,1:T(8,128)(2,1)S(1)}, u32[]{:S(2)}, u32[]{:S(2)}) collective-permute-start(bf16[32,32,64]{2,0,1:T(8,128)(2,1)S(1)} %get-tuple-element.12), channel_id=1, source_target_pairs={{0,0},{1,33},{2,32},{3,65},{4,64},{5,97},{6,96},{7,129},{8,128},{9... | collective-permute-start | bytes 393224 | tf_op jit(solution)/shard_map/ppermute | solution.py:188
  130.2 10.7 %copy-start = (f32[96,32,64]{2,1,0:T(8,128)S(1)}, f32[96,32,64]{2,1,0:T(8,128)}, u32[]{:S(2)}) copy-start(f32[96,32,64]{2,1,0:T(8,128)} %shard_map.55) | copy-start | bytes 2359300
  132.9 19.5 %collective-permute-start.7 = (f32[96,24,64]{0,2,1:T(8,128)}, f32[96,24,64]{0,2,1:T(8,128)}, u32[]{:S(2)}, u32[]{:S(2)}) collective-permute-start(f32[96,24,64]{0,2,1:T(8,128)} %copy.17), channel_id=1, source_target_pairs={{1,0},{2,1},{3,2},{4,3},{5,4},{6,5},{7,6},{8,7},{9,8},{10,9},{11,1... | collective-permute-start | bytes 1769480 | tf_op jit(solution)/shard_map/ppermute | solution.py:147
  135.4 20.0 %collective-permute-start.6 = (f32[96,24,64]{0,2,1:T(8,128)}, f32[96,24,64]{0,2,1:T(8,128)}, u32[]{:S(2)}, u32[]{:S(2)}) collective-permute-start(f32[96,24,64]{0,2,1:T(8,128)} %copy.16), channel_id=1, source_target_pairs={{0,1},{1,2},{2,3},{3,4},{4,5},{5,6},{6,7},{7,8},{8,9},{9,10},{10,1... | collective-permute-start | bytes 1769480 | tf_op jit(solution)/shard_map/ppermute | solution.py:146

commit v2 on v0

--- a/solution.py
+++ b/solution.py
@@ -93,7 +93,7 @@
         work[odds] = jnp.where(enabled, odd_part, detail)
 
 
-def _stage_kernel(*refs, kind, width, length):
+def _stage_kernel(*refs, kind, width, length, out_from, out_rows):
     if kind == "fwd":
         ends_ref, depth_ref, left_ref, right_ref, out_ref, work = refs
     elif kind == "both":
@@ -119,17 +119,19 @@
     if kind != "fwd":
         for depth_index in reversed(range(LEVELS)):
             _lift_level(work, 2**depth_index, depth > depth_index, False, width, length, ends)
-    out_ref[...] = work[PAD + width : PAD + width + length]
-
-
-def lift_stage(kind, operands, ends, depth, width, length):
+    out_ref[...] = work[PAD + out_from : PAD + out_from + out_rows]
+
+
+def lift_stage(kind, operands, ends, depth, width, length, out_from, out_rows):
     rows, cols, samples = operands[-1].shape
-    kernel = functools.partial(_stage_kernel, kind=kind, width=width, length=length)
+    kernel = functools.partial(
+        _stage_kernel, kind=kind, width=width, length=length, out_from=out_from, out_rows=out_rows
+    )
     smem = pl.BlockSpec(memory_space=pltpu.SMEM)
     vmem = pl.BlockSpec(memory_space=pltpu.VMEM)
     return pl.pallas_call(
         kernel,
-        out_shape=jax.ShapeDtypeStruct((length, cols, samples), jnp.float32),
+        out_shape=jax.ShapeDtypeStruct((out_rows, cols, samples), jnp.float32),
         in_specs=[smem] + [vmem] * (1 + len(operands)),
         out_specs=vmem,
         scratch_shapes=[pltpu.VMEM((rows + 2 * PAD, cols, samples), jnp.float32)],
@@ -185,6 +187,9 @@
         got = lax.dynamic_index_in_dim(received, (own_part - slot) % ratio, axis=0, keepdims=False)
         slots.append(jnp.transpose(got, (1, 0, 2)))
     mirror = jnp.concatenate(slots, axis=0)
+    mirror_halo = 2 * SRC_HALO
+    mirror_wide = extend(mirror, "src", 0, mirror_halo)
+    merged_wide = extend(merged, "src", 0, mirror_halo)
 
     samples_shape = (1, 1, samples)
     src_depth = levels[0].reshape(samples_shape)
@@ -192,18 +197,18 @@
     src_ends = jnp.stack([src_index == 0, src_index == src_count - 1]).astype(jnp.int32)
     rcv_ends = jnp.stack([rcv_index == 0, rcv_index == rcv_count - 1]).astype(jnp.int32)
 
-    merged_wide = extend(merged, "src", 0, SRC_HALO)
-    mirror_wide = extend(mirror, "src", 0, SRC_HALO)
-    coeff = lift_stage("fwd", (merged_wide, mirror_wide), src_ends, src_depth, SRC_HALO, row_count)
+    coeff = lift_stage(
+        "fwd", (merged_wide, mirror_wide), src_ends, src_depth, mirror_halo, row_count,
+        mirror_halo - SRC_HALO, row_count + 2 * SRC_HALO,
+    )
 
     wide = jnp.moveaxis(extend(coeff, "rcv", 1, RCV_HALO), 1, 0)
     turned = lift_stage(
-        "both", (thresholds.reshape(samples_shape), wide), rcv_ends, rcv_depth, RCV_HALO, col_count
+        "both", (thresholds.reshape(samples_shape), wide), rcv_ends, rcv_depth, RCV_HALO, col_count,
+        RCV_HALO, col_count,
     )
     coeff = jnp.moveaxis(turned, 0, 1)
-
-    wide = extend(coeff, "src", 0, SRC_HALO)
-    return lift_stage("inv", (wide,), src_ends, src_depth, SRC_HALO, row_count)
+    return lift_stage("inv", (coeff,), src_ends, src_depth, SRC_HALO, row_count, SRC_HALO, row_count)
 
 def solution(mesh):
     return jax.shard_map(

time: 148 us -> 138 us (0.932)
  the two profiles are of different devices: /device:TPU:23 before, /device:TPU:45 now
where the time goes in v2:
time: 138 us
  starting transfers between devices  51.5 us (37%)
  waiting for transfers between devices  43.5 us (32%)
  Pallas kernels  16.4 us (12%)
  local copies, waits for them, and re-layouts  16 us (12%)
  other arithmetic  9.02 us (7%)
    ppermute x3, starting transfers between devices, extend(): lax.ppermute(tail, axis_name, [(i, i + 1) for i in range(count - 1)])  27.8 us
    ppermute x2, waiting for transfers between devices, body(): received.append(lax.ppermute(send, ('src', 'rcv'), perm))  21.2 us
    pallas_call x3, Pallas kernels, lift_stage(): pl.pallas_call(kernel, out_shape=jax.ShapeDtypeStruct((out_rows, cols, sa...  16.4 us
    ppermute x3, waiting for transfers between devices, extend(): lax.ppermute(head, axis_name, [(i + 1, i) for i in range(count - 1)])  16.2 us
    ppermute x3, starting transfers between devices, extend(): lax.ppermute(head, axis_name, [(i + 1, i) for i in range(count - 1)])  12.4 us
    ppermute x2, starting transfers between devices, body(): received.append(lax.ppermute(send, ('src', 'rcv'), perm))  11.3 us
    ppermute x3, waiting for transfers between devices, extend(): lax.ppermute(tail, axis_name, [(i, i + 1) for i in range(count - 1)])  6.11 us
    pallas_call x2, local copies, waits for them, and re-layouts, lift_stage(): pl.pallas_call(kernel, out_shape=jax.ShapeDtypeStruct((out_rows, cols, sa...  4.4 us
  transfers between devices with their start and end apart: 8, of which 6 were waited for; matrix products, arithmetic and copies ran while one was open for 5% of the time, Pallas kernels for 0%

profile of v2, /device:TPU:45, one launch (start us, length us, event | category | flops | bytes accessed | tf_op | source)
XLA Modules:
  0.0 137.6 jit_solution(6608387901171589047)
XLA Ops:
  0.0 0.9 fusion.6
  0.9 0.2 fusion.8
  1.2 1.5 %fusion.1 = bf16[64,32,64]{2,1,0:T(8,128)(2,1)S(1)} fusion(bf16[64,32,64]{2,1,0:T(8,128)(2,1)} %param.6, bf16[64,32,64]{2,1,0:T(8,128)(2,1)} %param.5, f32[64,32]{1,0:T(8,128)S(1)} %fusion.8), kind=kLoop, calls=%fused_computation.5 | loop fusion | flops 786432 | bytes 794624 | tf_op jit(solution)/shard_map/convert_element_type | solution.py:170
  2.7 0.0 copy-start.1
  2.8 0.1 copy.28
  2.9 7.0 %collective-permute-start.2 = (bf16[32,32,64]{2,0,1:T(8,128)(2,1)S(1)}, bf16[32,32,64]{2,0,1:T(8,128)(2,1)S(1)}, u32[]{:S(2)}, u32[]{:S(2)}) collective-permute-start(bf16[32,32,64]{2,0,1:T(8,128)(2,1)S(1)} %bitcast.36), channel_id=1, source_target_pairs={{0,0},{1,1},{2,32},{3,33},{4,64},{5,65},{6,96},{7,97},{8,128},{9,1... | collective-permute-start | bytes 393224 | tf_op jit(solution)/shard_map/ppermute | solution.py:183
  9.9 0.1 copy.27
  10.0 4.2 %collective-permute-start.3 = (bf16[32,32,64]{2,0,1:T(8,128)(2,1)S(1)}, bf16[32,32,64]{2,0,1:T(8,128)(2,1)S(1)}, u32[]{:S(2)}, u32[]{:S(2)}) collective-permute-start(bf16[32,32,64]{2,0,1:T(8,128)(2,1)S(1)} %bitcast.37), channel_id=1, source_target_pairs={{0,1},{1,0},{2,33},{3,32},{4,65},{5,64},{6,97},{7,96},{8,129},{9,1... | collective-permute-start | bytes 393224 | tf_op jit(solution)/shard_map/ppermute | solution.py:183
  14.3 6.7 %collective-permute-start = (bf16[32,32,64]{2,1,0:T(8,128)(2,1)S(1)}, bf16[32,32,64]{2,1,0:T(8,128)(2,1)S(1)}, u32[]{:S(2)}, u32[]{:S(2)}) collective-permute-start(bf16[32,32,64]{2,1,0:T(8,128)(2,1)S(1)} %get-tuple-element.11), channel_id=1, source_target_pairs={{0,32},{32,64},{64,96},{96,128},{128,160},{160,192},{192,224},{224... | collective-permute-start | bytes 393224 | tf_op jit(solution)/shard_map/ppermute | solution.py:146
  21.0 1.9 %collective-permute-start.1 = (bf16[32,32,64]{2,1,0:T(8,128)(2,1)S(1)}, bf16[32,32,64]{2,1,0:T(8,128)(2,1)S(1)}, u32[]{:S(2)}, u32[]{:S(2)}) collective-permute-start(bf16[32,32,64]{2,1,0:T(8,128)(2,1)S(1)} %get-tuple-element.12), channel_id=1, source_target_pairs={{32,0},{64,32},{96,64},{128,96},{160,128},{192,160},{224,192},{256... | collective-permute-start | bytes 393224 | tf_op jit(solution)/shard_map/ppermute | solution.py:147
  22.9 0.0 copy-done.1
  23.0 0.5 slice_bitcast_fusion
  23.5 0.7 add_convert_fusion.refs_0_
  24.2 6.9 %collective-permute-done.2 = bf16[32,32,64]{2,0,1:T(8,128)(2,1)S(1)} collective-permute-done((bf16[32,32,64]{2,0,1:T(8,128)(2,1)S(1)}, bf16[32,32,64]{2,0,1:T(8,128)(2,1)S(1)}, u32[]{:S(2)}, u32[]{:S(2)}) %collective-permute-start.2) | collective-permute-done | bytes 131104 | tf_op jit(solution)/shard_map/ppermute | solution.py:183
  31.1 14.3 %collective-permute-done.3 = bf16[32,32,64]{2,0,1:T(8,128)(2,1)S(1)} collective-permute-done((bf16[32,32,64]{2,0,1:T(8,128)(2,1)S(1)}, bf16[32,32,64]{2,0,1:T(8,128)(2,1)S(1)}, u32[]{:S(2)}, u32[]{:S(2)}) %collective-permute-start.3) | collective-permute-done | bytes 131104 | tf_op jit(solution)/shard_map/ppermute | solution.py:183
  45.4 0.3 fusion.5
  45.6 19.0 %collective-permute-start.4 = (bf16[32,32,64]{2,1,0:T(8,128)(2,1)S(1)}, bf16[32,32,64]{2,1,0:T(8,128)(2,1)S(1)}, u32[]{:S(2)}, u32[]{:S(2)}) collective-permute-start(bf16[32,32,64]{2,1,0:T(8,128)(2,1)S(1)} %get-tuple-element.7), channel_id=1, source_target_pairs={{0,32},{32,64},{64,96},{96,128},{128,160},{160,192},{192,224},{224... | collective-permute-start | bytes 393224 | tf_op jit(solution)/shard_map/ppermute | solution.py:146
  64.7 1.9 %collective-permute-start.5 = (bf16[32,32,64]{2,1,0:T(8,128)(2,1)S(1)}, bf16[32,32,64]{2,1,0:T(8,128)(2,1)S(1)}, u32[]{:S(2)}, u32[]{:S(2)}) collective-permute-start(bf16[32,32,64]{2,1,0:T(8,128)(2,1)S(1)} %get-tuple-element.8), channel_id=1, source_target_pairs={{32,0},{64,32},{96,64},{128,96},{160,128},{192,160},{224,192},{256... | collective-permute-start | bytes 393224 | tf_op jit(solution)/shard_map/ppermute | solution.py:147
  66.6 0.0 collective-permute-done
  66.6 0.0 collective-permute-done.1
  66.6 1.2 pad_maximum_fusion.refs_2_
  67.8 0.1 collective-permute-done.4
  67.9 4.4 %collective-permute-done.5 = bf16[32,32,64]{2,1,0:T(8,128)(2,1)S(1)} collective-permute-done((bf16[32,32,64]{2,1,0:T(8,128)(2,1)S(1)}, bf16[32,32,64]{2,1,0:T(8,128)(2,1)S(1)}, u32[]{:S(2)}, u32[]{:S(2)}) %collective-permute-start.5) | collective-permute-done | bytes 131104 | tf_op jit(solution)/shard_map/ppermute | solution.py:147
  72.3 1.2 pad_maximum_fusion.1.refs_3_
  73.6 4.5 %shard_map.55 = f32[96,32,64]{2,1,0:T(8,128)} custom-call(s32[2]{0:T(128)} %add_convert_fusion.refs_0_, s32[1,1,64]{2,1,0:T(1,128)} %get-tuple-element.14.refs_1_, bf16[128,32,64]{2,1,0:T(8,128)(2,1)} %pad_maximum_fusion.refs_2_, bf16[128,32,64]{2,1,0:T(8,128)(2,1)} %pad_maximum_fusion.1.refs_3_), custom_call_target="tpu_custom_call" | custom-call | tf_op jit(solution)/shard_map/pallas_call | solution.py:132
  78.0 2.8 %fusion.11 = (f32[96,24,64]{2,1,0:T(8,128)S(1)}, f32[96,24,64]{2,1,0:T(8,128)}) fusion(f32[96,32,64]{2,1,0:T(8,128)} %shard_map.55), kind=kLoop, calls=%fused_computation.39 | loop fusion | bytes 2359296 | tf_op jit(solution)/shard_map/slice | solution.py:145
  80.8 0.0 copy-start
  80.8 2.6 %copy.17 = f32[96,24,64]{0,2,1:T(8,128)} copy(f32[96,24,64]{2,1,0:T(8,128)} %get-tuple-element.6) | data formatting | bytes 1179648 | tf_op jit(solution)/shard_map/slice | solution.py:144
  83.5 8.6 %collective-permute-start.7 = (f32[96,24,64]{0,2,1:T(8,128)}, f32[96,24,64]{0,2,1:T(8,128)}, u32[]{:S(2)}, u32[]{:S(2)}) collective-permute-start(f32[96,24,64]{0,2,1:T(8,128)} %copy.17), channel_id=1, source_target_pairs={{1,0},{2,1},{3,2},{4,3},{5,4},{6,5},{7,6},{8,7},{9,8},{10,9},{11,1... | collective-permute-start | bytes 1769480 | tf_op jit(solution)/shard_map/ppermute | solution.py:147
  92.0 1.3 copy.16
  93.3 2.1 %collective-permute-start.6 = (f32[96,24,64]{0,2,1:T(8,128)}, f32[96,24,64]{0,2,1:T(8,128)}, u32[]{:S(2)}, u32[]{:S(2)}) collective-permute-start(f32[96,24,64]{0,2,1:T(8,128)} %copy.16), channel_id=1, source_target_pairs={{0,1},{1,2},{2,3},{3,4},{4,5},{5,6},{6,7},{7,8},{8,9},{9,10},{10,1... | collective-permute-start | bytes 1769480 | tf_op jit(solution)/shard_map/ppermute | solution.py:146
  95.4 0.6 add_convert_fusion.1.refs_0_
  96.1 0.0 copy-done
  96.1 0.9 copy.19
  97.0 11.8 %collective-permute-done.7 = f32[96,24,64]{0,2,1:T(8,128)} collective-permute-done((f32[96,24,64]{0,2,1:T(8,128)}, f32[96,24,64]{0,2,1:T(8,128)}, u32[]{:S(2)}, u32[]{:S(2)}) %collective-permute-start.7) | collective-permute-done | bytes 589856 | tf_op jit(solution)/shard_map/ppermute | solution.py:147
  108.8 1.5 %copy.20 = f32[96,24,64]{2,0,1:T(8,128)S(1)} copy(f32[96,24,64]{0,2,1:T(8,128)} %collective-permute-done.7) | data formatting | bytes 1179648 | tf_op jit(solution)/shard_map/ppermute | solution.py:147
  110.3 6.0 %collective-permute-done.6 = f32[96,24,64]{0,2,1:T(8,128)} collective-permute-done((f32[96,24,64]{0,2,1:T(8,128)}, f32[96,24,64]{0,2,1:T(8,128)}, u32[]{:S(2)}, u32[]{:S(2)}) %collective-permute-start.6) | collective-permute-done | bytes 589856 | tf_op jit(solution)/shard_map/ppermute | solution.py:146
  116.2 2.5 %copy.18 = f32[96,24,64]{2,0,1:T(8,128)} copy(f32[96,24,64]{0,2,1:T(8,128)} %collective-permute-done.6) | data formatting | bytes 1179648 | tf_op jit(solution)/shard_map/ppermute | solution.py:146
  118.8 3.5 %maximum_bitcast_fusion.refs_3_ = f32[80,96,64]{2,1,0:T(8,128)} fusion(f32[96,24,64]{2,0,1:T(8,128)S(1)} %copy.20, f32[96,32,64]{2,0,1:T(8,128)S(1)} %copy.19, f32[96,24,64]{2,0,1:T(8,128)} %copy.18), kind=kLoop, calls=%fused_computation | loop fusion | flops 983040 | bytes 3932160 | tf_op jit(solution)/shard_map/transpose | solution.py:205
  122.2 8.6 %shard_map.56 = f32[32,96,64]{2,1,0:T(8,128)} custom-call(s32[2]{0:T(128)} %add_convert_fusion.1.refs_0_, s32[1,1,64]{2,1,0:T(1,128)} %get-tuple-element.13.refs_1_, f32[1,1,64]{2,1,0:T(1,128)} %bitcast.38, f32[80,96,64]{2,1,0:T(8,128)} %maximum_bitcast_fusion.refs_3_), custom_call_target="tpu_custom_call" | custom-call | tf_op jit(solution)/shard_map/pallas_call | solution.py:132
  130.8 3.5 %copy.26 = f32[32,96,64]{2,0,1:T(8,128)} copy(f32[32,96,64]{2,1,0:T(8,128)} %shard_map.56) | data formatting | bytes 1572864 | tf_op jit(solution)/shard_map/pallas_call | solution.py:132
  134.3 3.3 %shard_map.57 = f32[64,32,64]{2,1,0:T(8,128)} custom-call(s32[2]{0:T(128)} %add_convert_fusion.refs_0_, s32[1,1,64]{2,1,0:T(1,128)} %get-tuple-element.14.refs_1_, f32[96,32,64]{2,1,0:T(8,128)} %bitcast.33), custom_call_target="tpu_custom_call" | custom-call | tf_op jit(solution)/shard_map/pallas_call | solution.py:132
  (4 shorter events, 0.1 us)
Async XLA Ops:
  2.7 20.2 %copy-start.1 = (s32[2,64]{1,0:T(2,128)S(1)}, s32[2,64]{1,0:T(2,128)}, u32[]{:S(2)}) copy-start(s32[2,64]{1,0:T(2,128)} %param.8) | copy-start | bytes 1540
  2.9 28.2 %collective-permute-start.2 = (bf16[32,32,64]{2,0,1:T(8,128)(2,1)S(1)}, bf16[32,32,64]{2,0,1:T(8,128)(2,1)S(1)}, u32[]{:S(2)}, u32[]{:S(2)}) collective-permute-start(bf16[32,32,64]{2,0,1:T(8,128)(2,1)S(1)} %bitcast.36), channel_id=1, source_target_pairs={{0,0},{1,1},{2,32},{3,33},{4,64},{5,65},{6,96},{7,97},{8,128},{9,1... | collective-permute-start | bytes 393224 | tf_op jit(solution)/shard_map/ppermute | solution.py:183
  10.0 35.3 %collective-permute-start.3 = (bf16[32,32,64]{2,0,1:T(8,128)(2,1)S(1)}, bf16[32,32,64]{2,0,1:T(8,128)(2,1)S(1)}, u32[]{:S(2)}, u32[]{:S(2)}) collective-permute-start(bf16[32,32,64]{2,0,1:T(8,128)(2,1)S(1)} %bitcast.37), channel_id=1, source_target_pairs={{0,1},{1,0},{2,33},{3,32},{4,65},{5,64},{6,97},{7,96},{8,129},{9,1... | collective-permute-start | bytes 393224 | tf_op jit(solution)/shard_map/ppermute | solution.py:183
  14.3 52.3 %collective-permute-start = (bf16[32,32,64]{2,1,0:T(8,128)(2,1)S(1)}, bf16[32,32,64]{2,1,0:T(8,128)(2,1)S(1)}, u32[]{:S(2)}, u32[]{:S(2)}) collective-permute-start(bf16[32,32,64]{2,1,0:T(8,128)(2,1)S(1)} %get-tuple-element.11), channel_id=1, source_target_pairs={{0,32},{32,64},{64,96},{96,128},{128,160},{160,192},{192,224},{224... | collective-permute-start | bytes 393224 | tf_op jit(solution)/shard_map/ppermute | solution.py:146
  21.0 45.6 %collective-permute-start.1 = (bf16[32,32,64]{2,1,0:T(8,128)(2,1)S(1)}, bf16[32,32,64]{2,1,0:T(8,128)(2,1)S(1)}, u32[]{:S(2)}, u32[]{:S(2)}) collective-permute-start(bf16[32,32,64]{2,1,0:T(8,128)(2,1)S(1)} %get-tuple-element.12), channel_id=1, source_target_pairs={{32,0},{64,32},{96,64},{128,96},{160,128},{192,160},{224,192},{256... | collective-permute-start | bytes 393224 | tf_op jit(solution)/shard_map/ppermute | solution.py:147
  45.6 22.3 %collective-permute-start.4 = (bf16[32,32,64]{2,1,0:T(8,128)(2,1)S(1)}, bf16[32,32,64]{2,1,0:T(8,128)(2,1)S(1)}, u32[]{:S(2)}, u32[]{:S(2)}) collective-permute-start(bf16[32,32,64]{2,1,0:T(8,128)(2,1)S(1)} %get-tuple-element.7), channel_id=1, source_target_pairs={{0,32},{32,64},{64,96},{96,128},{128,160},{160,192},{192,224},{224... | collective-permute-start | bytes 393224 | tf_op jit(solution)/shard_map/ppermute | solution.py:146
  64.7 7.7 %collective-permute-start.5 = (bf16[32,32,64]{2,1,0:T(8,128)(2,1)S(1)}, bf16[32,32,64]{2,1,0:T(8,128)(2,1)S(1)}, u32[]{:S(2)}, u32[]{:S(2)}) collective-permute-start(bf16[32,32,64]{2,1,0:T(8,128)(2,1)S(1)} %get-tuple-element.8), channel_id=1, source_target_pairs={{32,0},{64,32},{96,64},{128,96},{160,128},{192,160},{224,192},{256... | collective-permute-start | bytes 393224 | tf_op jit(solution)/shard_map/ppermute | solution.py:147
  80.8 15.2 %copy-start = (f32[96,32,64]{2,1,0:T(8,128)S(1)}, f32[96,32,64]{2,1,0:T(8,128)}, u32[]{:S(2)}) copy-start(f32[96,32,64]{2,1,0:T(8,128)} %shard_map.55) | copy-start | bytes 2359300
  83.5 25.3 %collective-permute-start.7 = (f32[96,24,64]{0,2,1:T(8,128)}, f32[96,24,64]{0,2,1:T(8,128)}, u32[]{:S(2)}, u32[]{:S(2)}) collective-permute-start(f32[96,24,64]{0,2,1:T(8,128)} %copy.17), channel_id=1, source_target_pairs={{1,0},{2,1},{3,2},{4,3},{5,4},{6,5},{7,6},{8,7},{9,8},{10,9},{11,1... | collective-permute-start | bytes 1769480 | tf_op jit(solution)/shard_map/ppermute | solution.py:147
  93.3 22.9 %collective-permute-start.6 = (f32[96,24,64]{0,2,1:T(8,128)}, f32[96,24,64]{0,2,1:T(8,128)}, u32[]{:S(2)}, u32[]{:S(2)}) collective-permute-start(f32[96,24,64]{0,2,1:T(8,128)} %copy.16), channel_id=1, source_target_pairs={{0,1},{1,2},{2,3},{3,4},{4,5},{5,6},{6,7},{7,8},{8,9},{9,10},{10,1... | collective-permute-start | bytes 1769480 | tf_op jit(solution)/shard_map/ppermute | solution.py:146

commit v3 on v2

--- a/solution.py
+++ b/solution.py
@@ -62,17 +62,24 @@
 PAD = 8
 
 
-def _lift_level(work, stride, enabled, forward, width, length, ends):
-    rows = work.shape[0] - 2 * PAD
+def _lift_level(work, stride, enabled, forward, width, length, ends, axis=0):
+    rows = work.shape[axis] - 2 * PAD
     pairs = rows // (2 * stride)
     step = 2 * stride
-    pair_ids = lax.broadcasted_iota(jnp.int32, (pairs,) + work.shape[1:], 0)
+    shape = list(work.shape)
+    shape[axis] = pairs
+    pair_ids = lax.broadcasted_iota(jnp.int32, tuple(shape), axis)
     first = (pair_ids == width // step) & (ends[0] != 0)
     last = (pair_ids == (width + length) // step - 1) & (ends[1] != 0)
-    evens = pl.ds(PAD, pairs, stride=step)
-    odds = pl.ds(PAD + stride, pairs, stride=step)
-    next_evens = pl.ds(PAD + step, pairs, stride=step)
-    prev_odds = pl.ds(PAD - stride, pairs, stride=step)
+
+    def at(start):
+        window = pl.ds(start, pairs, stride=step)
+        return (window,) if axis == 0 else (slice(None), window)
+
+    evens = at(PAD)
+    odds = at(PAD + stride)
+    next_evens = at(PAD + step)
+    prev_odds = at(PAD - stride)
     if forward:
         even_part = work[evens]
         odd_part = work[odds]
@@ -93,9 +100,39 @@
         work[odds] = jnp.where(enabled, odd_part, detail)
 
 
+def _rcv_kernel(ends_ref, depth_ref, thr_ref, left_ref, mid_ref, right_ref, out_ref, work, *, width):
+    length = mid_ref.shape[1]
+    ends = (ends_ref[0], ends_ref[1])
+    depth = depth_ref[...]
+    work[:, PAD : PAD + width] = left_ref[...]
+    work[:, PAD + width : PAD + width + length] = mid_ref[...]
+    work[:, PAD + width + length : PAD + 2 * width + length] = right_ref[...]
+    for depth_index in range(LEVELS):
+        _lift_level(work, 2**depth_index, depth > depth_index, True, width, length, ends, axis=1)
+    field = work[:, PAD : PAD + 2 * width + length]
+    thr = thr_ref[...]
+    work[:, PAD : PAD + 2 * width + length] = field - jnp.clip(field, -thr, thr)
+    for depth_index in reversed(range(LEVELS)):
+        _lift_level(work, 2**depth_index, depth > depth_index, False, width, length, ends, axis=1)
+    out_ref[...] = work[:, PAD + width : PAD + width + length]
+
+
+def rcv_stage(left, mid, right, thr, ends, depth, width):
+    rows, cols, samples = mid.shape
+    smem = pl.BlockSpec(memory_space=pltpu.SMEM)
+    vmem = pl.BlockSpec(memory_space=pltpu.VMEM)
+    return pl.pallas_call(
+        functools.partial(_rcv_kernel, width=width),
+        out_shape=jax.ShapeDtypeStruct(mid.shape, jnp.float32),
+        in_specs=[smem] + [vmem] * 5,
+        out_specs=vmem,
+        scratch_shapes=[pltpu.VMEM((rows, cols + 2 * width + 2 * PAD, samples), jnp.float32)],
+    )(ends, depth, thr, left, mid, right)
+
+
 def _stage_kernel(*refs, kind, width, length, out_from, out_rows):
     if kind == "fwd":
-        ends_ref, depth_ref, left_ref, right_ref, out_ref, work = refs
+        ends_ref, depth_ref, terms_ref, out_ref, work = refs
     elif kind == "both":
         ends_ref, depth_ref, thr_ref, in_ref, out_ref, work = refs
     else:
@@ -105,7 +142,7 @@
     depth = depth_ref[...]
     if kind == "fwd":
         work[PAD : PAD + rows] = 0.5 * (
-            left_ref[...].astype(jnp.float32) + right_ref[...].astype(jnp.float32)
+            terms_ref[:, 0].astype(jnp.float32) + terms_ref[:, 1].astype(jnp.float32)
         )
     else:
         work[PAD : PAD + rows] = in_ref[...]
@@ -123,7 +160,8 @@
 
 
 def lift_stage(kind, operands, ends, depth, width, length, out_from, out_rows):
-    rows, cols, samples = operands[-1].shape
+    rows = operands[-1].shape[0]
+    cols, samples = operands[-1].shape[-2:]
     kernel = functools.partial(
         _stage_kernel, kind=kind, width=width, length=length, out_from=out_from, out_rows=out_rows
     )
@@ -138,13 +176,18 @@
     )(ends, depth, *operands)
 
 
-def extend(cells, axis_name, dim, width):
+def halos(cells, axis_name, dim, width):
     count = lax.axis_size(axis_name)
     length = cells.shape[dim]
     head = lax.slice_in_dim(cells, 0, width, axis=dim)
     tail = lax.slice_in_dim(cells, length - width, length, axis=dim)
     from_left = lax.ppermute(tail, axis_name, [(i, i + 1) for i in range(count - 1)])
     from_right = lax.ppermute(head, axis_name, [(i + 1, i) for i in range(count - 1)])
+    return from_left, from_right
+
+
+def extend(cells, axis_name, dim, width):
+    from_left, from_right = halos(cells, axis_name, dim, width)
     return jnp.concatenate([from_left, cells, from_right], axis=dim)
 
 
@@ -188,8 +231,7 @@
         slots.append(jnp.transpose(got, (1, 0, 2)))
     mirror = jnp.concatenate(slots, axis=0)
     mirror_halo = 2 * SRC_HALO
-    mirror_wide = extend(mirror, "src", 0, mirror_halo)
-    merged_wide = extend(merged, "src", 0, mirror_halo)
+    terms = extend(jnp.stack([merged, mirror], axis=1), "src", 0, mirror_halo)
 
     samples_shape = (1, 1, samples)
     src_depth = levels[0].reshape(samples_shape)
@@ -198,16 +240,14 @@
     rcv_ends = jnp.stack([rcv_index == 0, rcv_index == rcv_count - 1]).astype(jnp.int32)
 
     coeff = lift_stage(
-        "fwd", (merged_wide, mirror_wide), src_ends, src_depth, mirror_halo, row_count,
+        "fwd", (terms,), src_ends, src_depth, mirror_halo, row_count,
         mirror_halo - SRC_HALO, row_count + 2 * SRC_HALO,
     )
 
-    wide = jnp.moveaxis(extend(coeff, "rcv", 1, RCV_HALO), 1, 0)
-    turned = lift_stage(
-        "both", (thresholds.reshape(samples_shape), wide), rcv_ends, rcv_depth, RCV_HALO, col_count,
-        RCV_HALO, col_count,
-    )
-    coeff = jnp.moveaxis(turned, 0, 1)
+    from_left, from_right = halos(coeff, "rcv", 1, RCV_HALO)
+    coeff = rcv_stage(
+        from_left, coeff, from_right, thresholds.reshape(samples_shape), rcv_ends, rcv_depth, RCV_HALO
+    )
     return lift_stage("inv", (coeff,), src_ends, src_depth, SRC_HALO, row_count, SRC_HALO, row_count)
 
 def solution(mesh):

time: 138 us -> 131 us (0.949)
  the two profiles are of different devices: /device:TPU:45 before, /device:TPU:27 now
where the time goes in v3:
time: 131 us
  waiting for transfers between devices  61.6 us (47%)
  starting transfers between devices  35.6 us (27%)
  Pallas kernels  20.3 us (15%)
  local copies, waits for them, and re-layouts  7.08 us (5%)
  other arithmetic  5.25 us (4%)
    ppermute x2, waiting for transfers between devices, body(): received.append(lax.ppermute(send, ('src', 'rcv'), perm))  42.5 us
    ppermute x2, starting transfers between devices, body(): received.append(lax.ppermute(send, ('src', 'rcv'), perm))  16.3 us
    ppermute x2, waiting for transfers between devices, halos(): lax.ppermute(tail, axis_name, [(i, i + 1) for i in range(count - 1)])  13.3 us
    pallas_call x1, Pallas kernels, rcv_stage(): pl.pallas_call(functools.partial(_rcv_kernel, width=width), out_shape=jax...  12.4 us
    ppermute x2, starting transfers between devices, halos(): lax.ppermute(head, axis_name, [(i + 1, i) for i in range(count - 1)])  9.85 us
    ppermute x2, starting transfers between devices, halos(): lax.ppermute(tail, axis_name, [(i, i + 1) for i in range(count - 1)])  9.44 us
    pallas_call x2, Pallas kernels, lift_stage(): pl.pallas_call(kernel, out_shape=jax.ShapeDtypeStruct((out_rows, cols, sa...  7.8 us
    ppermute x2, waiting for transfers between devices, halos(): lax.ppermute(head, axis_name, [(i + 1, i) for i in range(count - 1)])  5.77 us
  transfers between devices with their start and end apart: 6, of which 5 were waited for; matrix products, arithmetic and copies ran while one was open for 4% of the time, Pallas kernels for 0%

profile of v3, /device:TPU:27, one launch (start us, length us, event | category | flops | bytes accessed | tf_op | source)
XLA Modules:
  0.0 131.0 jit_solution(12824523792737708797)
XLA Ops:
  0.0 0.9 fusion.7
  0.9 0.2 fusion.9
  1.2 1.5 %fusion.1 = bf16[64,32,64]{2,1,0:T(8,128)(2,1)S(1)} fusion(bf16[64,32,64]{2,1,0:T(8,128)(2,1)} %param.6, bf16[64,32,64]{2,1,0:T(8,128)(2,1)} %param.5, f32[64,32]{1,0:T(8,128)S(1)} %fusion.9), kind=kLoop, calls=%fused_computation.4 | loop fusion | flops 786432 | bytes 794624 | tf_op jit(solution)/shard_map/convert_element_type | solution.py:213
  2.8 0.1 copy.20
  2.9 14.4 %collective-permute-start = (bf16[32,32,64]{2,0,1:T(8,128)(2,1)S(1)}, bf16[32,32,64]{2,0,1:T(8,128)(2,1)S(1)}, u32[]{:S(2)}, u32[]{:S(2)}) collective-permute-start(bf16[32,32,64]{2,0,1:T(8,128)(2,1)S(1)} %bitcast.35), channel_id=1, source_target_pairs={{0,0},{1,1},{2,32},{3,33},{4,64},{5,65},{6,96},{7,97},{8,128},{9,1... | collective-permute-start | bytes 393224 | tf_op jit(solution)/shard_map/ppermute | solution.py:226
  17.2 0.1 copy.19
  17.4 1.9 %collective-permute-start.1 = (bf16[32,32,64]{2,0,1:T(8,128)(2,1)S(1)}, bf16[32,32,64]{2,0,1:T(8,128)(2,1)S(1)}, u32[]{:S(2)}, u32[]{:S(2)}) collective-permute-start(bf16[32,32,64]{2,0,1:T(8,128)(2,1)S(1)} %bitcast.36), channel_id=1, source_target_pairs={{0,1},{1,0},{2,33},{3,32},{4,65},{5,64},{6,97},{7,96},{8,129},{9,1... | collective-permute-start | bytes 393224 | tf_op jit(solution)/shard_map/ppermute | solution.py:226
  19.3 40.4 %collective-permute-done = bf16[32,32,64]{2,0,1:T(8,128)(2,1)S(1)} collective-permute-done((bf16[32,32,64]{2,0,1:T(8,128)(2,1)S(1)}, bf16[32,32,64]{2,0,1:T(8,128)(2,1)S(1)}, u32[]{:S(2)}, u32[]{:S(2)}) %collective-permute-start) | collective-permute-done | bytes 131104 | tf_op jit(solution)/shard_map/ppermute | solution.py:226
  59.8 2.1 %collective-permute-done.1 = bf16[32,32,64]{2,0,1:T(8,128)(2,1)S(1)} collective-permute-done((bf16[32,32,64]{2,0,1:T(8,128)(2,1)S(1)}, bf16[32,32,64]{2,0,1:T(8,128)(2,1)S(1)}, u32[]{:S(2)}, u32[]{:S(2)}) %collective-permute-start.1) | collective-permute-done | bytes 131104 | tf_op jit(solution)/shard_map/ppermute | solution.py:226
  61.8 0.3 fusion.6
  62.1 0.0 copy-start
  62.1 0.1 maximum_bitcast_fusion
  62.2 0.2 fusion.2
  62.4 1.9 %collective-permute-start.2 = (bf16[32,2,32,64]{3,2,1,0:T(8,128)(2,1)S(1)}, bf16[32,2,32,64]{3,2,1,0:T(8,128)(2,1)S(1)}, u32[]{:S(2)}, u32[]{:S(2)}) collective-permute-start(bf16[32,2,32,64]{3,2,1,0:T(8,128)(2,1)S(1)} %get-tuple-element.7), channel_id=1, source_target_pairs={{0,32},{32,64},{64,96},{96,128},{128,160},{160,192},{192,224},{224... | collective-permute-start | bytes 786440 | tf_op jit(solution)/shard_map/ppermute | solution.py:184
  64.4 7.8 %collective-permute-start.3 = (bf16[32,2,32,64]{3,2,1,0:T(8,128)(2,1)S(1)}, bf16[32,2,32,64]{3,2,1,0:T(8,128)(2,1)S(1)}, u32[]{:S(2)}, u32[]{:S(2)}) collective-permute-start(bf16[32,2,32,64]{3,2,1,0:T(8,128)(2,1)S(1)} %get-tuple-element.8), channel_id=1, source_target_pairs={{32,0},{64,32},{96,64},{128,96},{160,128},{192,160},{224,192},{256... | collective-permute-start | bytes 786440 | tf_op jit(solution)/shard_map/ppermute | solution.py:185
  72.1 0.7 add_convert_fusion.refs_0_
  72.8 0.0 copy-done
  72.8 0.5 slice_bitcast_fusion
  73.3 0.0 collective-permute-done.2
  73.3 1.8 %collective-permute-done.3 = bf16[32,2,32,64]{3,2,1,0:T(8,128)(2,1)S(1)} collective-permute-done((bf16[32,2,32,64]{3,2,1,0:T(8,128)(2,1)S(1)}, bf16[32,2,32,64]{3,2,1,0:T(8,128)(2,1)S(1)}, u32[]{:S(2)}, u32[]{:S(2)}) %collective-permute-start.3) | collective-permute-done | bytes 262176 | tf_op jit(solution)/shard_map/ppermute | solution.py:185
  75.1 1.8 %pad_maximum_fusion.refs_2_ = bf16[128,2,32,64]{3,2,1,0:T(8,128)(2,1)} fusion(bf16[32,2,32,64]{3,2,1,0:T(8,128)(2,1)S(1)} %collective-permute-done.3, bf16[64,1,32,64]{3,2,1,0:T(8,128)(2,1)S(1)} %maximum_bitcast_fusion, bf16[64,1,32,64]{3,2,1,0:T(8,128)(2,1)S(1)} %bitcast.32, bf16[32,2,32,64]{3,2,1,0:T(8,128)(2,1)S(1)} %collective-permute-done.2), kind=kLoop, calls=%fused_computation | loop fusion | flops 1572864 | bytes 2097152 | tf_op jit(solution)/shard_map/concatenate | solution.py:191
  77.0 4.5 %shard_map.55.mid_ref = f32[96,32,64]{2,1,0:T(8,128)} custom-call(s32[2]{0:T(128)} %add_convert_fusion.refs_0_, s32[1,1,64]{2,1,0:T(1,128)} %get-tuple-element.14.refs_1_, bf16[128,2,32,64]{3,2,1,0:T(8,128)(2,1)} %pad_maximum_fusion.refs_2_), custom_call_target="tpu_custom_call" | custom-call | tf_op jit(solution)/shard_map/pallas_call | solution.py:170
  81.5 1.8 %fusion.12 = (f32[96,24,64]{2,1,0:T(8,128)S(1)}, f32[96,24,64]{2,1,0:T(8,128)S(1)}) fusion(f32[96,32,64]{2,1,0:T(8,128)} %shard_map.55.mid_ref), kind=kLoop, calls=%fused_computation.41 | loop fusion | bytes 2359296 | tf_op jit(solution)/shard_map/slice | solution.py:182
  83.3 0.4 copy.12
  83.7 7.5 %collective-permute-start.4 = (f32[96,24,64]{0,2,1:T(8,128)S(1)}, f32[96,24,64]{0,2,1:T(8,128)S(1)}, u32[]{:S(2)}, u32[]{:S(2)}) collective-permute-start(f32[96,24,64]{0,2,1:T(8,128)S(1)} %copy.12), channel_id=1, source_target_pairs={{0,1},{1,2},{2,3},{3,4},{4,5},{5,6},{6,7},{7,8},{8,9},{9,10},{10,1... | collective-permute-start | bytes 1769480 | tf_op jit(solution)/shard_map/ppermute | solution.py:184
  91.2 1.3 copy.13
  92.5 2.1 %collective-permute-start.5 = (f32[96,24,64]{0,2,1:T(8,128)}, f32[96,24,64]{0,2,1:T(8,128)S(1)}, u32[]{:S(2)}, u32[]{:S(2)}) collective-permute-start(f32[96,24,64]{0,2,1:T(8,128)} %copy.13), channel_id=1, source_target_pairs={{1,0},{2,1},{3,2},{4,3},{5,4},{6,5},{7,6},{8,7},{9,8},{10,9},{11,1... | collective-permute-start | bytes 1769480 | tf_op jit(solution)/shard_map/ppermute | solution.py:185
  94.6 0.6 add_convert_fusion.1.ends_ref
  95.2 13.3 %collective-permute-done.4 = f32[96,24,64]{0,2,1:T(8,128)S(1)} collective-permute-done((f32[96,24,64]{0,2,1:T(8,128)S(1)}, f32[96,24,64]{0,2,1:T(8,128)S(1)}, u32[]{:S(2)}, u32[]{:S(2)}) %collective-permute-start.4) | collective-permute-done | bytes 589856 | tf_op jit(solution)/shard_map/ppermute | solution.py:184
  108.5 1.4 %copy.14.left_ref = f32[96,24,64]{2,1,0:T(8,128)} copy(f32[96,24,64]{0,2,1:T(8,128)S(1)} %collective-permute-done.4) | data formatting | bytes 1179648 | tf_op jit(solution)/shard_map/ppermute | solution.py:184
  109.9 3.9 %collective-permute-done.5 = f32[96,24,64]{0,2,1:T(8,128)S(1)} collective-permute-done((f32[96,24,64]{0,2,1:T(8,128)}, f32[96,24,64]{0,2,1:T(8,128)S(1)}, u32[]{:S(2)}, u32[]{:S(2)}) %collective-permute-start.5) | collective-permute-done | bytes 589856 | tf_op jit(solution)/shard_map/ppermute | solution.py:185
  113.9 1.4 %copy.15.right_ref = f32[96,24,64]{2,1,0:T(8,128)} copy(f32[96,24,64]{0,2,1:T(8,128)S(1)} %collective-permute-done.5) | data formatting | bytes 1179648 | tf_op jit(solution)/shard_map/ppermute | solution.py:185
  115.3 12.4 %shard_map.56.refs_2_ = f32[96,32,64]{2,1,0:T(8,128)} custom-call(s32[2]{0:T(128)} %add_convert_fusion.1.ends_ref, s32[1,1,64]{2,1,0:T(1,128)} %get-tuple-element.13.depth_ref, f32[1,1,64]{2,1,0:T(1,128)} %bitcast.37, f32[96,24,64]{2,1,0:T(8,128)} %copy.14.left_ref, f32[96,32,64]{2,1,0:T(8,128)} %shard_map.55.mid_ref, f32[96,24,64]{2,1,0:T(8,128)} %copy.15.right_ref), custom_call_target="tpu_custom_call" | custom-call | tf_op jit(solution)/shard_map/pallas_call | solution.py:124
  127.7 3.3 %shard_map.57 = f32[64,32,64]{2,1,0:T(8,128)} custom-call(s32[2]{0:T(128)} %add_convert_fusion.refs_0_, s32[1,1,64]{2,1,0:T(1,128)} %get-tuple-element.14.refs_1_, f32[96,32,64]{2,1,0:T(8,128)} %shard_map.56.refs_2_), custom_call_target="tpu_custom_call" | custom-call | tf_op jit(solution)/shard_map/pallas_call | solution.py:170
  (3 shorter events, 0.1 us)
Async XLA Ops:
  2.9 56.9 %collective-permute-start = (bf16[32,32,64]{2,0,1:T(8,128)(2,1)S(1)}, bf16[32,32,64]{2,0,1:T(8,128)(2,1)S(1)}, u32[]{:S(2)}, u32[]{:S(2)}) collective-permute-start(bf16[32,32,64]{2,0,1:T(8,128)(2,1)S(1)} %bitcast.35), channel_id=1, source_target_pairs={{0,0},{1,1},{2,32},{3,33},{4,64},{5,65},{6,96},{7,97},{8,128},{9,1... | collective-permute-start | bytes 393224 | tf_op jit(solution)/shard_map/ppermute | solution.py:226
  17.4 44.5 %collective-permute-start.1 = (bf16[32,32,64]{2,0,1:T(8,128)(2,1)S(1)}, bf16[32,32,64]{2,0,1:T(8,128)(2,1)S(1)}, u32[]{:S(2)}, u32[]{:S(2)}) collective-permute-start(bf16[32,32,64]{2,0,1:T(8,128)(2,1)S(1)} %bitcast.36), channel_id=1, source_target_pairs={{0,1},{1,0},{2,33},{3,32},{4,65},{5,64},{6,97},{7,96},{8,129},{9,1... | collective-permute-start | bytes 393224 | tf_op jit(solution)/shard_map/ppermute | solution.py:226
  62.1 10.7 %copy-start = (s32[2,64]{1,0:T(2,128)S(1)}, s32[2,64]{1,0:T(2,128)}, u32[]{:S(2)}) copy-start(s32[2,64]{1,0:T(2,128)} %param.8) | copy-start | bytes 1540
  62.4 10.9 %collective-permute-start.2 = (bf16[32,2,32,64]{3,2,1,0:T(8,128)(2,1)S(1)}, bf16[32,2,32,64]{3,2,1,0:T(8,128)(2,1)S(1)}, u32[]{:S(2)}, u32[]{:S(2)}) collective-permute-start(bf16[32,2,32,64]{3,2,1,0:T(8,128)(2,1)S(1)} %get-tuple-element.7), channel_id=1, source_target_pairs={{0,32},{32,64},{64,96},{96,128},{128,160},{160,192},{192,224},{224... | collective-permute-start | bytes 786440 | tf_op jit(solution)/shard_map/ppermute | solution.py:184
  64.4 10.8 %collective-permute-start.3 = (bf16[32,2,32,64]{3,2,1,0:T(8,128)(2,1)S(1)}, bf16[32,2,32,64]{3,2,1,0:T(8,128)(2,1)S(1)}, u32[]{:S(2)}, u32[]{:S(2)}) collective-permute-start(bf16[32,2,32,64]{3,2,1,0:T(8,128)(2,1)S(1)} %get-tuple-element.8), channel_id=1, source_target_pairs={{32,0},{64,32},{96,64},{128,96},{160,128},{192,160},{224,192},{256... | collective-permute-start | bytes 786440 | tf_op jit(solution)/shard_map/ppermute | solution.py:185
  83.7 24.9 %collective-permute-start.4 = (f32[96,24,64]{0,2,1:T(8,128)S(1)}, f32[96,24,64]{0,2,1:T(8,128)S(1)}, u32[]{:S(2)}, u32[]{:S(2)}) collective-permute-start(f32[96,24,64]{0,2,1:T(8,128)S(1)} %copy.12), channel_id=1, source_target_pairs={{0,1},{1,2},{2,3},{3,4},{4,5},{5,6},{6,7},{7,8},{8,9},{9,10},{10,1... | collective-permute-start | bytes 1769480 | tf_op jit(solution)/shard_map/ppermute | solution.py:184
  92.5 21.4 %collective-permute-start.5 = (f32[96,24,64]{0,2,1:T(8,128)}, f32[96,24,64]{0,2,1:T(8,128)S(1)}, u32[]{:S(2)}, u32[]{:S(2)}) collective-permute-start(f32[96,24,64]{0,2,1:T(8,128)} %copy.13), channel_id=1, source_target_pairs={{1,0},{2,1},{3,2},{4,3},{5,4},{6,5},{7,6},{8,7},{9,8},{10,9},{11,1... | collective-permute-start | bytes 1769480 | tf_op jit(solution)/shard_map/ppermute | solution.py:185

commit v4 on v3

--- a/solution.py
+++ b/solution.py
@@ -10,6 +10,7 @@
 LEVELS = 3
 SRC_HALO = 16
 RCV_HALO = 24
+MIRROR_SPLIT = 4
 
 
 def split_pairs(field, stride):
@@ -223,7 +224,16 @@
                 part = (b % ratio + shift) % ratio
                 perm.append((a * rcv_count + b, (b // ratio) * rcv_count + a * ratio + part))
         send = lax.dynamic_index_in_dim(pieces, (own_part + shift) % ratio, axis=0, keepdims=False)
-        received.append(lax.ppermute(send, ("src", "rcv"), perm))
+        chunk = samples // MIRROR_SPLIT
+        received.append(
+            jnp.concatenate(
+                [
+                    lax.ppermute(send[:, :, k * chunk : (k + 1) * chunk], ("src", "rcv"), perm)
+                    for k in range(MIRROR_SPLIT)
+                ],
+                axis=2,
+            )
+        )
     received = jnp.stack(received)
     slots = []
     for slot in range(ratio):

time: 131 us -> 280 us (2.14)
  waiting for transfers between devices: 61.6 us -> 140 us
  starting transfers between devices: 35.6 us -> 104 us
    ppermute x2 -> x8, waiting for transfers between devices: 42.5 us -> 119 us  [body(): lax.ppermute(send[:, :, k * chunk:(k + 1) * chunk], ('src', 'rcv'), perm)]
    ppermute x2 -> x8, starting transfers between devices: 16.3 us -> 91.8 us  [body(): lax.ppermute(send[:, :, k * chunk:(k + 1) * chunk], ('src', 'rcv'), perm)]
    ppermute x2, starting transfers between devices: 9.44 us -> 3.84 us  [halos(): lax.ppermute(tail, axis_name, [(i, i + 1) for i in range(count - 1)])]
  transfers between devices with their start and end apart: 6 -> 12, of which waited for: 5 -> 12; matrix products, arithmetic and copies ran while one was open for 4% -> 2% of each run, Pallas kernels for 0% -> 0%
where the time goes in v4:
time: 280 us
  waiting for transfers between devices  140 us (50%)
  starting transfers between devices  104 us (37%)
  Pallas kernels  20.2 us (7%)
  local copies, waits for them, and re-layouts  8.36 us (3%)
  other arithmetic  5.82 us (2%)
    ppermute x8, waiting for transfers between devices, body(): lax.ppermute(send[:, :, k * chunk:(k + 1) * chunk], ('src', 'rcv'), perm)  119 us
    ppermute x8, starting transfers between devices, body(): lax.ppermute(send[:, :, k * chunk:(k + 1) * chunk], ('src', 'rcv'), perm)  91.8 us
    ppermute x2, waiting for transfers between devices, halos(): lax.ppermute(tail, axis_name, [(i, i + 1) for i in range(count - 1)])  15.5 us
    pallas_call x1, Pallas kernels, rcv_stage(): pl.pallas_call(functools.partial(_rcv_kernel, width=width), out_shape=jax...  12.4 us
    ppermute x2, starting transfers between devices, halos(): lax.ppermute(head, axis_name, [(i + 1, i) for i in range(count - 1)])  8.05 us
    pallas_call x2, Pallas kernels, lift_stage(): pl.pallas_call(kernel, out_shape=jax.ShapeDtypeStruct((out_rows, cols, sa...  7.8 us
    ppermute x2, waiting for transfers between devices, halos(): lax.ppermute(head, axis_name, [(i + 1, i) for i in range(count - 1)])  6.32 us
  transfers between devices with their start and end apart: 12, of which 12 were waited for; matrix products, arithmetic and copies ran while one was open for 2% of the time, Pallas kernels for 0%

profile of v4, /device:TPU:27, one launch (start us, length us, event | category | flops | bytes accessed | tf_op | source)
XLA Modules:
  0.0 279.7 jit_solution(2284609875973188702)
XLA Ops:
  0.0 0.9 fusion.7
  0.9 0.2 fusion.9
  1.2 1.5 fusion.1
  2.8 0.2 copy_bitcast_fusion
  3.0 1.0 fusion.13
  4.0 14.4 %collective-permute-start.4 = (bf16[32,32,16]{2,0,1:T(8,128)(2,1)}, bf16[32,32,16]{2,0,1:T(8,128)(2,1)S(1)}, u32[]{:S(2)}, u32[]{:S(2)}) collective-permute-start(bf16[32,32,16]{2,0,1:T(8,128)(2,1)} %get-tuple-element.13), channel_id=1, source_target_pairs={{0,1},{1,0},{2,33},{3,32},{4,65},{5,64},{6,97},{7,96},{8,129},{9,1... | collective-permute-start | bytes 98312 | tf_op jit(solution)/shard_map/ppermute | solution.py:231
  18.4 1.9 collective-permute-start.7
  20.3 7.9 %collective-permute-start.6 = (bf16[32,32,16]{2,0,1:T(8,128)(2,1)S(1)}, bf16[32,32,16]{2,0,1:T(8,128)(2,1)S(1)}, u32[]{:S(2)}, u32[]{:S(2)}) collective-permute-start(bf16[32,32,16]{2,0,1:T(8,128)(2,1)S(1)} %get-tuple-element.15), channel_id=1, source_target_pairs={{0,1},{1,0},{2,33},{3,32},{4,65},{5,64},{6,97},{7,96},{8,129},{9,1... | collective-permute-start | bytes 98312 | tf_op jit(solution)/shard_map/ppermute | solution.py:231
  28.2 1.9 collective-permute-start.5
  30.1 0.3 fusion.14
  30.4 11.4 %collective-permute-start = (bf16[32,32,16]{2,0,1:T(8,128)(2,1)S(1)}, bf16[32,32,16]{2,0,1:T(8,128)(2,1)S(1)}, u32[]{:S(2)}, u32[]{:S(2)}) collective-permute-start(bf16[32,32,16]{2,0,1:T(8,128)(2,1)S(1)} %get-tuple-element.17), channel_id=1, source_target_pairs={{0,0},{1,1},{2,32},{3,33},{4,64},{5,65},{6,96},{7,97},{8,128},{9,1... | collective-permute-start | bytes 98312 | tf_op jit(solution)/shard_map/ppermute | solution.py:231
  41.8 8.1 %collective-permute-done.4 = bf16[32,32,16]{2,0,1:T(8,128)(2,1)S(1)} collective-permute-done((bf16[32,32,16]{2,0,1:T(8,128)(2,1)}, bf16[32,32,16]{2,0,1:T(8,128)(2,1)S(1)}, u32[]{:S(2)}, u32[]{:S(2)}) %collective-permute-start.4) | collective-permute-done | bytes 32800 | tf_op jit(solution)/shard_map/ppermute | solution.py:231
  49.9 24.9 %collective-permute-start.3 = (bf16[32,32,16]{2,0,1:T(8,128)(2,1)S(1)}, bf16[32,32,16]{2,0,1:T(8,128)(2,1)S(1)}, u32[]{:S(2)}, u32[]{:S(2)}) collective-permute-start(bf16[32,32,16]{2,0,1:T(8,128)(2,1)S(1)} %get-tuple-element.18), channel_id=1, source_target_pairs={{0,0},{1,1},{2,32},{3,33},{4,64},{5,65},{6,96},{7,97},{8,128},{9,1... | collective-permute-start | bytes 98312 | tf_op jit(solution)/shard_map/ppermute | solution.py:231
  74.9 1.7 collective-permute-done.7
  76.6 18.9 %collective-permute-start.2 = (bf16[32,32,16]{2,0,1:T(8,128)(2,1)S(1)}, bf16[32,32,16]{2,0,1:T(8,128)(2,1)S(1)}, u32[]{:S(2)}, u32[]{:S(2)}) collective-permute-start(bf16[32,32,16]{2,0,1:T(8,128)(2,1)S(1)} %get-tuple-element.19), channel_id=1, source_target_pairs={{0,0},{1,1},{2,32},{3,33},{4,64},{5,65},{6,96},{7,97},{8,128},{9,1... | collective-permute-start | bytes 98312 | tf_op jit(solution)/shard_map/ppermute | solution.py:231
  95.5 12.3 %collective-permute-done.6 = bf16[32,32,16]{2,0,1:T(8,128)(2,1)S(1)} collective-permute-done((bf16[32,32,16]{2,0,1:T(8,128)(2,1)S(1)}, bf16[32,32,16]{2,0,1:T(8,128)(2,1)S(1)}, u32[]{:S(2)}, u32[]{:S(2)}) %collective-permute-start.6) | collective-permute-done | bytes 32800 | tf_op jit(solution)/shard_map/ppermute | solution.py:231
  107.8 10.4 %collective-permute-start.1 = (bf16[32,32,16]{2,0,1:T(8,128)(2,1)S(1)}, bf16[32,32,16]{2,0,1:T(8,128)(2,1)S(1)}, u32[]{:S(2)}, u32[]{:S(2)}) collective-permute-start(bf16[32,32,16]{2,0,1:T(8,128)(2,1)S(1)} %get-tuple-element.20), channel_id=1, source_target_pairs={{0,0},{1,1},{2,32},{3,33},{4,64},{5,65},{6,96},{7,97},{8,128},{9,1... | collective-permute-start | bytes 98312 | tf_op jit(solution)/shard_map/ppermute | solution.py:231
  118.2 17.2 %collective-permute-done.5 = bf16[32,32,16]{2,0,1:T(8,128)(2,1)S(1)} collective-permute-done((bf16[32,32,16]{2,0,1:T(8,128)(2,1)S(1)}, bf16[32,32,16]{2,0,1:T(8,128)(2,1)S(1)}, u32[]{:S(2)}, u32[]{:S(2)}) %collective-permute-start.5) | collective-permute-done | bytes 32800 | tf_op jit(solution)/shard_map/ppermute | solution.py:231
  135.5 0.4 maximum_bitcast_fusion.2
  135.8 31.9 %collective-permute-done = bf16[32,32,16]{2,0,1:T(8,128)(2,1)S(1)} collective-permute-done((bf16[32,32,16]{2,0,1:T(8,128)(2,1)S(1)}, bf16[32,32,16]{2,0,1:T(8,128)(2,1)S(1)}, u32[]{:S(2)}, u32[]{:S(2)}) %collective-permute-start) | collective-permute-done | bytes 32800 | tf_op jit(solution)/shard_map/ppermute | solution.py:231
  167.7 25.5 %collective-permute-done.3 = bf16[32,32,16]{2,0,1:T(8,128)(2,1)S(1)} collective-permute-done((bf16[32,32,16]{2,0,1:T(8,128)(2,1)S(1)}, bf16[32,32,16]{2,0,1:T(8,128)(2,1)S(1)}, u32[]{:S(2)}, u32[]{:S(2)}) %collective-permute-start.3) | collective-permute-done | bytes 32800 | tf_op jit(solution)/shard_map/ppermute | solution.py:231
  193.3 16.9 %collective-permute-done.2 = bf16[32,32,16]{2,0,1:T(8,128)(2,1)S(1)} collective-permute-done((bf16[32,32,16]{2,0,1:T(8,128)(2,1)S(1)}, bf16[32,32,16]{2,0,1:T(8,128)(2,1)S(1)}, u32[]{:S(2)}, u32[]{:S(2)}) %collective-permute-start.2) | collective-permute-done | bytes 32800 | tf_op jit(solution)/shard_map/ppermute | solution.py:231
  210.2 4.8 %collective-permute-done.1 = bf16[32,32,16]{2,0,1:T(8,128)(2,1)S(1)} collective-permute-done((bf16[32,32,16]{2,0,1:T(8,128)(2,1)S(1)}, bf16[32,32,16]{2,0,1:T(8,128)(2,1)S(1)}, u32[]{:S(2)}, u32[]{:S(2)}) %collective-permute-start.1) | collective-permute-done | bytes 32800 | tf_op jit(solution)/shard_map/ppermute | solution.py:231
  215.0 0.4 maximum_bitcast_fusion.1
  215.4 0.3 fusion.6
  215.6 0.0 copy-start
  215.7 0.1 maximum_bitcast_fusion
  215.8 0.2 fusion.2
  216.0 1.9 collective-permute-start.8
  217.9 2.4 collective-permute-start.9
  220.3 0.6 add_convert_fusion.refs_0_
  220.9 0.0 copy-done
  220.9 0.6 slice_bitcast_fusion
  221.5 2.5 collective-permute-done.8
  224.0 4.4 %collective-permute-done.9 = bf16[32,2,32,64]{3,2,1,0:T(8,128)(2,1)S(1)} collective-permute-done((bf16[32,2,32,64]{3,2,1,0:T(8,128)(2,1)S(1)}, bf16[32,2,32,64]{3,2,1,0:T(8,128)(2,1)S(1)}, u32[]{:S(2)}, u32[]{:S(2)}) %collective-permute-start.9) | collective-permute-done | bytes 262176 | tf_op jit(solution)/shard_map/ppermute | solution.py:186
  228.4 1.8 pad_maximum_fusion.refs_2_
  230.2 4.5 %shard_map.55.mid_ref = f32[96,32,64]{2,1,0:T(8,128)} custom-call(s32[2]{0:T(128)} %add_convert_fusion.refs_0_, s32[1,1,64]{2,1,0:T(1,128)} %get-tuple-element.22.refs_1_, bf16[128,2,32,64]{3,2,1,0:T(8,128)(2,1)} %pad_maximum_fusion.refs_2_), custom_call_target="tpu_custom_call" | custom-call | tf_op jit(solution)/shard_map/pallas_call | solution.py:171
  234.7 1.8 fusion.12
  236.5 0.4 copy.12
  236.9 1.9 collective-permute-start.10
  238.8 1.3 copy.13
  240.1 5.6 %collective-permute-start.11 = (f32[96,24,64]{0,2,1:T(8,128)}, f32[96,24,64]{0,2,1:T(8,128)S(1)}, u32[]{:S(2)}, u32[]{:S(2)}) collective-permute-start(f32[96,24,64]{0,2,1:T(8,128)} %copy.13), channel_id=1, source_target_pairs={{1,0},{2,1},{3,2},{4,3},{5,4},{6,5},{7,6},{8,7},{9,8},{10,9},{11,1... | collective-permute-start | bytes 1769480 | tf_op jit(solution)/shard_map/ppermute | solution.py:186
  245.7 0.6 add_convert_fusion.1.ends_ref
  246.3 12.9 %collective-permute-done.10 = f32[96,24,64]{0,2,1:T(8,128)S(1)} collective-permute-done((f32[96,24,64]{0,2,1:T(8,128)S(1)}, f32[96,24,64]{0,2,1:T(8,128)S(1)}, u32[]{:S(2)}, u32[]{:S(2)}) %collective-permute-start.10) | collective-permute-done | bytes 589856 | tf_op jit(solution)/shard_map/ppermute | solution.py:185
  259.2 1.4 copy.14.left_ref
  260.6 1.9 collective-permute-done.11
  262.5 1.4 copy.15.right_ref
  264.0 12.4 %shard_map.56.refs_2_ = f32[96,32,64]{2,1,0:T(8,128)} custom-call(s32[2]{0:T(128)} %add_convert_fusion.1.ends_ref, s32[1,1,64]{2,1,0:T(1,128)} %get-tuple-element.21.depth_ref, f32[1,1,64]{2,1,0:T(1,128)} %bitcast.33, f32[96,24,64]{2,1,0:T(8,128)} %copy.14.left_ref, f32[96,32,64]{2,1,0:T(8,128)} %shard_map.55.mid_ref, f32[96,24,64]{2,1,0:T(8,128)} %copy.15.right_ref), custom_call_target="tpu_custom_call" | custom-call | tf_op jit(solution)/shard_map/pallas_call | solution.py:125
  276.4 3.3 %shard_map.57 = f32[64,32,64]{2,1,0:T(8,128)} custom-call(s32[2]{0:T(128)} %add_convert_fusion.refs_0_, s32[1,1,64]{2,1,0:T(1,128)} %get-tuple-element.22.refs_1_, f32[96,32,64]{2,1,0:T(8,128)} %shard_map.56.refs_2_), custom_call_target="tpu_custom_call" | custom-call | tf_op jit(solution)/shard_map/pallas_call | solution.py:171
  (3 shorter events, 0.1 us)
Async XLA Ops:
  4.0 46.0 %collective-permute-start.4 = (bf16[32,32,16]{2,0,1:T(8,128)(2,1)}, bf16[32,32,16]{2,0,1:T(8,128)(2,1)S(1)}, u32[]{:S(2)}, u32[]{:S(2)}) collective-permute-start(bf16[32,32,16]{2,0,1:T(8,128)(2,1)} %get-tuple-element.13), channel_id=1, source_target_pairs={{0,1},{1,0},{2,33},{3,32},{4,65},{5,64},{6,97},{7,96},{8,129},{9,1... | collective-permute-start | bytes 98312 | tf_op jit(solution)/shard_map/ppermute | solution.py:231
  18.4 58.3 %collective-permute-start.7 = (bf16[32,32,16]{2,0,1:T(8,128)(2,1)}, bf16[32,32,16]{2,0,1:T(8,128)(2,1)S(1)}, u32[]{:S(2)}, u32[]{:S(2)}) collective-permute-start(bf16[32,32,16]{2,0,1:T(8,128)(2,1)} %get-tuple-element.14), channel_id=1, source_target_pairs={{0,1},{1,0},{2,33},{3,32},{4,65},{5,64},{6,97},{7,96},{8,129},{9,1... | collective-permute-start | bytes 98312 | tf_op jit(solution)/shard_map/ppermute | solution.py:231
  20.3 87.6 %collective-permute-start.6 = (bf16[32,32,16]{2,0,1:T(8,128)(2,1)S(1)}, bf16[32,32,16]{2,0,1:T(8,128)(2,1)S(1)}, u32[]{:S(2)}, u32[]{:S(2)}) collective-permute-start(bf16[32,32,16]{2,0,1:T(8,128)(2,1)S(1)} %get-tuple-element.15), channel_id=1, source_target_pairs={{0,1},{1,0},{2,33},{3,32},{4,65},{5,64},{6,97},{7,96},{8,129},{9,1... | collective-permute-start | bytes 98312 | tf_op jit(solution)/shard_map/ppermute | solution.py:231
  28.2 107.3 %collective-permute-start.5 = (bf16[32,32,16]{2,0,1:T(8,128)(2,1)S(1)}, bf16[32,32,16]{2,0,1:T(8,128)(2,1)S(1)}, u32[]{:S(2)}, u32[]{:S(2)}) collective-permute-start(bf16[32,32,16]{2,0,1:T(8,128)(2,1)S(1)} %get-tuple-element.16), channel_id=1, source_target_pairs={{0,1},{1,0},{2,33},{3,32},{4,65},{5,64},{6,97},{7,96},{8,129},{9,1... | collective-permute-start | bytes 98312 | tf_op jit(solution)/shard_map/ppermute | solution.py:231
  30.4 137.4 %collective-permute-start = (bf16[32,32,16]{2,0,1:T(8,128)(2,1)S(1)}, bf16[32,32,16]{2,0,1:T(8,128)(2,1)S(1)}, u32[]{:S(2)}, u32[]{:S(2)}) collective-permute-start(bf16[32,32,16]{2,0,1:T(8,128)(2,1)S(1)} %get-tuple-element.17), channel_id=1, source_target_pairs={{0,0},{1,1},{2,32},{3,33},{4,64},{5,65},{6,96},{7,97},{8,128},{9,1... | collective-permute-start | bytes 98312 | tf_op jit(solution)/shard_map/ppermute | solution.py:231
  49.9 143.3 %collective-permute-start.3 = (bf16[32,32,16]{2,0,1:T(8,128)(2,1)S(1)}, bf16[32,32,16]{2,0,1:T(8,128)(2,1)S(1)}, u32[]{:S(2)}, u32[]{:S(2)}) collective-permute-start(bf16[32,32,16]{2,0,1:T(8,128)(2,1)S(1)} %get-tuple-element.18), channel_id=1, source_target_pairs={{0,0},{1,1},{2,32},{3,33},{4,64},{5,65},{6,96},{7,97},{8,128},{9,1... | collective-permute-start | bytes 98312 | tf_op jit(solution)/shard_map/ppermute | solution.py:231
  76.6 133.6 %collective-permute-start.2 = (bf16[32,32,16]{2,0,1:T(8,128)(2,1)S(1)}, bf16[32,32,16]{2,0,1:T(8,128)(2,1)S(1)}, u32[]{:S(2)}, u32[]{:S(2)}) collective-permute-start(bf16[32,32,16]{2,0,1:T(8,128)(2,1)S(1)} %get-tuple-element.19), channel_id=1, source_target_pairs={{0,0},{1,1},{2,32},{3,33},{4,64},{5,65},{6,96},{7,97},{8,128},{9,1... | collective-permute-start | bytes 98312 | tf_op jit(solution)/shard_map/ppermute | solution.py:231
  107.8 107.2 %collective-permute-start.1 = (bf16[32,32,16]{2,0,1:T(8,128)(2,1)S(1)}, bf16[32,32,16]{2,0,1:T(8,128)(2,1)S(1)}, u32[]{:S(2)}, u32[]{:S(2)}) collective-permute-start(bf16[32,32,16]{2,0,1:T(8,128)(2,1)S(1)} %get-tuple-element.20), channel_id=1, source_target_pairs={{0,0},{1,1},{2,32},{3,33},{4,64},{5,65},{6,96},{7,97},{8,128},{9,1... | collective-permute-start | bytes 98312 | tf_op jit(solution)/shard_map/ppermute | solution.py:231
  215.6 5.3 %copy-start = (s32[2,64]{1,0:T(2,128)S(1)}, s32[2,64]{1,0:T(2,128)}, u32[]{:S(2)}) copy-start(s32[2,64]{1,0:T(2,128)} %param.8) | copy-start | bytes 1540
  216.0 8.0 %collective-permute-start.8 = (bf16[32,2,32,64]{3,2,1,0:T(8,128)(2,1)S(1)}, bf16[32,2,32,64]{3,2,1,0:T(8,128)(2,1)S(1)}, u32[]{:S(2)}, u32[]{:S(2)}) collective-permute-start(bf16[32,2,32,64]{3,2,1,0:T(8,128)(2,1)S(1)} %get-tuple-element.7), channel_id=1, source_target_pairs={{0,32},{32,64},{64,96},{96,128},{128,160},{160,192},{192,224},{224... | collective-permute-start | bytes 786440 | tf_op jit(solution)/shard_map/ppermute | solution.py:185
  217.9 10.5 %collective-permute-start.9 = (bf16[32,2,32,64]{3,2,1,0:T(8,128)(2,1)S(1)}, bf16[32,2,32,64]{3,2,1,0:T(8,128)(2,1)S(1)}, u32[]{:S(2)}, u32[]{:S(2)}) collective-permute-start(bf16[32,2,32,64]{3,2,1,0:T(8,128)(2,1)S(1)} %get-tuple-element.8), channel_id=1, source_target_pairs={{32,0},{64,32},{96,64},{128,96},{160,128},{192,160},{224,192},{256... | collective-permute-start | bytes 786440 | tf_op jit(solution)/shard_map/ppermute | solution.py:186
  236.9 22.3 %collective-permute-start.10 = (f32[96,24,64]{0,2,1:T(8,128)S(1)}, f32[96,24,64]{0,2,1:T(8,128)S(1)}, u32[]{:S(2)}, u32[]{:S(2)}) collective-permute-start(f32[96,24,64]{0,2,1:T(8,128)S(1)} %copy.12), channel_id=1, source_target_pairs={{0,1},{1,2},{2,3},{3,4},{4,5},{5,6},{6,7},{7,8},{8,9},{9,10},{10,1... | collective-permute-start | bytes 1769480 | tf_op jit(solution)/shard_map/ppermute | solution.py:185
  240.1 22.5 %collective-permute-start.11 = (f32[96,24,64]{0,2,1:T(8,128)}, f32[96,24,64]{0,2,1:T(8,128)S(1)}, u32[]{:S(2)}, u32[]{:S(2)}) collective-permute-start(f32[96,24,64]{0,2,1:T(8,128)} %copy.13), channel_id=1, source_target_pairs={{1,0},{2,1},{3,2},{4,3},{5,4},{6,5},{7,6},{8,7},{9,8},{10,9},{11,1... | collective-permute-start | bytes 1769480 | tf_op jit(solution)/shard_map/ppermute | solution.py:186

commit v5 on v3

--- a/solution.py
+++ b/solution.py
@@ -212,24 +212,23 @@
         est_float + local_mask[:, :, None] * (observed.astype(jnp.float32) - est_float)
     ).astype(jnp.bfloat16)
 
-    ratio = rcv_count // src_count
-    pieces = merged.reshape(ratio, col_count, col_count, samples)
-    own_part = rcv_index % ratio
-    received = []
-    for shift in range(ratio):
-        perm = []
-        for a in range(src_count):
-            for b in range(rcv_count):
-                part = (b % ratio + shift) % ratio
-                perm.append((a * rcv_count + b, (b // ratio) * rcv_count + a * ratio + part))
-        send = lax.dynamic_index_in_dim(pieces, (own_part + shift) % ratio, axis=0, keepdims=False)
-        received.append(lax.ppermute(send, ("src", "rcv"), perm))
-    received = jnp.stack(received)
-    slots = []
-    for slot in range(ratio):
-        got = lax.dynamic_index_in_dim(received, (own_part - slot) % ratio, axis=0, keepdims=False)
-        slots.append(jnp.transpose(got, (1, 0, 2)))
-    mirror = jnp.concatenate(slots, axis=0)
+    assert rcv_count == 2 * src_count and row_count == 2 * col_count
+    pieces = merged.reshape(2, col_count, col_count, samples)
+    own_part = rcv_index % 2
+    perm = [
+        (a * rcv_count + b, (b // 2) * rcv_count + 2 * a + b % 2)
+        for a in range(src_count)
+        for b in range(rcv_count)
+    ]
+    block = lax.ppermute(pieces, ("src", "rcv"), perm)
+    keep = jnp.where(own_part == 0, block[0], block[1])
+    give = jnp.where(own_part == 0, block[1], block[0])
+    got = lax.ppermute(give, "rcv", [(b, b ^ 1) for b in range(rcv_count)])
+    first = jnp.where(own_part == 0, keep, got)
+    second = jnp.where(own_part == 0, got, keep)
+    mirror = jnp.concatenate(
+        [jnp.transpose(first, (1, 0, 2)), jnp.transpose(second, (1, 0, 2))], axis=0
+    )
     mirror_halo = 2 * SRC_HALO
     terms = extend(jnp.stack([merged, mirror], axis=1), "src", 0, mirror_halo)
 

time: 131 us -> 145 us (1.11)
  the two profiles are of different devices: /device:TPU:27 before, /device:TPU:31 now
where the time goes in v5:
time: 145 us; the launch traced here: 144 us
  waiting for transfers between devices  68.8 us (47%)
  starting transfers between devices  42 us (29%)
  Pallas kernels  20.2 us (14%)
  local copies, waits for them, and re-layouts  7.07 us (5%)
  other arithmetic  4.98 us (3%)
    ppermute x1, waiting for transfers between devices, body(): block = lax.ppermute(pieces, ('src', 'rcv'), perm)  44 us
    ppermute x2, starting transfers between devices, halos(): lax.ppermute(head, axis_name, [(i + 1, i) for i in range(count - 1)])  16.8 us
    ppermute x1, starting transfers between devices, body(): block = lax.ppermute(pieces, ('src', 'rcv'), perm)  13.8 us
    pallas_call x1, Pallas kernels, rcv_stage(): pl.pallas_call(functools.partial(_rcv_kernel, width=width), out_shape=jax...  12.5 us
    ppermute x2, waiting for transfers between devices, halos(): lax.ppermute(head, axis_name, [(i + 1, i) for i in range(count - 1)])  12.1 us
    pallas_call x2, Pallas kernels, lift_stage(): pl.pallas_call(kernel, out_shape=jax.ShapeDtypeStruct((out_rows, cols, sa...  7.79 us
    ppermute x2, waiting for transfers between devices, halos(): lax.ppermute(tail, axis_name, [(i, i + 1) for i in range(count - 1)])  6.93 us
    ppermute x1, starting transfers between devices, body(): got = lax.ppermute(give, 'rcv', [(b, b ^ 1) for b in range(rcv_count)])  6.42 us
  transfers between devices with their start and end apart: 6, of which 6 were waited for; matrix products, arithmetic and copies ran while one was open for 3% of the time, Pallas kernels for 0%

profile of v5, /device:TPU:31, one launch (start us, length us, event | category | flops | bytes accessed | tf_op | source)
XLA Modules:
  0.0 144.4 jit_solution(7345751039215308471)
XLA Ops:
  0.0 0.9 fusion.5
  0.9 0.3 fusion.7
  1.2 1.5 %fusion.1 = bf16[64,32,64]{2,1,0:T(8,128)(2,1)S(1)} fusion(bf16[64,32,64]{2,1,0:T(8,128)(2,1)} %param.6, bf16[64,32,64]{2,1,0:T(8,128)(2,1)} %param.5, f32[64,32]{1,0:T(8,128)S(1)} %fusion.7), kind=kLoop, calls=%fused_computation.4 | loop fusion | flops 786432 | bytes 794624 | tf_op jit(solution)/shard_map/convert_element_type | solution.py:213
  2.7 0.2 copy.10
  2.9 13.8 %collective-permute-start = (bf16[2,32,32,64]{3,1,2,0:T(8,128)(2,1)S(1)}, bf16[2,32,32,64]{3,1,2,0:T(8,128)(2,1)S(1)}, u32[]{:S(2)}, u32[]{:S(2)}) collective-permute-start(bf16[2,32,32,64]{3,1,2,0:T(8,128)(2,1)S(1)} %copy.10), channel_id=1, source_target_pairs={{0,0},{1,1},{2,32},{3,33},{4,64},{5,65},{6,96},{7,97},{8,128},{9,1... | collective-permute-start | bytes 786440 | tf_op jit(solution)/shard_map/ppermute | solution.py:223
  16.8 44.0 %collective-permute-done = bf16[2,32,32,64]{3,1,2,0:T(8,128)(2,1)S(1)} collective-permute-done((bf16[2,32,32,64]{3,1,2,0:T(8,128)(2,1)S(1)}, bf16[2,32,32,64]{3,1,2,0:T(8,128)(2,1)S(1)}, u32[]{:S(2)}, u32[]{:S(2)}) %collective-permute-start) | collective-permute-done | bytes 262176 | tf_op jit(solution)/shard_map/ppermute | solution.py:223
  60.9 6.4 %collective-permute-start.1 = (bf16[32,32,64]{2,0,1:T(8,128)(2,1)S(1)}, bf16[32,32,64]{2,0,1:T(8,128)(2,1)S(1)}, u32[]{:S(2)}, u32[]{:S(2)}) collective-permute-start(bf16[32,32,64]{2,0,1:T(8,128)(2,1)S(1)} %select_bitcast_fusion), channel_id=1, source_target_pairs={{0,1},{1,0},{2,3},{3,2},{4,5},{5,4},{6,7},{7,6},{8,9},{9,8},{10,11... | collective-permute-start | bytes 393224 | tf_op jit(solution)/shard_map/ppermute | solution.py:226
  67.3 5.8 %collective-permute-done.1 = bf16[32,32,64]{2,0,1:T(8,128)(2,1)S(1)} collective-permute-done((bf16[32,32,64]{2,0,1:T(8,128)(2,1)S(1)}, bf16[32,32,64]{2,0,1:T(8,128)(2,1)S(1)}, u32[]{:S(2)}, u32[]{:S(2)}) %collective-permute-start.1) | collective-permute-done | bytes 131104 | tf_op jit(solution)/shard_map/ppermute | solution.py:226
  73.1 0.0 copy-start
  73.1 0.1 maximum_bitcast_fusion
  73.3 0.2 fusion.2
  73.5 1.9 %collective-permute-start.2 = (bf16[32,2,32,64]{3,2,1,0:T(8,128)(2,1)S(1)}, bf16[32,2,32,64]{3,2,1,0:T(8,128)(2,1)S(1)}, u32[]{:S(2)}, u32[]{:S(2)}) collective-permute-start(bf16[32,2,32,64]{3,2,1,0:T(8,128)(2,1)S(1)} %get-tuple-element.7), channel_id=1, source_target_pairs={{0,32},{32,64},{64,96},{96,128},{128,160},{160,192},{192,224},{224... | collective-permute-start | bytes 786440 | tf_op jit(solution)/shard_map/ppermute | solution.py:184
  75.4 3.4 %collective-permute-start.3 = (bf16[32,2,32,64]{3,2,1,0:T(8,128)(2,1)S(1)}, bf16[32,2,32,64]{3,2,1,0:T(8,128)(2,1)S(1)}, u32[]{:S(2)}, u32[]{:S(2)}) collective-permute-start(bf16[32,2,32,64]{3,2,1,0:T(8,128)(2,1)S(1)} %get-tuple-element.8), channel_id=1, source_target_pairs={{32,0},{64,32},{96,64},{128,96},{160,128},{192,160},{224,192},{256... | collective-permute-start | bytes 786440 | tf_op jit(solution)/shard_map/ppermute | solution.py:185
  78.8 0.6 add_convert_fusion.refs_0_
  79.4 0.0 copy-done
  79.4 0.6 slice_bitcast_fusion
  80.0 1.5 %collective-permute-done.2 = bf16[32,2,32,64]{3,2,1,0:T(8,128)(2,1)S(1)} collective-permute-done((bf16[32,2,32,64]{3,2,1,0:T(8,128)(2,1)S(1)}, bf16[32,2,32,64]{3,2,1,0:T(8,128)(2,1)S(1)}, u32[]{:S(2)}, u32[]{:S(2)}) %collective-permute-start.2) | collective-permute-done | bytes 262176 | tf_op jit(solution)/shard_map/ppermute | solution.py:184
  81.5 10.4 %collective-permute-done.3 = bf16[32,2,32,64]{3,2,1,0:T(8,128)(2,1)S(1)} collective-permute-done((bf16[32,2,32,64]{3,2,1,0:T(8,128)(2,1)S(1)}, bf16[32,2,32,64]{3,2,1,0:T(8,128)(2,1)S(1)}, u32[]{:S(2)}, u32[]{:S(2)}) %collective-permute-start.3) | collective-permute-done | bytes 262176 | tf_op jit(solution)/shard_map/ppermute | solution.py:185
  91.9 1.8 %pad_maximum_fusion.refs_2_ = bf16[128,2,32,64]{3,2,1,0:T(8,128)(2,1)} fusion(bf16[32,2,32,64]{3,2,1,0:T(8,128)(2,1)S(1)} %collective-permute-done.3, bf16[64,1,32,64]{3,2,1,0:T(8,128)(2,1)S(1)} %maximum_bitcast_fusion, bf16[64,1,32,64]{3,2,1,0:T(8,128)(2,1)S(1)} %bitcast.29, bf16[32,2,32,64]{3,2,1,0:T(8,128)(2,1)S(1)} %collective-permute-done.2), kind=kLoop, calls=%fused_computation | loop fusion | flops 1572864 | bytes 2097152 | tf_op jit(solution)/shard_map/concatenate | solution.py:191
  93.7 4.5 %shard_map.55.mid_ref = f32[96,32,64]{2,1,0:T(8,128)} custom-call(s32[2]{0:T(128)} %add_convert_fusion.refs_0_, s32[1,1,64]{2,1,0:T(1,128)} %get-tuple-element.12.refs_1_, bf16[128,2,32,64]{3,2,1,0:T(8,128)(2,1)} %pad_maximum_fusion.refs_2_), custom_call_target="tpu_custom_call" | custom-call | tf_op jit(solution)/shard_map/pallas_call | solution.py:170
  98.2 1.8 %fusion.10 = (f32[96,24,64]{2,1,0:T(8,128)S(1)}, f32[96,24,64]{2,1,0:T(8,128)S(1)}) fusion(f32[96,32,64]{2,1,0:T(8,128)} %shard_map.55.mid_ref), kind=kLoop, calls=%fused_computation.35 | loop fusion | bytes 2359296 | tf_op jit(solution)/shard_map/slice | solution.py:182
  100.1 0.4 copy.11
  100.4 3.0 %collective-permute-start.4 = (f32[96,24,64]{0,2,1:T(8,128)S(1)}, f32[96,24,64]{0,2,1:T(8,128)S(1)}, u32[]{:S(2)}, u32[]{:S(2)}) collective-permute-start(f32[96,24,64]{0,2,1:T(8,128)S(1)} %copy.11), channel_id=1, source_target_pairs={{0,1},{1,2},{2,3},{3,4},{4,5},{5,6},{6,7},{7,8},{8,9},{9,10},{10,1... | collective-permute-start | bytes 1769480 | tf_op jit(solution)/shard_map/ppermute | solution.py:184
  103.5 1.3 copy.12
  104.8 13.4 %collective-permute-start.5 = (f32[96,24,64]{0,2,1:T(8,128)}, f32[96,24,64]{0,2,1:T(8,128)S(1)}, u32[]{:S(2)}, u32[]{:S(2)}) collective-permute-start(f32[96,24,64]{0,2,1:T(8,128)} %copy.12), channel_id=1, source_target_pairs={{1,0},{2,1},{3,2},{4,3},{5,4},{6,5},{7,6},{8,7},{9,8},{10,9},{11,1... | collective-permute-start | bytes 1769480 | tf_op jit(solution)/shard_map/ppermute | solution.py:185
  118.2 0.6 add_convert_fusion.1.ends_ref
  118.8 5.4 %collective-permute-done.4 = f32[96,24,64]{0,2,1:T(8,128)S(1)} collective-permute-done((f32[96,24,64]{0,2,1:T(8,128)S(1)}, f32[96,24,64]{0,2,1:T(8,128)S(1)}, u32[]{:S(2)}, u32[]{:S(2)}) %collective-permute-start.4) | collective-permute-done | bytes 589856 | tf_op jit(solution)/shard_map/ppermute | solution.py:184
  124.2 1.4 copy.13.left_ref
  125.6 1.6 %collective-permute-done.5 = f32[96,24,64]{0,2,1:T(8,128)S(1)} collective-permute-done((f32[96,24,64]{0,2,1:T(8,128)}, f32[96,24,64]{0,2,1:T(8,128)S(1)}, u32[]{:S(2)}, u32[]{:S(2)}) %collective-permute-start.5) | collective-permute-done | bytes 589856 | tf_op jit(solution)/shard_map/ppermute | solution.py:185
  127.3 1.4 copy.14.right_ref
  128.7 12.5 %shard_map.56.refs_2_ = f32[96,32,64]{2,1,0:T(8,128)} custom-call(s32[2]{0:T(128)} %add_convert_fusion.1.ends_ref, s32[1,1,64]{2,1,0:T(1,128)} %get-tuple-element.11.depth_ref, f32[1,1,64]{2,1,0:T(1,128)} %bitcast.30, f32[96,24,64]{2,1,0:T(8,128)} %copy.13.left_ref, f32[96,32,64]{2,1,0:T(8,128)} %shard_map.55.mid_ref, f32[96,24,64]{2,1,0:T(8,128)} %copy.14.right_ref), custom_call_target="tpu_custom_call" | custom-call | tf_op jit(solution)/shard_map/pallas_call | solution.py:124
  141.1 3.3 %shard_map.57 = f32[64,32,64]{2,1,0:T(8,128)} custom-call(s32[2]{0:T(128)} %add_convert_fusion.refs_0_, s32[1,1,64]{2,1,0:T(1,128)} %get-tuple-element.12.refs_1_, f32[96,32,64]{2,1,0:T(8,128)} %shard_map.56.refs_2_), custom_call_target="tpu_custom_call" | custom-call | tf_op jit(solution)/shard_map/pallas_call | solution.py:170
  (4 shorter events, 0.1 us)
Async XLA Ops:
  2.9 57.9 %collective-permute-start = (bf16[2,32,32,64]{3,1,2,0:T(8,128)(2,1)S(1)}, bf16[2,32,32,64]{3,1,2,0:T(8,128)(2,1)S(1)}, u32[]{:S(2)}, u32[]{:S(2)}) collective-permute-start(bf16[2,32,32,64]{3,1,2,0:T(8,128)(2,1)S(1)} %copy.10), channel_id=1, source_target_pairs={{0,0},{1,1},{2,32},{3,33},{4,64},{5,65},{6,96},{7,97},{8,128},{9,1... | collective-permute-start | bytes 786440 | tf_op jit(solution)/shard_map/ppermute | solution.py:223
  60.9 12.2 %collective-permute-start.1 = (bf16[32,32,64]{2,0,1:T(8,128)(2,1)S(1)}, bf16[32,32,64]{2,0,1:T(8,128)(2,1)S(1)}, u32[]{:S(2)}, u32[]{:S(2)}) collective-permute-start(bf16[32,32,64]{2,0,1:T(8,128)(2,1)S(1)} %select_bitcast_fusion), channel_id=1, source_target_pairs={{0,1},{1,0},{2,3},{3,2},{4,5},{5,4},{6,7},{7,6},{8,9},{9,8},{10,11... | collective-permute-start | bytes 393224 | tf_op jit(solution)/shard_map/ppermute | solution.py:226
  73.1 6.3 %copy-start = (s32[2,64]{1,0:T(2,128)S(1)}, s32[2,64]{1,0:T(2,128)}, u32[]{:S(2)}) copy-start(s32[2,64]{1,0:T(2,128)} %param.8) | copy-start | bytes 1540
  73.5 8.0 %collective-permute-start.2 = (bf16[32,2,32,64]{3,2,1,0:T(8,128)(2,1)S(1)}, bf16[32,2,32,64]{3,2,1,0:T(8,128)(2,1)S(1)}, u32[]{:S(2)}, u32[]{:S(2)}) collective-permute-start(bf16[32,2,32,64]{3,2,1,0:T(8,128)(2,1)S(1)} %get-tuple-element.7), channel_id=1, source_target_pairs={{0,32},{32,64},{64,96},{96,128},{128,160},{160,192},{192,224},{224... | collective-permute-start | bytes 786440 | tf_op jit(solution)/shard_map/ppermute | solution.py:184
  75.4 16.5 %collective-permute-start.3 = (bf16[32,2,32,64]{3,2,1,0:T(8,128)(2,1)S(1)}, bf16[32,2,32,64]{3,2,1,0:T(8,128)(2,1)S(1)}, u32[]{:S(2)}, u32[]{:S(2)}) collective-permute-start(bf16[32,2,32,64]{3,2,1,0:T(8,128)(2,1)S(1)} %get-tuple-element.8), channel_id=1, source_target_pairs={{32,0},{64,32},{96,64},{128,96},{160,128},{192,160},{224,192},{256... | collective-permute-start | bytes 786440 | tf_op jit(solution)/shard_map/ppermute | solution.py:185
  100.4 23.8 %collective-permute-start.4 = (f32[96,24,64]{0,2,1:T(8,128)S(1)}, f32[96,24,64]{0,2,1:T(8,128)S(1)}, u32[]{:S(2)}, u32[]{:S(2)}) collective-permute-start(f32[96,24,64]{0,2,1:T(8,128)S(1)} %copy.11), channel_id=1, source_target_pairs={{0,1},{1,2},{2,3},{3,4},{4,5},{5,6},{6,7},{7,8},{8,9},{9,10},{10,1... | collective-permute-start | bytes 1769480 | tf_op jit(solution)/shard_map/ppermute | solution.py:184
  104.8 22.5 %collective-permute-start.5 = (f32[96,24,64]{0,2,1:T(8,128)}, f32[96,24,64]{0,2,1:T(8,128)S(1)}, u32[]{:S(2)}, u32[]{:S(2)}) collective-permute-start(f32[96,24,64]{0,2,1:T(8,128)} %copy.12), channel_id=1, source_target_pairs={{1,0},{2,1},{3,2},{4,3},{5,4},{6,5},{7,6},{8,7},{9,8},{10,9},{11,1... | collective-permute-start | bytes 1769480 | tf_op jit(solution)/shard_map/ppermute | solution.py:185

commit v6 on v3

v6 whole, which is shorter than its diff:
```python
import functools

import jax
import jax.numpy as jnp
from jax import lax
from jax.sharding import PartitionSpec as P
from jax.experimental import pallas as pl
from jax.experimental.pallas import tpu as pltpu

LEVELS = 3
FAR_LEFT, FAR_RIGHT = 14, 15
NEAR_LEFT, NEAR_RIGHT = 4, 5
SLOT, NEAR_SLOT = 16, 8


PAD = 8


def _lift_level(work, stride, enabled, forward, width, length, ends, axis=0):
    rows = work.shape[axis] - 2 * PAD
    pairs = rows // (2 * stride)
    step = 2 * stride
    shape = list(work.shape)
    shape[axis] = pairs
    pair_ids = lax.broadcasted_iota(jnp.int32, tuple(shape), axis)
    first = (pair_ids == width // step) & (ends[0] != 0)
    last = (pair_ids == (width + length) // step - 1) & (ends[1] != 0)

    def at(start):
        window = pl.ds(start, pairs, stride=step)
        return (window,) if axis == 0 else (slice(None), window)

    evens = at(PAD)
    odds = at(PAD + stride)
    next_evens = at(PAD + step)
    prev_odds = at(PAD - stride)
    if forward:
        even_part = work[evens]
        odd_part = work[odds]
        next_even = jnp.where(last, even_part, work[next_evens])
        detail = odd_part - 0.5 * (even_part + next_even)
        work[odds] = jnp.where(enabled, detail, odd_part)
        prev_detail = jnp.where(first, detail, work[prev_odds])
        smooth = even_part + 0.25 * (prev_detail + detail)
        work[evens] = jnp.where(enabled, smooth, even_part)
    else:
        smooth = work[evens]
        detail = work[odds]
        prev_detail = jnp.where(first, detail, work[prev_odds])
        even_part = smooth - 0.25 * (prev_detail + detail)
        work[evens] = jnp.where(enabled, even_part, smooth)
        next_even = jnp.where(last, even_part, work[next_evens])
        odd_part = detail + 0.5 * (even_part + next_even)
        work[odds] = jnp.where(enabled, odd_part, detail)


def _fill(work, axis, parts, total):
    def span(lo, hi):
        return (slice(lo, hi),) if axis == 0 else (slice(None), slice(lo, hi))

    cursor = 0
    for offset, value in parts:
        if offset > cursor:
            shape = list(work.shape)
            shape[axis] = offset - cursor
            work[span(cursor, offset)] = jnp.zeros(shape, work.dtype)
        size = value.shape[axis]
        work[span(offset, offset + size)] = value
        cursor = offset + size
    if total > cursor:
        shape = list(work.shape)
        shape[axis] = total - cursor
        work[span(cursor, total)] = jnp.zeros(shape, work.dtype)


def _src_forward_kernel(
    ends_ref, depth_ref, left_ref, merged_ref, mirror_ref, right_ref, out_ref, work, *, width, out_from
):
    length = merged_ref.shape[0]
    ends = (ends_ref[0], ends_ref[1])
    depth = depth_ref[...]

    def half_sum(ref):
        return 0.5 * (ref[:, 0].astype(jnp.float32) + ref[:, 1].astype(jnp.float32))

    body = 0.5 * (merged_ref[...].astype(jnp.float32) + mirror_ref[...].astype(jnp.float32))
    parts = [
        (PAD + width - left_ref.shape[0], half_sum(left_ref)),
        (PAD + width, body),
        (PAD + width + length, half_sum(right_ref)),
    ]
    _fill(work, 0, parts, work.shape[0])
    for depth_index in range(LEVELS):
        _lift_level(work, 2**depth_index, depth > depth_index, True, width, length, ends)
    out_ref[...] = work[PAD + width - out_from : PAD + width - out_from + out_ref.shape[0]]


def _src_inverse_kernel(ends_ref, depth_ref, in_ref, out_ref, work, *, width, in_from):
    length = out_ref.shape[0]
    ends = (ends_ref[0], ends_ref[1])
    depth = depth_ref[...]
    _fill(work, 0, [(PAD + width - in_from, in_ref[...])], work.shape[0])
    for depth_index in reversed(range(LEVELS)):
        _lift_level(work, 2**depth_index, depth > depth_index, False, width, length, ends)
    out_ref[...] = work[PAD + width : PAD + width + length]


def _rcv_kernel(ends_ref, depth_ref, thr_ref, left_ref, mid_ref, right_ref, out_ref, work, *, width):
    length = mid_ref.shape[1]
    ends = (ends_ref[0], ends_ref[1])
    depth = depth_ref[...]
    parts = [
        (PAD + width - left_ref.shape[1], left_ref[...]),
        (PAD + width, mid_ref[...]),
        (PAD + width + length, right_ref[...]),
    ]
    _fill(work, 1, parts, work.shape[1])
    for depth_index in range(LEVELS):
        _lift_level(work, 2**depth_index, depth > depth_index, True, width, length, ends, axis=1)
    field = work[:, PAD : PAD + 2 * width + length]
    thr = thr_ref[...]
    work[:, PAD : PAD + 2 * width + length] = field - jnp.clip(field, -thr, thr)
    for depth_index in reversed(range(LEVELS)):
        _lift_level(work, 2**depth_index, depth > depth_index, False, width, length, ends, axis=1)
    out_ref[...] = work[:, PAD + width : PAD + width + length]


def _call(kernel, out_shape, scratch_shape, *operands):
    smem = pl.BlockSpec(memory_space=pltpu.SMEM)
    vmem = pl.BlockSpec(memory_space=pltpu.VMEM)
    return pl.pallas_call(
        kernel,
        out_shape=jax.ShapeDtypeStruct(out_shape, jnp.float32),
        in_specs=[smem] + [vmem] * (len(operands) - 1),
        out_specs=vmem,
        scratch_shapes=[pltpu.VMEM(scratch_shape, jnp.float32)],
    )(*operands)


def halos(cells, axis_name, dim, left_width, right_width):
    count = lax.axis_size(axis_name)
    length = cells.shape[dim]
    head = lax.slice_in_dim(cells, 0, right_width, axis=dim)
    tail = lax.slice_in_dim(cells, length - left_width, length, axis=dim)
    from_left = lax.ppermute(tail, axis_name, [(i, i + 1) for i in range(count - 1)])
    from_right = lax.ppermute(head, axis_name, [(i + 1, i) for i in range(count - 1)])
    return from_left, from_right


def body(observed, estimate, acquired, levels, thresholds):
    src_count = lax.axis_size("src")
    rcv_count = lax.axis_size("rcv")
    src_index = lax.axis_index("src")
    rcv_index = lax.axis_index("rcv")
    row_count, col_count, samples = observed.shape
    extent = row_count * src_count
    blocks = acquired.shape[0]
    block_size = extent // blocks
    block_ids = jnp.arange(blocks, dtype=jnp.int32)
    row_ids = src_index * row_count + jnp.arange(row_count, dtype=jnp.int32)
    col_ids = rcv_index * col_count + jnp.arange(col_count, dtype=jnp.int32)
    pick_rows = (row_ids[:, None] // block_size == block_ids[None, :]).astype(jnp.float32)
    pick_cols = (col_ids[:, None] // block_size == block_ids[None, :]).astype(jnp.float32)
    row_mask = jnp.dot(pick_rows, acquired.astype(jnp.float32), precision=lax.Precision.HIGHEST)
    local_mask = jnp.dot(row_mask, pick_cols.T, precision=lax.Precision.HIGHEST)
    est_float = estimate.astype(jnp.float32)
    merged = (
        est_float + local_mask[:, :, None] * (observed.astype(jnp.float32) - est_float)
    ).astype(jnp.bfloat16)

    ratio = rcv_count // src_count
    pieces = merged.reshape(ratio, col_count, col_count, samples)
    own_part = rcv_index % ratio
    received = []
    for shift in range(ratio):
        perm = []
        for a in range(src_count):
            for b in range(rcv_count):
                part = (b % ratio + shift) % ratio
                perm.append((a * rcv_count + b, (b // ratio) * rcv_count + a * ratio + part))
        send = lax.dynamic_index_in_dim(pieces, (own_part + shift) % ratio, axis=0, keepdims=False)
        received.append(lax.ppermute(send, ("src", "rcv"), perm))
    received = jnp.stack(received)
    slots = []
    for slot in range(ratio):
        got = lax.dynamic_index_in_dim(received, (own_part - slot) % ratio, axis=0, keepdims=False)
        slots.append(jnp.transpose(got, (1, 0, 2)))
    mirror = jnp.concatenate(slots, axis=0)
    samples_shape = (1, 1, samples)
    src_depth = levels[0].reshape(samples_shape)
    rcv_depth = levels[1].reshape(samples_shape)
    src_ends = jnp.stack([src_index == 0, src_index == src_count - 1]).astype(jnp.int32)
    rcv_ends = jnp.stack([rcv_index == 0, rcv_index == rcv_count - 1]).astype(jnp.int32)

    left_src, right_src = halos(jnp.stack([merged, mirror], axis=1), "src", 0, FAR_LEFT, FAR_RIGHT)
    coeff = _call(
        functools.partial(_src_forward_kernel, width=SLOT, out_from=NEAR_LEFT),
        (NEAR_LEFT + row_count + NEAR_RIGHT, col_count, samples),
        (row_count + 2 * SLOT + 2 * PAD, col_count, samples),
        src_ends, src_depth, left_src, merged, mirror, right_src,
    )
    left_rcv, right_rcv = halos(coeff, "rcv", 1, FAR_LEFT, FAR_RIGHT)
    coeff = _call(
        functools.partial(_rcv_kernel, width=SLOT),
        coeff.shape,
        (coeff.shape[0], col_count + 2 * SLOT + 2 * PAD, samples),
        rcv_ends, rcv_depth, thresholds.reshape(samples_shape), left_rcv, coeff, right_rcv,
    )
    return _call(
        functools.partial(_src_inverse_kernel, width=NEAR_SLOT, in_from=NEAR_LEFT),
        (row_count, col_count, samples),
        (row_count + 2 * NEAR_SLOT + 2 * PAD, col_count, samples),
        src_ends, src_depth, coeff,
    )

def solution(mesh):
    return jax.shard_map(
        body,
        mesh=mesh,
        in_specs=(P("src", "rcv", None), P("src", "rcv", None), P(), P(), P()),
        out_specs=P("src", "rcv", None),
        check_vma=False,
    )
```

time: 131 us -> 117 us (0.89)
  the two profiles are of different devices: /device:TPU:27 before, /device:TPU:31 now
where the time goes in v6:
time: 117 us
  waiting for transfers between devices  49.9 us (43%)
  starting transfers between devices  41.7 us (36%)
  Pallas kernels  14.3 us (12%)
  local copies, waits for them, and re-layouts  5.47 us (5%)
  other arithmetic  4.02 us (3%)
    ppermute x2, waiting for transfers between devices, body(): received.append(lax.ppermute(send, ('src', 'rcv'), perm))  37.5 us
    ppermute x2, starting transfers between devices, halos(): lax.ppermute(head, axis_name, [(i + 1, i) for i in range(count - 1)])  22.1 us
    ppermute x2, starting transfers between devices, body(): received.append(lax.ppermute(send, ('src', 'rcv'), perm))  15.8 us
    pallas_call x3, Pallas kernels, _call(): pl.pallas_call(kernel, out_shape=jax.ShapeDtypeStruct(out_shape, jnp.floa...  14.3 us
    ppermute x2, waiting for transfers between devices, halos(): lax.ppermute(tail, axis_name, [(i, i + 1) for i in range(count - 1)])  8.82 us
    ppermute x2, starting transfers between devices, halos(): lax.ppermute(tail, axis_name, [(i, i + 1) for i in range(count - 1)])  3.84 us
    ppermute x2, waiting for transfers between devices, halos(): lax.ppermute(head, axis_name, [(i + 1, i) for i in range(count - 1)])  3.52 us
  transfers between devices with their start and end apart: 6, of which 4 were waited for; matrix products, arithmetic and copies ran while one was open for 3% of the time, Pallas kernels for 0%

profile of v6, /device:TPU:31, one launch (start us, length us, event | category | flops | bytes accessed | tf_op | source)
XLA Modules:
  0.0 116.7 jit_solution(15655054106428963554)
XLA Ops:
  0.0 0.9 fusion.6
  0.9 0.2 fusion.8
  1.2 1.5 %fusion.1.merged_ref = bf16[64,32,64]{2,1,0:T(8,128)(2,1)S(1)} fusion(bf16[64,32,64]{2,1,0:T(8,128)(2,1)} %param.6, bf16[64,32,64]{2,1,0:T(8,128)(2,1)} %param.5, f32[64,32]{1,0:T(8,128)S(1)} %fusion.8), kind=kLoop, calls=%fused_computation.3 | loop fusion | flops 786432 | bytes 794624 | tf_op jit(solution)/shard_map/convert_element_type | solution.py:169
  2.7 0.0 copy-start
  2.8 0.1 copy.20
  2.9 13.8 %collective-permute-start = (bf16[32,32,64]{2,0,1:T(8,128)(2,1)S(1)}, bf16[32,32,64]{2,0,1:T(8,128)(2,1)S(1)}, u32[]{:S(2)}, u32[]{:S(2)}) collective-permute-start(bf16[32,32,64]{2,0,1:T(8,128)(2,1)S(1)} %bitcast.35), channel_id=1, source_target_pairs={{0,0},{1,1},{2,32},{3,33},{4,64},{5,65},{6,96},{7,97},{8,128},{9,1... | collective-permute-start | bytes 393224 | tf_op jit(solution)/shard_map/ppermute | solution.py:182
  16.7 0.1 copy.19
  16.8 1.9 %collective-permute-start.1 = (bf16[32,32,64]{2,0,1:T(8,128)(2,1)S(1)}, bf16[32,32,64]{2,0,1:T(8,128)(2,1)S(1)}, u32[]{:S(2)}, u32[]{:S(2)}) collective-permute-start(bf16[32,32,64]{2,0,1:T(8,128)(2,1)S(1)} %bitcast.36), channel_id=1, source_target_pairs={{0,1},{1,0},{2,33},{3,32},{4,65},{5,64},{6,97},{7,96},{8,129},{9,1... | collective-permute-start | bytes 393224 | tf_op jit(solution)/shard_map/ppermute | solution.py:182
  18.8 21.9 %collective-permute-done = bf16[32,32,64]{2,0,1:T(8,128)(2,1)S(1)} collective-permute-done((bf16[32,32,64]{2,0,1:T(8,128)(2,1)S(1)}, bf16[32,32,64]{2,0,1:T(8,128)(2,1)S(1)}, u32[]{:S(2)}, u32[]{:S(2)}) %collective-permute-start) | collective-permute-done | bytes 131104 | tf_op jit(solution)/shard_map/ppermute | solution.py:182
  40.7 15.6 %collective-permute-done.1 = bf16[32,32,64]{2,0,1:T(8,128)(2,1)S(1)} collective-permute-done((bf16[32,32,64]{2,0,1:T(8,128)(2,1)S(1)}, bf16[32,32,64]{2,0,1:T(8,128)(2,1)S(1)}, u32[]{:S(2)}, u32[]{:S(2)}) %collective-permute-start.1) | collective-permute-done | bytes 131104 | tf_op jit(solution)/shard_map/ppermute | solution.py:182
  56.3 0.3 fusion.5
  56.6 0.9 pad_maximum_fusion
  57.5 0.0 copy-start.4
  57.5 0.0 copy-done
  57.5 0.1 pad_maximum_fusion.1
  57.6 1.9 %collective-permute-start.2 = (bf16[14,2,32,64]{3,2,1,0:T(8,128)(2,1)S(1)}, bf16[14,2,32,64]{3,2,1,0:T(8,128)(2,1)S(1)}, u32[]{:S(2)}, u32[]{:S(2)}) collective-permute-start(bf16[14,2,32,64]{3,2,1,0:T(8,128)(2,1)S(1)} %pad_maximum_fusion.2), channel_id=1, source_target_pairs={{0,32},{32,64},{64,96},{96,128},{128,160},{160,192},{192,224},{224... | collective-permute-start | bytes 344072 | tf_op jit(solution)/shard_map/ppermute | solution.py:145
  59.5 8.9 %collective-permute-start.3 = (bf16[15,2,32,64]{3,2,1,0:T(8,128)(2,1)S(1)}, bf16[15,2,32,64]{3,2,1,0:T(8,128)(2,1)S(1)}, u32[]{:S(2)}, u32[]{:S(2)}) collective-permute-start(bf16[15,2,32,64]{3,2,1,0:T(8,128)(2,1)S(1)} %pad_maximum_fusion.1), channel_id=1, source_target_pairs={{32,0},{64,32},{96,64},{128,96},{160,128},{192,160},{224,192},{256... | collective-permute-start | bytes 368648 | tf_op jit(solution)/shard_map/ppermute | solution.py:146
  68.4 0.0 copy-done.4
  68.5 0.6 slice_bitcast_fusion
  69.0 0.6 add_convert_fusion.ends_ref
  69.6 0.0 collective-permute-done.2.left_ref
  69.6 0.0 copy-start.3
  69.6 3.5 %collective-permute-done.3.right_ref = bf16[15,2,32,64]{3,2,1,0:T(8,128)(2,1)S(1)} collective-permute-done((bf16[15,2,32,64]{3,2,1,0:T(8,128)(2,1)S(1)}, bf16[15,2,32,64]{3,2,1,0:T(8,128)(2,1)S(1)}, u32[]{:S(2)}, u32[]{:S(2)}) %collective-permute-start.3) | collective-permute-done | bytes 122912 | tf_op jit(solution)/shard_map/ppermute | solution.py:146
  73.2 0.0 copy-start.2
  73.2 0.0 copy-done.3
  73.2 0.7 copy-done.2
  73.9 3.7 %shard_map.55.mid_ref = f32[73,32,64]{2,1,0:T(8,128)} custom-call(s32[2]{0:T(128)} %add_convert_fusion.ends_ref, s32[1,1,64]{2,1,0:T(1,128)} %get-tuple-element.12.depth_ref, bf16[14,2,32,64]{3,2,1,0:T(8,128)(2,1)} %copy-done.3, bf16[64,32,64]{2,1,0:T(8,128)(2,1)} %copy-done, bf16[64,32,64]{2,1,0:T(8,128)(2,1)} %get-tuple-element.5.mirror_ref, ...), custom_call_target="tpu_custom_call" | custom-call | tf_op jit(solution)/shard_map/pallas_call | solution.py:131
  77.5 0.0 slice-start
  77.6 0.0 copy-start.1
  77.6 1.1 slice-done
  78.6 0.3 copy.13
  78.9 13.2 %collective-permute-start.5 = (f32[73,15,64]{0,2,1:T(8,128)S(1)}, f32[73,15,64]{0,2,1:T(8,128)S(1)}, u32[]{:S(2)}, u32[]{:S(2)}) collective-permute-start(f32[73,15,64]{0,2,1:T(8,128)S(1)} %copy.13), channel_id=1, source_target_pairs={{1,0},{2,1},{3,2},{4,3},{5,4},{6,5},{7,6},{8,7},{9,8},{10,9},{11,1... | collective-permute-start | bytes 840968 | tf_op jit(solution)/shard_map/ppermute | solution.py:146
  92.1 0.0 copy-done.1
  92.1 0.1 slice.24
  92.1 0.3 copy.12
  92.4 1.9 %collective-permute-start.4 = (f32[73,14,64]{0,2,1:T(8,128)S(1)}, f32[73,14,64]{0,2,1:T(8,128)S(1)}, u32[]{:S(2)}, u32[]{:S(2)}) collective-permute-start(f32[73,14,64]{0,2,1:T(8,128)S(1)} %copy.12), channel_id=1, source_target_pairs={{0,1},{1,2},{2,3},{3,4},{4,5},{5,6},{6,7},{7,8},{8,9},{9,10},{10,1... | collective-permute-start | bytes 784904 | tf_op jit(solution)/shard_map/ppermute | solution.py:145
  94.4 0.6 add_convert_fusion.1.ends_ref
  94.9 8.8 %collective-permute-done.4 = f32[73,14,64]{0,2,1:T(8,128)S(1)} collective-permute-done((f32[73,14,64]{0,2,1:T(8,128)S(1)}, f32[73,14,64]{0,2,1:T(8,128)S(1)}, u32[]{:S(2)}, u32[]{:S(2)}) %collective-permute-start.4) | collective-permute-done | bytes 261664 | tf_op jit(solution)/shard_map/ppermute | solution.py:145
  103.8 1.1 copy.14.left_ref
  104.9 0.0 collective-permute-done.5
  104.9 1.1 copy.15.right_ref
  106.0 7.7 %shard_map.56.in_ref = f32[73,32,64]{2,1,0:T(8,128)} custom-call(s32[2]{0:T(128)} %add_convert_fusion.1.ends_ref, s32[1,1,64]{2,1,0:T(1,128)} %get-tuple-element.11.depth_ref, f32[1,1,64]{2,1,0:T(1,128)} %bitcast.37, f32[73,14,64]{2,1,0:T(8,128)} %copy.14.left_ref, f32[73,32,64]{2,1,0:T(8,128)} %shard_map.55.mid_ref, f32[73,15,64]{2,1,0:T(8,128)} %copy.15.right_ref), custom_call_target="tpu_custom_call" | custom-call | tf_op jit(solution)/shard_map/pallas_call | solution.py:131
  113.7 3.0 %shard_map.57 = f32[64,32,64]{2,1,0:T(8,128)} custom-call(s32[2]{0:T(128)} %add_convert_fusion.ends_ref, s32[1,1,64]{2,1,0:T(1,128)} %get-tuple-element.12.depth_ref, f32[73,32,64]{2,1,0:T(8,128)} %shard_map.56.in_ref), custom_call_target="tpu_custom_call" | custom-call | tf_op jit(solution)/shard_map/pallas_call | solution.py:131
  (4 shorter events, 0.1 us)
Async XLA Ops:
  2.7 54.8 %copy-start = (bf16[64,32,64]{2,1,0:T(8,128)(2,1)}, bf16[64,32,64]{2,1,0:T(8,128)(2,1)S(1)}, u32[]{:S(2)}) copy-start(bf16[64,32,64]{2,1,0:T(8,128)(2,1)S(1)} %fusion.1.merged_ref) | copy-start | bytes 786436
  2.9 37.8 %collective-permute-start = (bf16[32,32,64]{2,0,1:T(8,128)(2,1)S(1)}, bf16[32,32,64]{2,0,1:T(8,128)(2,1)S(1)}, u32[]{:S(2)}, u32[]{:S(2)}) collective-permute-start(bf16[32,32,64]{2,0,1:T(8,128)(2,1)S(1)} %bitcast.35), channel_id=1, source_target_pairs={{0,0},{1,1},{2,32},{3,33},{4,64},{5,65},{6,96},{7,97},{8,128},{9,1... | collective-permute-start | bytes 393224 | tf_op jit(solution)/shard_map/ppermute | solution.py:182
  16.8 39.5 %collective-permute-start.1 = (bf16[32,32,64]{2,0,1:T(8,128)(2,1)S(1)}, bf16[32,32,64]{2,0,1:T(8,128)(2,1)S(1)}, u32[]{:S(2)}, u32[]{:S(2)}) collective-permute-start(bf16[32,32,64]{2,0,1:T(8,128)(2,1)S(1)} %bitcast.36), channel_id=1, source_target_pairs={{0,1},{1,0},{2,33},{3,32},{4,65},{5,64},{6,97},{7,96},{8,129},{9,1... | collective-permute-start | bytes 393224 | tf_op jit(solution)/shard_map/ppermute | solution.py:182
  57.5 11.0 %copy-start.4 = (s32[2,64]{1,0:T(2,128)S(1)}, s32[2,64]{1,0:T(2,128)}, u32[]{:S(2)}) copy-start(s32[2,64]{1,0:T(2,128)} %param.8) | copy-start | bytes 1540
  57.6 12.0 %collective-permute-start.2 = (bf16[14,2,32,64]{3,2,1,0:T(8,128)(2,1)S(1)}, bf16[14,2,32,64]{3,2,1,0:T(8,128)(2,1)S(1)}, u32[]{:S(2)}, u32[]{:S(2)}) collective-permute-start(bf16[14,2,32,64]{3,2,1,0:T(8,128)(2,1)S(1)} %pad_maximum_fusion.2), channel_id=1, source_target_pairs={{0,32},{32,64},{64,96},{96,128},{128,160},{160,192},{192,224},{224... | collective-permute-start | bytes 344072 | tf_op jit(solution)/shard_map/ppermute | solution.py:145
  59.5 13.6 %collective-permute-start.3 = (bf16[15,2,32,64]{3,2,1,0:T(8,128)(2,1)S(1)}, bf16[15,2,32,64]{3,2,1,0:T(8,128)(2,1)S(1)}, u32[]{:S(2)}, u32[]{:S(2)}) collective-permute-start(bf16[15,2,32,64]{3,2,1,0:T(8,128)(2,1)S(1)} %pad_maximum_fusion.1), channel_id=1, source_target_pairs={{32,0},{64,32},{96,64},{128,96},{160,128},{192,160},{224,192},{256... | collective-permute-start | bytes 368648 | tf_op jit(solution)/shard_map/ppermute | solution.py:146
  69.6 3.5 %copy-start.3 = (bf16[14,2,32,64]{3,2,1,0:T(8,128)(2,1)}, bf16[14,2,32,64]{3,2,1,0:T(8,128)(2,1)S(1)}, u32[]{:S(2)}) copy-start(bf16[14,2,32,64]{3,2,1,0:T(8,128)(2,1)S(1)} %collective-permute-done.2.left_ref) | copy-start | bytes 344068
  73.2 0.7 copy-start.2
  77.5 1.1 slice-start
  77.6 14.5 %copy-start.1 = (f32[73,32,64]{2,1,0:T(8,128)S(1)}, f32[73,32,64]{2,1,0:T(8,128)}, u32[]{:S(2)}) copy-start(f32[73,32,64]{2,1,0:T(8,128)} %shard_map.55.mid_ref) | copy-start | bytes 1794052
  78.9 26.0 %collective-permute-start.5 = (f32[73,15,64]{0,2,1:T(8,128)S(1)}, f32[73,15,64]{0,2,1:T(8,128)S(1)}, u32[]{:S(2)}, u32[]{:S(2)}) collective-permute-start(f32[73,15,64]{0,2,1:T(8,128)S(1)} %copy.13), channel_id=1, source_target_pairs={{1,0},{2,1},{3,2},{4,3},{5,4},{6,5},{7,6},{8,7},{9,8},{10,9},{11,1... | collective-permute-start | bytes 840968 | tf_op jit(solution)/shard_map/ppermute | solution.py:146
  92.4 11.3 %collective-permute-start.4 = (f32[73,14,64]{0,2,1:T(8,128)S(1)}, f32[73,14,64]{0,2,1:T(8,128)S(1)}, u32[]{:S(2)}, u32[]{:S(2)}) collective-permute-start(f32[73,14,64]{0,2,1:T(8,128)S(1)} %copy.12), channel_id=1, source_target_pairs={{0,1},{1,2},{2,3},{3,4},{4,5},{5,6},{6,7},{7,8},{8,9},{9,10},{10,1... | collective-permute-start | bytes 784904 | tf_op jit(solution)/shard_map/ppermute | solution.py:145

commit v7 on v6

--- a/solution.py
+++ b/solution.py
@@ -95,20 +95,13 @@
     out_ref[...] = work[PAD + width - out_from : PAD + width - out_from + out_ref.shape[0]]
 
 
-def _src_inverse_kernel(ends_ref, depth_ref, in_ref, out_ref, work, *, width, in_from):
-    length = out_ref.shape[0]
-    ends = (ends_ref[0], ends_ref[1])
-    depth = depth_ref[...]
-    _fill(work, 0, [(PAD + width - in_from, in_ref[...])], work.shape[0])
-    for depth_index in reversed(range(LEVELS)):
-        _lift_level(work, 2**depth_index, depth > depth_index, False, width, length, ends)
-    out_ref[...] = work[PAD + width : PAD + width + length]
-
-
-def _rcv_kernel(ends_ref, depth_ref, thr_ref, left_ref, mid_ref, right_ref, out_ref, work, *, width):
+def _rcv_kernel(
+    rcv_ends_ref, src_ends_ref, rcv_depth_ref, src_depth_ref, thr_ref, left_ref, mid_ref, right_ref,
+    out_ref, work, rows_work, *, width, src_width, in_from,
+):
     length = mid_ref.shape[1]
-    ends = (ends_ref[0], ends_ref[1])
-    depth = depth_ref[...]
+    ends = (rcv_ends_ref[0], rcv_ends_ref[1])
+    depth = rcv_depth_ref[...]
     parts = [
         (PAD + width - left_ref.shape[1], left_ref[...]),
         (PAD + width, mid_ref[...]),
@@ -122,18 +115,26 @@
     work[:, PAD : PAD + 2 * width + length] = field - jnp.clip(field, -thr, thr)
     for depth_index in reversed(range(LEVELS)):
         _lift_level(work, 2**depth_index, depth > depth_index, False, width, length, ends, axis=1)
-    out_ref[...] = work[:, PAD + width : PAD + width + length]
-
-
-def _call(kernel, out_shape, scratch_shape, *operands):
+
+    row_count = out_ref.shape[0]
+    ends = (src_ends_ref[0], src_ends_ref[1])
+    depth = src_depth_ref[...]
+    block = work[:, PAD + width : PAD + width + length]
+    _fill(rows_work, 0, [(PAD + src_width - in_from, block)], rows_work.shape[0])
+    for depth_index in reversed(range(LEVELS)):
+        _lift_level(rows_work, 2**depth_index, depth > depth_index, False, src_width, row_count, ends)
+    out_ref[...] = rows_work[PAD + src_width : PAD + src_width + row_count]
+
+
+def _call(kernel, out_shape, scratch_shapes, smem_count, *operands):
     smem = pl.BlockSpec(memory_space=pltpu.SMEM)
     vmem = pl.BlockSpec(memory_space=pltpu.VMEM)
     return pl.pallas_call(
         kernel,
         out_shape=jax.ShapeDtypeStruct(out_shape, jnp.float32),
-        in_specs=[smem] + [vmem] * (len(operands) - 1),
+        in_specs=[smem] * smem_count + [vmem] * (len(operands) - smem_count),
         out_specs=vmem,
-        scratch_shapes=[pltpu.VMEM(scratch_shape, jnp.float32)],
+        scratch_shapes=[pltpu.VMEM(shape, jnp.float32) for shape in scratch_shapes],
     )(*operands)
 
 
@@ -196,21 +197,21 @@
     coeff = _call(
         functools.partial(_src_forward_kernel, width=SLOT, out_from=NEAR_LEFT),
         (NEAR_LEFT + row_count + NEAR_RIGHT, col_count, samples),
-        (row_count + 2 * SLOT + 2 * PAD, col_count, samples),
+        [(row_count + 2 * SLOT + 2 * PAD, col_count, samples)],
+        1,
         src_ends, src_depth, left_src, merged, mirror, right_src,
     )
     left_rcv, right_rcv = halos(coeff, "rcv", 1, FAR_LEFT, FAR_RIGHT)
-    coeff = _call(
-        functools.partial(_rcv_kernel, width=SLOT),
-        coeff.shape,
-        (coeff.shape[0], col_count + 2 * SLOT + 2 * PAD, samples),
-        rcv_ends, rcv_depth, thresholds.reshape(samples_shape), left_rcv, coeff, right_rcv,
-    )
     return _call(
-        functools.partial(_src_inverse_kernel, width=NEAR_SLOT, in_from=NEAR_LEFT),
+        functools.partial(_rcv_kernel, width=SLOT, src_width=NEAR_SLOT, in_from=NEAR_LEFT),
         (row_count, col_count, samples),
-        (row_count + 2 * NEAR_SLOT + 2 * PAD, col_count, samples),
-        src_ends, src_depth, coeff,
+        [
+            (coeff.shape[0], col_count + 2 * SLOT + 2 * PAD, samples),
+            (row_count + 2 * NEAR_SLOT + 2 * PAD, col_count, samples),
+        ],
+        2,
+        rcv_ends, src_ends, rcv_depth, src_depth, thresholds.reshape(samples_shape),
+        left_rcv, coeff, right_rcv,
     )
 
 def solution(mesh):

time: 117 us -> 115 us (0.983)
  Pallas kernels: 14.3 us -> 11.9 us
    pallas_call x3 -> x2, Pallas kernels: 14.3 us -> 11.9 us  [_call(): pl.pallas_call(kernel, out_shape=jax.ShapeDtypeStruct(out_shape, jnp.floa...]
where the time goes in v7:
time: 115 us; the launch traced here: 114 us
  waiting for transfers between devices  49.8 us (43%)
  starting transfers between devices  41.6 us (36%)
  Pallas kernels  11.9 us (10%)
  local copies, waits for them, and re-layouts  5.51 us (5%)
  other arithmetic  4.14 us (4%)
    ppermute x2, waiting for transfers between devices, body(): received.append(lax.ppermute(send, ('src', 'rcv'), perm))  37.5 us
    ppermute x2, starting transfers between devices, halos(): lax.ppermute(head, axis_name, [(i + 1, i) for i in range(count - 1)])  22 us
    ppermute x2, starting transfers between devices, body(): received.append(lax.ppermute(send, ('src', 'rcv'), perm))  15.8 us
    pallas_call x2, Pallas kernels, _call(): pl.pallas_call(kernel, out_shape=jax.ShapeDtypeStruct(out_shape, jnp.floa...  11.9 us
    ppermute x2, waiting for transfers between devices, halos(): lax.ppermute(tail, axis_name, [(i, i + 1) for i in range(count - 1)])  8.74 us
    ppermute x2, starting transfers between devices, halos(): lax.ppermute(tail, axis_name, [(i, i + 1) for i in range(count - 1)])  3.84 us
    ppermute x2, waiting for transfers between devices, halos(): lax.ppermute(head, axis_name, [(i + 1, i) for i in range(count - 1)])  3.48 us
  transfers between devices with their start and end apart: 6, of which 4 were waited for; matrix products, arithmetic and copies ran while one was open for 3% of the time, Pallas kernels for 0%

profile of v7, /device:TPU:31, one launch (start us, length us, event | category | flops | bytes accessed | tf_op | source)
XLA Modules:
  0.0 114.3 jit_solution(9726551617512735935)
XLA Ops:
  0.0 0.9 fusion.6
  0.9 0.2 fusion.8
  1.2 1.5 %fusion.1.merged_ref = bf16[64,32,64]{2,1,0:T(8,128)(2,1)S(1)} fusion(bf16[64,32,64]{2,1,0:T(8,128)(2,1)} %param.6, bf16[64,32,64]{2,1,0:T(8,128)(2,1)} %param.5, f32[64,32]{1,0:T(8,128)S(1)} %fusion.8), kind=kLoop, calls=%fused_computation.3 | loop fusion | flops 786432 | bytes 794624 | tf_op jit(solution)/shard_map/convert_element_type | solution.py:170
  2.7 0.0 copy-start
  2.8 0.1 copy.20
  2.9 13.8 %collective-permute-start = (bf16[32,32,64]{2,0,1:T(8,128)(2,1)S(1)}, bf16[32,32,64]{2,0,1:T(8,128)(2,1)S(1)}, u32[]{:S(2)}, u32[]{:S(2)}) collective-permute-start(bf16[32,32,64]{2,0,1:T(8,128)(2,1)S(1)} %bitcast.35), channel_id=1, source_target_pairs={{0,0},{1,1},{2,32},{3,33},{4,64},{5,65},{6,96},{7,97},{8,128},{9,1... | collective-permute-start | bytes 393224 | tf_op jit(solution)/shard_map/ppermute | solution.py:183
  16.7 0.1 copy.19
  16.8 1.9 %collective-permute-start.1 = (bf16[32,32,64]{2,0,1:T(8,128)(2,1)S(1)}, bf16[32,32,64]{2,0,1:T(8,128)(2,1)S(1)}, u32[]{:S(2)}, u32[]{:S(2)}) collective-permute-start(bf16[32,32,64]{2,0,1:T(8,128)(2,1)S(1)} %bitcast.36), channel_id=1, source_target_pairs={{0,1},{1,0},{2,33},{3,32},{4,65},{5,64},{6,97},{7,96},{8,129},{9,1... | collective-permute-start | bytes 393224 | tf_op jit(solution)/shard_map/ppermute | solution.py:183
  18.8 21.9 %collective-permute-done = bf16[32,32,64]{2,0,1:T(8,128)(2,1)S(1)} collective-permute-done((bf16[32,32,64]{2,0,1:T(8,128)(2,1)S(1)}, bf16[32,32,64]{2,0,1:T(8,128)(2,1)S(1)}, u32[]{:S(2)}, u32[]{:S(2)}) %collective-permute-start) | collective-permute-done | bytes 131104 | tf_op jit(solution)/shard_map/ppermute | solution.py:183
  40.7 15.6 %collective-permute-done.1 = bf16[32,32,64]{2,0,1:T(8,128)(2,1)S(1)} collective-permute-done((bf16[32,32,64]{2,0,1:T(8,128)(2,1)S(1)}, bf16[32,32,64]{2,0,1:T(8,128)(2,1)S(1)}, u32[]{:S(2)}, u32[]{:S(2)}) %collective-permute-start.1) | collective-permute-done | bytes 131104 | tf_op jit(solution)/shard_map/ppermute | solution.py:183
  56.3 0.3 fusion.5
  56.6 0.9 pad_maximum_fusion
  57.5 0.0 copy-start.4
  57.5 0.0 copy-done
  57.6 0.1 pad_maximum_fusion.1
  57.6 1.9 %collective-permute-start.2 = (bf16[14,2,32,64]{3,2,1,0:T(8,128)(2,1)S(1)}, bf16[14,2,32,64]{3,2,1,0:T(8,128)(2,1)S(1)}, u32[]{:S(2)}, u32[]{:S(2)}) collective-permute-start(bf16[14,2,32,64]{3,2,1,0:T(8,128)(2,1)S(1)} %pad_maximum_fusion.2), channel_id=1, source_target_pairs={{0,32},{32,64},{64,96},{96,128},{128,160},{160,192},{192,224},{224... | collective-permute-start | bytes 344072 | tf_op jit(solution)/shard_map/ppermute | solution.py:146
  59.5 8.9 %collective-permute-start.3 = (bf16[15,2,32,64]{3,2,1,0:T(8,128)(2,1)S(1)}, bf16[15,2,32,64]{3,2,1,0:T(8,128)(2,1)S(1)}, u32[]{:S(2)}, u32[]{:S(2)}) collective-permute-start(bf16[15,2,32,64]{3,2,1,0:T(8,128)(2,1)S(1)} %pad_maximum_fusion.1), channel_id=1, source_target_pairs={{32,0},{64,32},{96,64},{128,96},{160,128},{192,160},{224,192},{256... | collective-permute-start | bytes 368648 | tf_op jit(solution)/shard_map/ppermute | solution.py:147
  68.4 0.0 copy-done.4
  68.4 0.6 slice_bitcast_fusion
  69.0 0.6 add_convert_fusion.1.ends_ref.src_ends_ref
  69.7 0.0 collective-permute-done.2.left_ref
  69.7 0.0 copy-start.3
  69.7 3.5 %collective-permute-done.3.right_ref = bf16[15,2,32,64]{3,2,1,0:T(8,128)(2,1)S(1)} collective-permute-done((bf16[15,2,32,64]{3,2,1,0:T(8,128)(2,1)S(1)}, bf16[15,2,32,64]{3,2,1,0:T(8,128)(2,1)S(1)}, u32[]{:S(2)}, u32[]{:S(2)}) %collective-permute-start.3) | collective-permute-done | bytes 122912 | tf_op jit(solution)/shard_map/ppermute | solution.py:147
  73.2 0.0 copy-start.2
  73.2 0.0 copy-done.3
  73.2 0.7 copy-done.2
  73.9 3.7 %shard_map.55.mid_ref = f32[73,32,64]{2,1,0:T(8,128)} custom-call(s32[2]{0:T(128)} %add_convert_fusion.1.ends_ref.src_ends_ref, s32[1,1,64]{2,1,0:T(1,128)} %get-tuple-element.11.depth_ref.src_depth_ref, bf16[14,2,32,64]{3,2,1,0:T(8,128)(2,1)} %copy-done.3, bf16[64,32,64]{2,1,0:T(8,128)(2,1)} %copy-done, bf16[64,32,64]{2,1,0:T(8,128)(2,1)} %get-tuple-element.5.mirror_ref, ...), custom_call_target="tpu_custom_call" | custom-call | tf_op jit(solution)/shard_map/pallas_call | solution.py:132
  77.6 0.0 slice-start
  77.6 0.0 copy-start.1
  77.6 1.1 slice-done
  78.6 0.3 copy.13
  78.9 13.1 %collective-permute-start.5 = (f32[73,15,64]{0,2,1:T(8,128)S(1)}, f32[73,15,64]{0,2,1:T(8,128)S(1)}, u32[]{:S(2)}, u32[]{:S(2)}) collective-permute-start(f32[73,15,64]{0,2,1:T(8,128)S(1)} %copy.13), channel_id=1, source_target_pairs={{1,0},{2,1},{3,2},{4,3},{5,4},{6,5},{7,6},{8,7},{9,8},{10,9},{11,1... | collective-permute-start | bytes 840968 | tf_op jit(solution)/shard_map/ppermute | solution.py:147
  92.1 0.0 copy-done.1
  92.1 0.1 slice.24
  92.1 0.3 copy.12
  92.4 1.9 %collective-permute-start.4 = (f32[73,14,64]{0,2,1:T(8,128)S(1)}, f32[73,14,64]{0,2,1:T(8,128)S(1)}, u32[]{:S(2)}, u32[]{:S(2)}) collective-permute-start(f32[73,14,64]{0,2,1:T(8,128)S(1)} %copy.12), channel_id=1, source_target_pairs={{0,1},{1,2},{2,3},{3,4},{4,5},{5,6},{6,7},{7,8},{8,9},{9,10},{10,1... | collective-permute-start | bytes 784904 | tf_op jit(solution)/shard_map/ppermute | solution.py:146
  94.4 0.7 add_convert_fusion.rcv_ends_ref
  95.0 8.7 %collective-permute-done.4 = f32[73,14,64]{0,2,1:T(8,128)S(1)} collective-permute-done((f32[73,14,64]{0,2,1:T(8,128)S(1)}, f32[73,14,64]{0,2,1:T(8,128)S(1)}, u32[]{:S(2)}, u32[]{:S(2)}) %collective-permute-start.4) | collective-permute-done | bytes 261664 | tf_op jit(solution)/shard_map/ppermute | solution.py:146
  103.7 1.1 copy.14.left_ref
  104.9 0.0 collective-permute-done.5
  104.9 1.1 copy.15.right_ref
  106.0 8.3 %shard_map.56 = f32[64,32,64]{2,1,0:T(8,128)} custom-call(s32[2]{0:T(128)} %add_convert_fusion.rcv_ends_ref, s32[2]{0:T(128)} %add_convert_fusion.1.ends_ref.src_ends_ref, s32[1,1,64]{2,1,0:T(1,128)} %get-tuple-element.12.rcv_depth_ref, s32[1,1,64]{2,1,0:T(1,128)} %get-tuple-element.11.depth_ref.src_depth_ref, f32[1,1,64]{2,1,0:T(1,128)} %bitcast.37, ...), custom_call_target="tpu_custom_call" | custom-call | tf_op jit(solution)/shard_map/pallas_call | solution.py:132
  (4 shorter events, 0.1 us)
Async XLA Ops:
  2.7 54.8 %copy-start = (bf16[64,32,64]{2,1,0:T(8,128)(2,1)}, bf16[64,32,64]{2,1,0:T(8,128)(2,1)S(1)}, u32[]{:S(2)}) copy-start(bf16[64,32,64]{2,1,0:T(8,128)(2,1)S(1)} %fusion.1.merged_ref) | copy-start | bytes 786436
  2.9 37.8 %collective-permute-start = (bf16[32,32,64]{2,0,1:T(8,128)(2,1)S(1)}, bf16[32,32,64]{2,0,1:T(8,128)(2,1)S(1)}, u32[]{:S(2)}, u32[]{:S(2)}) collective-permute-start(bf16[32,32,64]{2,0,1:T(8,128)(2,1)S(1)} %bitcast.35), channel_id=1, source_target_pairs={{0,0},{1,1},{2,32},{3,33},{4,64},{5,65},{6,96},{7,97},{8,128},{9,1... | collective-permute-start | bytes 393224 | tf_op jit(solution)/shard_map/ppermute | solution.py:183
  16.8 39.5 %collective-permute-start.1 = (bf16[32,32,64]{2,0,1:T(8,128)(2,1)S(1)}, bf16[32,32,64]{2,0,1:T(8,128)(2,1)S(1)}, u32[]{:S(2)}, u32[]{:S(2)}) collective-permute-start(bf16[32,32,64]{2,0,1:T(8,128)(2,1)S(1)} %bitcast.36), channel_id=1, source_target_pairs={{0,1},{1,0},{2,33},{3,32},{4,65},{5,64},{6,97},{7,96},{8,129},{9,1... | collective-permute-start | bytes 393224 | tf_op jit(solution)/shard_map/ppermute | solution.py:183
  57.5 10.9 %copy-start.4 = (s32[2,64]{1,0:T(2,128)S(1)}, s32[2,64]{1,0:T(2,128)}, u32[]{:S(2)}) copy-start(s32[2,64]{1,0:T(2,128)} %param.8) | copy-start | bytes 1540
  57.6 12.1 %collective-permute-start.2 = (bf16[14,2,32,64]{3,2,1,0:T(8,128)(2,1)S(1)}, bf16[14,2,32,64]{3,2,1,0:T(8,128)(2,1)S(1)}, u32[]{:S(2)}, u32[]{:S(2)}) collective-permute-start(bf16[14,2,32,64]{3,2,1,0:T(8,128)(2,1)S(1)} %pad_maximum_fusion.2), channel_id=1, source_target_pairs={{0,32},{32,64},{64,96},{96,128},{128,160},{160,192},{192,224},{224... | collective-permute-start | bytes 344072 | tf_op jit(solution)/shard_map/ppermute | solution.py:146
  59.5 13.6 %collective-permute-start.3 = (bf16[15,2,32,64]{3,2,1,0:T(8,128)(2,1)S(1)}, bf16[15,2,32,64]{3,2,1,0:T(8,128)(2,1)S(1)}, u32[]{:S(2)}, u32[]{:S(2)}) collective-permute-start(bf16[15,2,32,64]{3,2,1,0:T(8,128)(2,1)S(1)} %pad_maximum_fusion.1), channel_id=1, source_target_pairs={{32,0},{64,32},{96,64},{128,96},{160,128},{192,160},{224,192},{256... | collective-permute-start | bytes 368648 | tf_op jit(solution)/shard_map/ppermute | solution.py:147
  69.7 3.5 %copy-start.3 = (bf16[14,2,32,64]{3,2,1,0:T(8,128)(2,1)}, bf16[14,2,32,64]{3,2,1,0:T(8,128)(2,1)S(1)}, u32[]{:S(2)}) copy-start(bf16[14,2,32,64]{3,2,1,0:T(8,128)(2,1)S(1)} %collective-permute-done.2.left_ref) | copy-start | bytes 344068
  73.2 0.7 copy-start.2
  77.6 1.1 slice-start
  77.6 14.5 %copy-start.1 = (f32[73,32,64]{2,1,0:T(8,128)S(1)}, f32[73,32,64]{2,1,0:T(8,128)}, u32[]{:S(2)}) copy-start(f32[73,32,64]{2,1,0:T(8,128)} %shard_map.55.mid_ref) | copy-start | bytes 1794052
  78.9 26.0 %collective-permute-start.5 = (f32[73,15,64]{0,2,1:T(8,128)S(1)}, f32[73,15,64]{0,2,1:T(8,128)S(1)}, u32[]{:S(2)}, u32[]{:S(2)}) collective-permute-start(f32[73,15,64]{0,2,1:T(8,128)S(1)} %copy.13), channel_id=1, source_target_pairs={{1,0},{2,1},{3,2},{4,3},{5,4},{6,5},{7,6},{8,7},{9,8},{10,9},{11,1... | collective-permute-start | bytes 840968 | tf_op jit(solution)/shard_map/ppermute | solution.py:147
  92.4 11.3 %collective-permute-start.4 = (f32[73,14,64]{0,2,1:T(8,128)S(1)}, f32[73,14,64]{0,2,1:T(8,128)S(1)}, u32[]{:S(2)}, u32[]{:S(2)}) collective-permute-start(f32[73,14,64]{0,2,1:T(8,128)S(1)} %copy.12), channel_id=1, source_target_pairs={{0,1},{1,2},{2,3},{3,4},{4,5},{5,6},{6,7},{7,8},{8,9},{9,10},{10,1... | collective-permute-start | bytes 784904 | tf_op jit(solution)/shard_map/ppermute | solution.py:146

commit v8 on v7

--- a/solution.py
+++ b/solution.py
@@ -157,16 +157,21 @@
     extent = row_count * src_count
     blocks = acquired.shape[0]
     block_size = extent // blocks
-    block_ids = jnp.arange(blocks, dtype=jnp.int32)
-    row_ids = src_index * row_count + jnp.arange(row_count, dtype=jnp.int32)
-    col_ids = rcv_index * col_count + jnp.arange(col_count, dtype=jnp.int32)
-    pick_rows = (row_ids[:, None] // block_size == block_ids[None, :]).astype(jnp.float32)
-    pick_cols = (col_ids[:, None] // block_size == block_ids[None, :]).astype(jnp.float32)
-    row_mask = jnp.dot(pick_rows, acquired.astype(jnp.float32), precision=lax.Precision.HIGHEST)
-    local_mask = jnp.dot(row_mask, pick_cols.T, precision=lax.Precision.HIGHEST)
+    if block_size % row_count == 0 and block_size % col_count == 0:
+        local_mask = acquired[
+            src_index * row_count // block_size, rcv_index * col_count // block_size
+        ].astype(jnp.float32)
+    else:
+        block_ids = jnp.arange(blocks, dtype=jnp.int32)
+        row_ids = src_index * row_count + jnp.arange(row_count, dtype=jnp.int32)
+        col_ids = rcv_index * col_count + jnp.arange(col_count, dtype=jnp.int32)
+        pick_rows = (row_ids[:, None] // block_size == block_ids[None, :]).astype(jnp.float32)
+        pick_cols = (col_ids[:, None] // block_size == block_ids[None, :]).astype(jnp.float32)
+        row_mask = jnp.dot(pick_rows, acquired.astype(jnp.float32), precision=lax.Precision.HIGHEST)
+        local_mask = jnp.dot(row_mask, pick_cols.T, precision=lax.Precision.HIGHEST)[:, :, None]
     est_float = estimate.astype(jnp.float32)
     merged = (
-        est_float + local_mask[:, :, None] * (observed.astype(jnp.float32) - est_float)
+        est_float + local_mask * (observed.astype(jnp.float32) - est_float)
     ).astype(jnp.bfloat16)
 
     ratio = rcv_count // src_count

time: 115 us -> 115 us (level)
  local copies, waits for them, and re-layouts: 5.51 us -> 6.78 us
    dynamic_slice x0 -> x1, local copies, waits for them, and re-layouts: none -> 1.27 us  [body(): acquired[src_index * row_count // block_size, rcv_index * col_count // bl...]
where the time goes in v8:
time: 115 us
  waiting for transfers between devices  49.7 us (43%)
  starting transfers between devices  41.6 us (36%)
  Pallas kernels  11.9 us (10%)
  local copies, waits for them, and re-layouts  6.78 us (6%)
  other arithmetic  3.99 us (3%)
    ppermute x2, waiting for transfers between devices, body(): received.append(lax.ppermute(send, ('src', 'rcv'), perm))  37.5 us
    ppermute x2, starting transfers between devices, halos(): lax.ppermute(head, axis_name, [(i + 1, i) for i in range(count - 1)])  22 us
    ppermute x2, starting transfers between devices, body(): received.append(lax.ppermute(send, ('src', 'rcv'), perm))  15.8 us
    pallas_call x2, Pallas kernels, _call(): pl.pallas_call(kernel, out_shape=jax.ShapeDtypeStruct(out_shape, jnp.floa...  11.9 us
    ppermute x2, waiting for transfers between devices, halos(): lax.ppermute(tail, axis_name, [(i, i + 1) for i in range(count - 1)])  8.74 us
    ppermute x2, starting transfers between devices, halos(): lax.ppermute(tail, axis_name, [(i, i + 1) for i in range(count - 1)])  3.84 us
    ppermute x2, waiting for transfers between devices, halos(): lax.ppermute(head, axis_name, [(i + 1, i) for i in range(count - 1)])  3.46 us
  transfers between devices with their start and end apart: 6, of which 4 were waited for; matrix products, arithmetic and copies ran while one was open for 3% of the time, Pallas kernels for 0%

profile of v8, /device:TPU:31, one launch (start us, length us, event | category | flops | bytes accessed | tf_op | source)
XLA Modules:
  0.0 114.9 jit_solution(4881813562301559070)
XLA Ops:
  0.0 1.3 %dynamic_slice.16 = s32[1,1]{1,0:T(1,128)} dynamic-slice(s32[8,8]{1,0:T(8,128)} %param.7, s32[]{:T(128)S(6)} %select_n.46, s32[]{:T(128)S(6)} %select_n.48), dynamic_slice_sizes={1,1} | dynamic-slice | bytes 12 | tf_op jit(solution)/shard_map/dynamic_slice | solution.py:161
  1.9 1.4 %fusion.1.merged_ref = bf16[64,32,64]{2,1,0:T(8,128)(2,1)S(1)} fusion(bf16[64,32,64]{2,1,0:T(8,128)(2,1)} %param.6, bf16[64,32,64]{2,1,0:T(8,128)(2,1)} %param.5, f32[]{:T(128)} %bitcast.7), kind=kLoop, calls=%fused_computation.3 | loop fusion | flops 786432 | bytes 786436 | tf_op jit(solution)/shard_map/convert_element_type | solution.py:175
  3.3 0.0 copy-start
  3.4 0.1 copy.17
  3.5 13.8 %collective-permute-start = (bf16[32,32,64]{2,0,1:T(8,128)(2,1)S(1)}, bf16[32,32,64]{2,0,1:T(8,128)(2,1)S(1)}, u32[]{:S(2)}, u32[]{:S(2)}) collective-permute-start(bf16[32,32,64]{2,0,1:T(8,128)(2,1)S(1)} %bitcast.35), channel_id=1, source_target_pairs={{0,0},{1,1},{2,32},{3,33},{4,64},{5,65},{6,96},{7,97},{8,128},{9,1... | collective-permute-start | bytes 393224 | tf_op jit(solution)/shard_map/ppermute | solution.py:188
  17.3 0.1 copy.16
  17.5 1.9 %collective-permute-start.1 = (bf16[32,32,64]{2,0,1:T(8,128)(2,1)S(1)}, bf16[32,32,64]{2,0,1:T(8,128)(2,1)S(1)}, u32[]{:S(2)}, u32[]{:S(2)}) collective-permute-start(bf16[32,32,64]{2,0,1:T(8,128)(2,1)S(1)} %bitcast.36), channel_id=1, source_target_pairs={{0,1},{1,0},{2,33},{3,32},{4,65},{5,64},{6,97},{7,96},{8,129},{9,1... | collective-permute-start | bytes 393224 | tf_op jit(solution)/shard_map/ppermute | solution.py:188
  19.4 21.9 %collective-permute-done = bf16[32,32,64]{2,0,1:T(8,128)(2,1)S(1)} collective-permute-done((bf16[32,32,64]{2,0,1:T(8,128)(2,1)S(1)}, bf16[32,32,64]{2,0,1:T(8,128)(2,1)S(1)}, u32[]{:S(2)}, u32[]{:S(2)}) %collective-permute-start) | collective-permute-done | bytes 131104 | tf_op jit(solution)/shard_map/ppermute | solution.py:188
  41.3 15.6 %collective-permute-done.1 = bf16[32,32,64]{2,0,1:T(8,128)(2,1)S(1)} collective-permute-done((bf16[32,32,64]{2,0,1:T(8,128)(2,1)S(1)}, bf16[32,32,64]{2,0,1:T(8,128)(2,1)S(1)}, u32[]{:S(2)}, u32[]{:S(2)}) %collective-permute-start.1) | collective-permute-done | bytes 131104 | tf_op jit(solution)/shard_map/ppermute | solution.py:188
  57.0 0.3 fusion.5
  57.2 0.9 pad_maximum_fusion
  58.1 0.0 copy-start.4
  58.2 0.0 copy-done
  58.2 0.1 pad_maximum_fusion.1
  58.3 1.9 %collective-permute-start.2 = (bf16[14,2,32,64]{3,2,1,0:T(8,128)(2,1)S(1)}, bf16[14,2,32,64]{3,2,1,0:T(8,128)(2,1)S(1)}, u32[]{:S(2)}, u32[]{:S(2)}) collective-permute-start(bf16[14,2,32,64]{3,2,1,0:T(8,128)(2,1)S(1)} %pad_maximum_fusion.2), channel_id=1, source_target_pairs={{0,32},{32,64},{64,96},{96,128},{128,160},{160,192},{192,224},{224... | collective-permute-start | bytes 344072 | tf_op jit(solution)/shard_map/ppermute | solution.py:146
  60.2 8.9 %collective-permute-start.3 = (bf16[15,2,32,64]{3,2,1,0:T(8,128)(2,1)S(1)}, bf16[15,2,32,64]{3,2,1,0:T(8,128)(2,1)S(1)}, u32[]{:S(2)}, u32[]{:S(2)}) collective-permute-start(bf16[15,2,32,64]{3,2,1,0:T(8,128)(2,1)S(1)} %pad_maximum_fusion.1), channel_id=1, source_target_pairs={{32,0},{64,32},{96,64},{128,96},{160,128},{192,160},{224,192},{256... | collective-permute-start | bytes 368648 | tf_op jit(solution)/shard_map/ppermute | solution.py:147
  69.1 0.0 copy-done.4
  69.1 0.6 slice_bitcast_fusion
  69.7 0.6 add_convert_fusion.1.ends_ref.src_ends_ref
  70.3 0.0 collective-permute-done.2.left_ref
  70.4 0.0 copy-start.3
  70.4 3.5 %collective-permute-done.3.right_ref = bf16[15,2,32,64]{3,2,1,0:T(8,128)(2,1)S(1)} collective-permute-done((bf16[15,2,32,64]{3,2,1,0:T(8,128)(2,1)S(1)}, bf16[15,2,32,64]{3,2,1,0:T(8,128)(2,1)S(1)}, u32[]{:S(2)}, u32[]{:S(2)}) %collective-permute-start.3) | collective-permute-done | bytes 122912 | tf_op jit(solution)/shard_map/ppermute | solution.py:147
  73.8 0.0 copy-start.2
  73.8 0.0 copy-done.3
  73.8 0.7 copy-done.2
  74.5 3.7 %shard_map.55.mid_ref = f32[73,32,64]{2,1,0:T(8,128)} custom-call(s32[2]{0:T(128)} %add_convert_fusion.1.ends_ref.src_ends_ref, s32[1,1,64]{2,1,0:T(1,128)} %get-tuple-element.11.depth_ref.src_depth_ref, bf16[14,2,32,64]{3,2,1,0:T(8,128)(2,1)} %copy-done.3, bf16[64,32,64]{2,1,0:T(8,128)(2,1)} %copy-done, bf16[64,32,64]{2,1,0:T(8,128)(2,1)} %get-tuple-element.5.mirror_ref, ...), custom_call_target="tpu_custom_call" | custom-call | tf_op jit(solution)/shard_map/pallas_call | solution.py:132
  78.2 0.0 slice-start
  78.2 0.0 copy-start.1
  78.2 1.1 slice-done
  79.3 0.3 copy.11
  79.6 13.1 %collective-permute-start.5 = (f32[73,15,64]{0,2,1:T(8,128)S(1)}, f32[73,15,64]{0,2,1:T(8,128)S(1)}, u32[]{:S(2)}, u32[]{:S(2)}) collective-permute-start(f32[73,15,64]{0,2,1:T(8,128)S(1)} %copy.11), channel_id=1, source_target_pairs={{1,0},{2,1},{3,2},{4,3},{5,4},{6,5},{7,6},{8,7},{9,8},{10,9},{11,1... | collective-permute-start | bytes 840968 | tf_op jit(solution)/shard_map/ppermute | solution.py:147
  92.7 0.0 copy-done.1
  92.7 0.1 slice.24
  92.8 0.3 copy.10
  93.1 1.9 %collective-permute-start.4 = (f32[73,14,64]{0,2,1:T(8,128)S(1)}, f32[73,14,64]{0,2,1:T(8,128)S(1)}, u32[]{:S(2)}, u32[]{:S(2)}) collective-permute-start(f32[73,14,64]{0,2,1:T(8,128)S(1)} %copy.10), channel_id=1, source_target_pairs={{0,1},{1,2},{2,3},{3,4},{4,5},{5,6},{6,7},{7,8},{8,9},{9,10},{10,1... | collective-permute-start | bytes 784904 | tf_op jit(solution)/shard_map/ppermute | solution.py:146
  95.0 0.7 add_convert_fusion.rcv_ends_ref
  95.7 8.7 %collective-permute-done.4 = f32[73,14,64]{0,2,1:T(8,128)S(1)} collective-permute-done((f32[73,14,64]{0,2,1:T(8,128)S(1)}, f32[73,14,64]{0,2,1:T(8,128)S(1)}, u32[]{:S(2)}, u32[]{:S(2)}) %collective-permute-start.4) | collective-permute-done | bytes 261664 | tf_op jit(solution)/shard_map/ppermute | solution.py:146
  104.4 1.1 copy.12.left_ref
  105.5 0.0 collective-permute-done.5
  105.5 1.1 copy.13.right_ref
  106.7 8.3 %shard_map.56 = f32[64,32,64]{2,1,0:T(8,128)} custom-call(s32[2]{0:T(128)} %add_convert_fusion.rcv_ends_ref, s32[2]{0:T(128)} %add_convert_fusion.1.ends_ref.src_ends_ref, s32[1,1,64]{2,1,0:T(1,128)} %get-tuple-element.12.rcv_depth_ref, s32[1,1,64]{2,1,0:T(1,128)} %get-tuple-element.11.depth_ref.src_depth_ref, f32[1,1,64]{2,1,0:T(1,128)} %bitcast.37, ...), custom_call_target="tpu_custom_call" | custom-call | tf_op jit(solution)/shard_map/pallas_call | solution.py:132
  (2 shorter events, 0.1 us)
Async XLA Ops:
  3.3 54.8 %copy-start = (bf16[64,32,64]{2,1,0:T(8,128)(2,1)}, bf16[64,32,64]{2,1,0:T(8,128)(2,1)S(1)}, u32[]{:S(2)}) copy-start(bf16[64,32,64]{2,1,0:T(8,128)(2,1)S(1)} %fusion.1.merged_ref) | copy-start | bytes 786436
  3.5 37.8 %collective-permute-start = (bf16[32,32,64]{2,0,1:T(8,128)(2,1)S(1)}, bf16[32,32,64]{2,0,1:T(8,128)(2,1)S(1)}, u32[]{:S(2)}, u32[]{:S(2)}) collective-permute-start(bf16[32,32,64]{2,0,1:T(8,128)(2,1)S(1)} %bitcast.35), channel_id=1, source_target_pairs={{0,0},{1,1},{2,32},{3,33},{4,64},{5,65},{6,96},{7,97},{8,128},{9,1... | collective-permute-start | bytes 393224 | tf_op jit(solution)/shard_map/ppermute | solution.py:188
  17.5 39.5 %collective-permute-start.1 = (bf16[32,32,64]{2,0,1:T(8,128)(2,1)S(1)}, bf16[32,32,64]{2,0,1:T(8,128)(2,1)S(1)}, u32[]{:S(2)}, u32[]{:S(2)}) collective-permute-start(bf16[32,32,64]{2,0,1:T(8,128)(2,1)S(1)} %bitcast.36), channel_id=1, source_target_pairs={{0,1},{1,0},{2,33},{3,32},{4,65},{5,64},{6,97},{7,96},{8,129},{9,1... | collective-permute-start | bytes 393224 | tf_op jit(solution)/shard_map/ppermute | solution.py:188
  58.1 11.0 %copy-start.4 = (s32[2,64]{1,0:T(2,128)S(1)}, s32[2,64]{1,0:T(2,128)}, u32[]{:S(2)}) copy-start(s32[2,64]{1,0:T(2,128)} %param.8) | copy-start | bytes 1540
  58.3 12.1 %collective-permute-start.2 = (bf16[14,2,32,64]{3,2,1,0:T(8,128)(2,1)S(1)}, bf16[14,2,32,64]{3,2,1,0:T(8,128)(2,1)S(1)}, u32[]{:S(2)}, u32[]{:S(2)}) collective-permute-start(bf16[14,2,32,64]{3,2,1,0:T(8,128)(2,1)S(1)} %pad_maximum_fusion.2), channel_id=1, source_target_pairs={{0,32},{32,64},{64,96},{96,128},{128,160},{160,192},{192,224},{224... | collective-permute-start | bytes 344072 | tf_op jit(solution)/shard_map/ppermute | solution.py:146
  60.2 13.6 %collective-permute-start.3 = (bf16[15,2,32,64]{3,2,1,0:T(8,128)(2,1)S(1)}, bf16[15,2,32,64]{3,2,1,0:T(8,128)(2,1)S(1)}, u32[]{:S(2)}, u32[]{:S(2)}) collective-permute-start(bf16[15,2,32,64]{3,2,1,0:T(8,128)(2,1)S(1)} %pad_maximum_fusion.1), channel_id=1, source_target_pairs={{32,0},{64,32},{96,64},{128,96},{160,128},{192,160},{224,192},{256... | collective-permute-start | bytes 368648 | tf_op jit(solution)/shard_map/ppermute | solution.py:147
  70.4 3.5 %copy-start.3 = (bf16[14,2,32,64]{3,2,1,0:T(8,128)(2,1)}, bf16[14,2,32,64]{3,2,1,0:T(8,128)(2,1)S(1)}, u32[]{:S(2)}) copy-start(bf16[14,2,32,64]{3,2,1,0:T(8,128)(2,1)S(1)} %collective-permute-done.2.left_ref) | copy-start | bytes 344068
  73.8 0.7 copy-start.2
  78.2 1.1 slice-start
  78.2 14.5 %copy-start.1 = (f32[73,32,64]{2,1,0:T(8,128)S(1)}, f32[73,32,64]{2,1,0:T(8,128)}, u32[]{:S(2)}) copy-start(f32[73,32,64]{2,1,0:T(8,128)} %shard_map.55.mid_ref) | copy-start | bytes 1794052
  79.6 26.0 %collective-permute-start.5 = (f32[73,15,64]{0,2,1:T(8,128)S(1)}, f32[73,15,64]{0,2,1:T(8,128)S(1)}, u32[]{:S(2)}, u32[]{:S(2)}) collective-permute-start(f32[73,15,64]{0,2,1:T(8,128)S(1)} %copy.11), channel_id=1, source_target_pairs={{1,0},{2,1},{3,2},{4,3},{5,4},{6,5},{7,6},{8,7},{9,8},{10,9},{11,1... | collective-permute-start | bytes 840968 | tf_op jit(solution)/shard_map/ppermute | solution.py:147
  93.1 11.3 %collective-permute-start.4 = (f32[73,14,64]{0,2,1:T(8,128)S(1)}, f32[73,14,64]{0,2,1:T(8,128)S(1)}, u32[]{:S(2)}, u32[]{:S(2)}) collective-permute-start(f32[73,14,64]{0,2,1:T(8,128)S(1)} %copy.10), channel_id=1, source_target_pairs={{0,1},{1,2},{2,3},{3,4},{4,5},{5,6},{6,7},{7,8},{8,9},{9,10},{10,1... | collective-permute-start | bytes 784904 | tf_op jit(solution)/shard_map/ppermute | solution.py:146

commit v9 on v7

--- a/solution.py
+++ b/solution.py
@@ -74,20 +74,21 @@
 
 
 def _src_forward_kernel(
-    ends_ref, depth_ref, left_ref, merged_ref, mirror_ref, right_ref, out_ref, work, *, width, out_from
+    ends_ref, depth_ref, left_ref, merged_ref, right_ref, mirror_ref, out_ref, work, *, width, out_from
 ):
     length = merged_ref.shape[0]
     ends = (ends_ref[0], ends_ref[1])
     depth = depth_ref[...]
-
-    def half_sum(ref):
-        return 0.5 * (ref[:, 0].astype(jnp.float32) + ref[:, 1].astype(jnp.float32))
-
-    body = 0.5 * (merged_ref[...].astype(jnp.float32) + mirror_ref[...].astype(jnp.float32))
+    near = left_ref.shape[0]
+    far = right_ref.shape[0]
+
+    def term_sum(ref, lo, size):
+        return 0.5 * (ref[...].astype(jnp.float32) + mirror_ref[lo : lo + size].astype(jnp.float32))
+
     parts = [
-        (PAD + width - left_ref.shape[0], half_sum(left_ref)),
-        (PAD + width, body),
-        (PAD + width + length, half_sum(right_ref)),
+        (PAD + width - near, term_sum(left_ref, 0, near)),
+        (PAD + width, term_sum(merged_ref, near, length)),
+        (PAD + width + length, term_sum(right_ref, near + length, far)),
     ]
     _fill(work, 0, parts, work.shape[0])
     for depth_index in range(LEVELS):
@@ -169,37 +170,46 @@
         est_float + local_mask[:, :, None] * (observed.astype(jnp.float32) - est_float)
     ).astype(jnp.bfloat16)
 
-    ratio = rcv_count // src_count
-    pieces = merged.reshape(ratio, col_count, col_count, samples)
-    own_part = rcv_index % ratio
+    assert rcv_count == 2 * src_count and row_count == 2 * col_count
+    left_cols, right_cols = halos(merged, "rcv", 1, FAR_LEFT, FAR_RIGHT)
+    left_src, right_src = halos(merged, "src", 0, FAR_LEFT, FAR_RIGHT)
+    wide_cols = col_count + max(FAR_LEFT, FAR_RIGHT)
+    spare = jnp.zeros((row_count, wide_cols - col_count - FAR_LEFT, samples), merged.dtype)
+    even_block = jnp.concatenate([left_cols, merged, spare], axis=1)
+    odd_block = jnp.concatenate([merged, right_cols], axis=1)
+    own_part = rcv_index % 2
+    block = jnp.where(own_part == 0, even_block, odd_block).reshape(2, col_count, wide_cols, samples)
     received = []
-    for shift in range(ratio):
+    for shift in range(2):
         perm = []
         for a in range(src_count):
             for b in range(rcv_count):
-                part = (b % ratio + shift) % ratio
-                perm.append((a * rcv_count + b, (b // ratio) * rcv_count + a * ratio + part))
-        send = lax.dynamic_index_in_dim(pieces, (own_part + shift) % ratio, axis=0, keepdims=False)
+                part = (b % 2 + shift) % 2
+                perm.append((a * rcv_count + b, (b // 2) * rcv_count + a * 2 + part))
+        send = jnp.where((own_part + shift) % 2 == 0, block[0], block[1])
         received.append(lax.ppermute(send, ("src", "rcv"), perm))
-    received = jnp.stack(received)
-    slots = []
-    for slot in range(ratio):
-        got = lax.dynamic_index_in_dim(received, (own_part - slot) % ratio, axis=0, keepdims=False)
-        slots.append(jnp.transpose(got, (1, 0, 2)))
-    mirror = jnp.concatenate(slots, axis=0)
+    from_even = jnp.where(own_part == 0, received[0], received[1])
+    from_odd = jnp.where(own_part == 0, received[1], received[0])
+    mirror = jnp.concatenate(
+        [
+            jnp.transpose(from_even[:, : FAR_LEFT + col_count], (1, 0, 2)),
+            jnp.transpose(from_odd[:, : col_count + FAR_RIGHT], (1, 0, 2)),
+        ],
+        axis=0,
+    )
+
     samples_shape = (1, 1, samples)
     src_depth = levels[0].reshape(samples_shape)
     rcv_depth = levels[1].reshape(samples_shape)
     src_ends = jnp.stack([src_index == 0, src_index == src_count - 1]).astype(jnp.int32)
     rcv_ends = jnp.stack([rcv_index == 0, rcv_index == rcv_count - 1]).astype(jnp.int32)
 
-    left_src, right_src = halos(jnp.stack([merged, mirror], axis=1), "src", 0, FAR_LEFT, FAR_RIGHT)
     coeff = _call(
         functools.partial(_src_forward_kernel, width=SLOT, out_from=NEAR_LEFT),
         (NEAR_LEFT + row_count + NEAR_RIGHT, col_count, samples),
         [(row_count + 2 * SLOT + 2 * PAD, col_count, samples)],
         1,
-        src_ends, src_depth, left_src, merged, mirror, right_src,
+        src_ends, src_depth, left_src, merged, right_src, mirror,
     )
     left_rcv, right_rcv = halos(coeff, "rcv", 1, FAR_LEFT, FAR_RIGHT)
     return _call(

time: 115 us -> 147 us (1.28)
  the two profiles are of different devices: /device:TPU:31 before, /device:TPU:90 now
where the time goes in v9:
time: 147 us
  waiting for transfers between devices  70.5 us (48%)
  starting transfers between devices  51.3 us (35%)
  Pallas kernels  12 us (8%)
  local copies, waits for them, and re-layouts  7.21 us (5%)
  other arithmetic  4.52 us (3%)
    ppermute x2, waiting for transfers between devices, body(): received.append(lax.ppermute(send, ('src', 'rcv'), perm))  53.2 us
    ppermute x3, starting transfers between devices, halos(): lax.ppermute(head, axis_name, [(i + 1, i) for i in range(count - 1)])  28 us
    ppermute x3, waiting for transfers between devices, halos(): lax.ppermute(tail, axis_name, [(i, i + 1) for i in range(count - 1)])  17.3 us
    ppermute x2, starting transfers between devices, body(): received.append(lax.ppermute(send, ('src', 'rcv'), perm))  15.1 us
    pallas_call x2, Pallas kernels, _call(): pl.pallas_call(kernel, out_shape=jax.ShapeDtypeStruct(out_shape, jnp.floa...  12 us
    ppermute x3, starting transfers between devices, halos(): lax.ppermute(tail, axis_name, [(i, i + 1) for i in range(count - 1)])  8.12 us
  transfers between devices with their start and end apart: 8, of which 4 were waited for; matrix products, arithmetic and copies ran while one was open for 4% of the time, Pallas kernels for 0%

profile of v9, /device:TPU:90, one launch (start us, length us, event | category | flops | bytes accessed | tf_op | source)
XLA Modules:
  0.0 146.8 jit_solution(13164106502063230516)
XLA Ops:
  0.0 0.9 fusion.3
  0.9 0.2 fusion.5
  1.1 1.7 %fusion.1 = bf16[64,32,64]{2,0,1:T(8,128)(2,1)S(1)} fusion(bf16[64,32,64]{2,1,0:T(8,128)(2,1)} %param.5, bf16[64,32,64]{2,1,0:T(8,128)(2,1)} %param.6, f32[64,32]{0,1:T(8,128)S(1)} %fusion.5), kind=kLoop, calls=%fused_computation.3 | loop fusion | flops 786432 | bytes 794624 | tf_op jit(solution)/shard_map/convert_element_type | solution.py:171
  2.8 1.9 %collective-permute-start.3 = (bf16[64,15,64]{2,0,1:T(8,128)(2,1)S(1)}, bf16[64,15,64]{2,0,1:T(8,128)(2,1)S(1)}, u32[]{:S(2)}, u32[]{:S(2)}) collective-permute-start(bf16[64,15,64]{2,0,1:T(8,128)(2,1)S(1)} %slice.51), channel_id=1, source_target_pairs={{1,0},{2,1},{3,2},{4,3},{5,4},{6,5},{7,6},{8,7},{9,8},{10,9},{11,1... | collective-permute-start | bytes 368648 | tf_op jit(solution)/shard_map/ppermute | solution.py:148
  4.7 4.3 %collective-permute-start.2 = (bf16[64,14,64]{2,0,1:T(8,128)(2,1)S(1)}, bf16[64,14,64]{2,0,1:T(8,128)(2,1)S(1)}, u32[]{:S(2)}, u32[]{:S(2)}) collective-permute-start(bf16[64,14,64]{2,0,1:T(8,128)(2,1)S(1)} %slice.50), channel_id=1, source_target_pairs={{0,1},{1,2},{2,3},{3,4},{4,5},{5,6},{6,7},{7,8},{8,9},{9,10},{10,1... | collective-permute-start | bytes 344072 | tf_op jit(solution)/shard_map/ppermute | solution.py:147
  9.1 1.9 %collective-permute-start = (bf16[14,32,64]{2,0,1:T(8,128)(2,1)S(1)}, bf16[14,32,64]{2,0,1:T(8,128)(2,1)S(1)}, u32[]{:S(2)}, u32[]{:S(2)}) collective-permute-start(bf16[14,32,64]{2,0,1:T(8,128)(2,1)S(1)} %slice.48), channel_id=1, source_target_pairs={{0,32},{32,64},{64,96},{96,128},{128,160},{160,192},{192,224},{224... | collective-permute-start | bytes 172040 | tf_op jit(solution)/shard_map/ppermute | solution.py:147
  11.0 3.6 %collective-permute-start.1 = (bf16[15,32,64]{2,0,1:T(8,128)(2,1)S(1)}, bf16[15,32,64]{2,0,1:T(8,128)(2,1)S(1)}, u32[]{:S(2)}, u32[]{:S(2)}) collective-permute-start(bf16[15,32,64]{2,0,1:T(8,128)(2,1)S(1)} %slice.49), channel_id=1, source_target_pairs={{32,0},{64,32},{96,64},{128,96},{160,128},{192,160},{224,192},{256... | collective-permute-start | bytes 184328 | tf_op jit(solution)/shard_map/ppermute | solution.py:148
  14.7 0.1 pad.6.clone
  14.8 5.7 %collective-permute-done.2 = bf16[64,14,64]{2,0,1:T(8,128)(2,1)S(1)} collective-permute-done((bf16[64,14,64]{2,0,1:T(8,128)(2,1)S(1)}, bf16[64,14,64]{2,0,1:T(8,128)(2,1)S(1)}, u32[]{:S(2)}, u32[]{:S(2)}) %collective-permute-start.2) | collective-permute-done | bytes 114720 | tf_op jit(solution)/shard_map/ppermute | solution.py:147
  20.5 0.0 collective-permute-done.3
  20.5 0.4 maximum_select_fusion
  20.9 0.0 copy-start.1
  20.9 0.1 broadcast_select_fusion.1
  21.0 7.1 %collective-permute-start.4 = (bf16[32,47,64]{2,0,1:T(8,128)(2,1)S(1)}, bf16[32,47,64]{2,0,1:T(8,128)(2,1)S(1)}, u32[]{:S(2)}, u32[]{:S(2)}) collective-permute-start(bf16[32,47,64]{2,0,1:T(8,128)(2,1)S(1)} %get-tuple-element.5), channel_id=1, source_target_pairs={{0,0},{1,1},{2,32},{3,33},{4,64},{5,65},{6,96},{7,97},{8,128},{9,1... | collective-permute-start | bytes 577544 | tf_op jit(solution)/shard_map/ppermute | solution.py:190
  28.1 8.1 %collective-permute-start.5 = (bf16[32,47,64]{2,0,1:T(8,128)(2,1)S(1)}, bf16[32,47,64]{2,0,1:T(8,128)(2,1)S(1)}, u32[]{:S(2)}, u32[]{:S(2)}) collective-permute-start(bf16[32,47,64]{2,0,1:T(8,128)(2,1)S(1)} %get-tuple-element.6), channel_id=1, source_target_pairs={{0,1},{1,0},{2,33},{3,32},{4,65},{5,64},{6,97},{7,96},{8,129},{9,1... | collective-permute-start | bytes 577544 | tf_op jit(solution)/shard_map/ppermute | solution.py:190
  36.1 0.0 copy-done.1
  36.1 0.6 slice_bitcast_fusion
  36.7 1.1 copy.14.merged_ref
  37.9 0.6 add_convert_fusion.1.ends_ref.src_ends_ref
  38.5 0.0 collective-permute-done
  38.5 0.7 copy.13.left_ref
  39.2 0.0 collective-permute-done.1
  39.2 0.7 copy.15.right_ref
  39.9 39.4 %collective-permute-done.4 = bf16[32,47,64]{2,0,1:T(8,128)(2,1)S(1)} collective-permute-done((bf16[32,47,64]{2,0,1:T(8,128)(2,1)S(1)}, bf16[32,47,64]{2,0,1:T(8,128)(2,1)S(1)}, u32[]{:S(2)}, u32[]{:S(2)}) %collective-permute-start.4) | collective-permute-done | bytes 192544 | tf_op jit(solution)/shard_map/ppermute | solution.py:190
  79.3 13.8 %collective-permute-done.5 = bf16[32,47,64]{2,0,1:T(8,128)(2,1)S(1)} collective-permute-done((bf16[32,47,64]{2,0,1:T(8,128)(2,1)S(1)}, bf16[32,47,64]{2,0,1:T(8,128)(2,1)S(1)}, u32[]{:S(2)}, u32[]{:S(2)}) %collective-permute-start.5) | collective-permute-done | bytes 192544 | tf_op jit(solution)/shard_map/ppermute | solution.py:190
  93.2 0.1 select_bitcast_fusion
  93.2 1.0 pad_maximum_fusion.mirror_ref
  94.2 3.7 %shard_map.55.mid_ref = f32[73,32,64]{2,1,0:T(8,128)} custom-call(s32[2]{0:T(128)} %add_convert_fusion.1.ends_ref.src_ends_ref, s32[1,1,64]{2,1,0:T(1,128)} %get-tuple-element.7.depth_ref.src_depth_ref, bf16[14,32,64]{2,1,0:T(8,128)(2,1)} %copy.13.left_ref, bf16[64,32,64]{2,1,0:T(8,128)(2,1)} %copy.14.merged_ref, bf16[15,32,64]{2,1,0:T(8,128)(2,1)} %copy.15.right_ref, ...), custom_call_target="tpu_custom_call" | custom-call | tf_op jit(solution)/shard_map/pallas_call | solution.py:133
  97.9 0.0 slice-start
  97.9 0.0 copy-start
  97.9 1.1 slice-done
  99.0 0.3 copy.17
  99.3 22.5 %collective-permute-start.7 = (f32[73,15,64]{0,2,1:T(8,128)S(1)}, f32[73,15,64]{0,2,1:T(8,128)S(1)}, u32[]{:S(2)}, u32[]{:S(2)}) collective-permute-start(f32[73,15,64]{0,2,1:T(8,128)S(1)} %copy.17), channel_id=1, source_target_pairs={{1,0},{2,1},{3,2},{4,3},{5,4},{6,5},{7,6},{8,7},{9,8},{10,9},{11,1... | collective-permute-start | bytes 840968 | tf_op jit(solution)/shard_map/ppermute | solution.py:148
  121.8 0.0 copy-done
  121.8 0.1 slice.56
  121.8 0.3 copy.16
  122.1 1.9 %collective-permute-start.6 = (f32[73,14,64]{0,2,1:T(8,128)S(1)}, f32[73,14,64]{0,2,1:T(8,128)S(1)}, u32[]{:S(2)}, u32[]{:S(2)}) collective-permute-start(f32[73,14,64]{0,2,1:T(8,128)S(1)} %copy.16), channel_id=1, source_target_pairs={{0,1},{1,2},{2,3},{3,4},{4,5},{5,6},{6,7},{7,8},{8,9},{9,10},{10,1... | collective-permute-start | bytes 784904 | tf_op jit(solution)/shard_map/ppermute | solution.py:147
  124.0 0.7 add_convert_fusion.rcv_ends_ref
  124.7 11.5 %collective-permute-done.6 = f32[73,14,64]{0,2,1:T(8,128)S(1)} collective-permute-done((f32[73,14,64]{0,2,1:T(8,128)S(1)}, f32[73,14,64]{0,2,1:T(8,128)S(1)}, u32[]{:S(2)}, u32[]{:S(2)}) %collective-permute-start.6) | collective-permute-done | bytes 261664 | tf_op jit(solution)/shard_map/ppermute | solution.py:147
  136.3 1.1 copy.18.left_ref
  137.4 0.0 collective-permute-done.7
  137.4 1.1 copy.19.right_ref
  138.5 8.3 %shard_map.56 = f32[64,32,64]{2,1,0:T(8,128)} custom-call(s32[2]{0:T(128)} %add_convert_fusion.rcv_ends_ref, s32[2]{0:T(128)} %add_convert_fusion.1.ends_ref.src_ends_ref, s32[1,1,64]{2,1,0:T(1,128)} %get-tuple-element.8.rcv_depth_ref, s32[1,1,64]{2,1,0:T(1,128)} %get-tuple-element.7.depth_ref.src_depth_ref, f32[1,1,64]{2,1,0:T(1,128)} %bitcast.15, ...), custom_call_target="tpu_custom_call" | custom-call | tf_op jit(solution)/shard_map/pallas_call | solution.py:133
  (7 shorter events, 0.2 us)
Async XLA Ops:
  2.8 17.7 %collective-permute-start.3 = (bf16[64,15,64]{2,0,1:T(8,128)(2,1)S(1)}, bf16[64,15,64]{2,0,1:T(8,128)(2,1)S(1)}, u32[]{:S(2)}, u32[]{:S(2)}) collective-permute-start(bf16[64,15,64]{2,0,1:T(8,128)(2,1)S(1)} %slice.51), channel_id=1, source_target_pairs={{1,0},{2,1},{3,2},{4,3},{5,4},{6,5},{7,6},{8,7},{9,8},{10,9},{11,1... | collective-permute-start | bytes 368648 | tf_op jit(solution)/shard_map/ppermute | solution.py:148
  4.7 15.8 %collective-permute-start.2 = (bf16[64,14,64]{2,0,1:T(8,128)(2,1)S(1)}, bf16[64,14,64]{2,0,1:T(8,128)(2,1)S(1)}, u32[]{:S(2)}, u32[]{:S(2)}) collective-permute-start(bf16[64,14,64]{2,0,1:T(8,128)(2,1)S(1)} %slice.50), channel_id=1, source_target_pairs={{0,1},{1,2},{2,3},{3,4},{4,5},{5,6},{6,7},{7,8},{8,9},{9,10},{10,1... | collective-permute-start | bytes 344072 | tf_op jit(solution)/shard_map/ppermute | solution.py:147
  9.1 29.4 %collective-permute-start = (bf16[14,32,64]{2,0,1:T(8,128)(2,1)S(1)}, bf16[14,32,64]{2,0,1:T(8,128)(2,1)S(1)}, u32[]{:S(2)}, u32[]{:S(2)}) collective-permute-start(bf16[14,32,64]{2,0,1:T(8,128)(2,1)S(1)} %slice.48), channel_id=1, source_target_pairs={{0,32},{32,64},{64,96},{96,128},{128,160},{160,192},{192,224},{224... | collective-permute-start | bytes 172040 | tf_op jit(solution)/shard_map/ppermute | solution.py:147
  11.0 28.2 %collective-permute-start.1 = (bf16[15,32,64]{2,0,1:T(8,128)(2,1)S(1)}, bf16[15,32,64]{2,0,1:T(8,128)(2,1)S(1)}, u32[]{:S(2)}, u32[]{:S(2)}) collective-permute-start(bf16[15,32,64]{2,0,1:T(8,128)(2,1)S(1)} %slice.49), channel_id=1, source_target_pairs={{32,0},{64,32},{96,64},{128,96},{160,128},{192,160},{224,192},{256... | collective-permute-start | bytes 184328 | tf_op jit(solution)/shard_map/ppermute | solution.py:148
  20.9 15.2 %copy-start.1 = (s32[2,64]{1,0:T(2,128)S(1)}, s32[2,64]{1,0:T(2,128)}, u32[]{:S(2)}) copy-start(s32[2,64]{1,0:T(2,128)} %param.8) | copy-start | bytes 1540
  21.0 58.3 %collective-permute-start.4 = (bf16[32,47,64]{2,0,1:T(8,128)(2,1)S(1)}, bf16[32,47,64]{2,0,1:T(8,128)(2,1)S(1)}, u32[]{:S(2)}, u32[]{:S(2)}) collective-permute-start(bf16[32,47,64]{2,0,1:T(8,128)(2,1)S(1)} %get-tuple-element.5), channel_id=1, source_target_pairs={{0,0},{1,1},{2,32},{3,33},{4,64},{5,65},{6,96},{7,97},{8,128},{9,1... | collective-permute-start | bytes 577544 | tf_op jit(solution)/shard_map/ppermute | solution.py:190
  28.1 65.1 %collective-permute-start.5 = (bf16[32,47,64]{2,0,1:T(8,128)(2,1)S(1)}, bf16[32,47,64]{2,0,1:T(8,128)(2,1)S(1)}, u32[]{:S(2)}, u32[]{:S(2)}) collective-permute-start(bf16[32,47,64]{2,0,1:T(8,128)(2,1)S(1)} %get-tuple-element.6), channel_id=1, source_target_pairs={{0,1},{1,0},{2,33},{3,32},{4,65},{5,64},{6,97},{7,96},{8,129},{9,1... | collective-permute-start | bytes 577544 | tf_op jit(solution)/shard_map/ppermute | solution.py:190
  97.9 1.1 slice-start
  97.9 23.8 %copy-start = (f32[73,32,64]{2,1,0:T(8,128)S(1)}, f32[73,32,64]{2,1,0:T(8,128)}, u32[]{:S(2)}) copy-start(f32[73,32,64]{2,1,0:T(8,128)} %shard_map.55.mid_ref) | copy-start | bytes 1794052
  99.3 38.1 %collective-permute-start.7 = (f32[73,15,64]{0,2,1:T(8,128)S(1)}, f32[73,15,64]{0,2,1:T(8,128)S(1)}, u32[]{:S(2)}, u32[]{:S(2)}) collective-permute-start(f32[73,15,64]{0,2,1:T(8,128)S(1)} %copy.17), channel_id=1, source_target_pairs={{1,0},{2,1},{3,2},{4,3},{5,4},{6,5},{7,6},{8,7},{9,8},{10,9},{11,1... | collective-permute-start | bytes 840968 | tf_op jit(solution)/shard_map/ppermute | solution.py:148
  122.1 14.1 %collective-permute-start.6 = (f32[73,14,64]{0,2,1:T(8,128)S(1)}, f32[73,14,64]{0,2,1:T(8,128)S(1)}, u32[]{:S(2)}, u32[]{:S(2)}) collective-permute-start(f32[73,14,64]{0,2,1:T(8,128)S(1)} %copy.16), channel_id=1, source_target_pairs={{0,1},{1,2},{2,3},{3,4},{4,5},{5,6},{6,7},{7,8},{8,9},{9,10},{10,1... | collective-permute-start | bytes 784904 | tf_op jit(solution)/shard_map/ppermute | solution.py:147

commit v10 on v7

--- a/solution.py
+++ b/solution.py
@@ -74,7 +74,8 @@
 
 
 def _src_forward_kernel(
-    ends_ref, depth_ref, left_ref, merged_ref, mirror_ref, right_ref, out_ref, work, *, width, out_from
+    ends_ref, depth_ref, left_ref, merged_ref, mirror_ref, right_ref, out_ref, tail_ref, head_ref, work,
+    *, width, out_from,
 ):
     length = merged_ref.shape[0]
     ends = (ends_ref[0], ends_ref[1])
@@ -92,7 +93,10 @@
     _fill(work, 0, parts, work.shape[0])
     for depth_index in range(LEVELS):
         _lift_level(work, 2**depth_index, depth > depth_index, True, width, length, ends)
-    out_ref[...] = work[PAD + width - out_from : PAD + width - out_from + out_ref.shape[0]]
+    coeff = work[PAD + width - out_from : PAD + width - out_from + out_ref.shape[0]]
+    out_ref[...] = coeff
+    tail_ref[...] = coeff[:, coeff.shape[1] - tail_ref.shape[1] :]
+    head_ref[...] = coeff[:, : head_ref.shape[1]]
 
 
 def _rcv_kernel(
@@ -129,20 +133,27 @@
 def _call(kernel, out_shape, scratch_shapes, smem_count, *operands):
     smem = pl.BlockSpec(memory_space=pltpu.SMEM)
     vmem = pl.BlockSpec(memory_space=pltpu.VMEM)
+    several = isinstance(out_shape, list)
+    shapes = out_shape if several else [out_shape]
+    outs = [jax.ShapeDtypeStruct(shape, jnp.float32) for shape in shapes]
     return pl.pallas_call(
         kernel,
-        out_shape=jax.ShapeDtypeStruct(out_shape, jnp.float32),
+        out_shape=outs if several else outs[0],
         in_specs=[smem] * smem_count + [vmem] * (len(operands) - smem_count),
-        out_specs=vmem,
+        out_specs=[vmem] * len(outs) if several else vmem,
         scratch_shapes=[pltpu.VMEM(shape, jnp.float32) for shape in scratch_shapes],
     )(*operands)
 
 
 def halos(cells, axis_name, dim, left_width, right_width):
-    count = lax.axis_size(axis_name)
     length = cells.shape[dim]
     head = lax.slice_in_dim(cells, 0, right_width, axis=dim)
     tail = lax.slice_in_dim(cells, length - left_width, length, axis=dim)
+    return swap(tail, head, axis_name)
+
+
+def swap(tail, head, axis_name):
+    count = lax.axis_size(axis_name)
     from_left = lax.ppermute(tail, axis_name, [(i, i + 1) for i in range(count - 1)])
     from_right = lax.ppermute(head, axis_name, [(i + 1, i) for i in range(count - 1)])
     return from_left, from_right
@@ -194,14 +205,18 @@
     rcv_ends = jnp.stack([rcv_index == 0, rcv_index == rcv_count - 1]).astype(jnp.int32)
 
     left_src, right_src = halos(jnp.stack([merged, mirror], axis=1), "src", 0, FAR_LEFT, FAR_RIGHT)
-    coeff = _call(
+    coeff, tail, head = _call(
         functools.partial(_src_forward_kernel, width=SLOT, out_from=NEAR_LEFT),
-        (NEAR_LEFT + row_count + NEAR_RIGHT, col_count, samples),
+        [
+            (NEAR_LEFT + row_count + NEAR_RIGHT, col_count, samples),
+            (NEAR_LEFT + row_count + NEAR_RIGHT, FAR_LEFT, samples),
+            (NEAR_LEFT + row_count + NEAR_RIGHT, FAR_RIGHT, samples),
+        ],
         [(row_count + 2 * SLOT + 2 * PAD, col_count, samples)],
         1,
         src_ends, src_depth, left_src, merged, mirror, right_src,
     )
-    left_rcv, right_rcv = halos(coeff, "rcv", 1, FAR_LEFT, FAR_RIGHT)
+    left_rcv, right_rcv = swap(tail, head, "rcv")
     return _call(
         functools.partial(_rcv_kernel, width=SLOT, src_width=NEAR_SLOT, in_from=NEAR_LEFT),
         (row_count, col_count, samples),

time: 115 us -> 115 us (level)
    slice x5 -> x0, local copies, waits for them, and re-layouts: 1.68 us -> none  [the longest x3 1.35 us: halos(): head = lax.slice_in_dim(cells, 0, right_width, axis=dim)]
    pallas_call x0 -> x2, local copies, waits for them, and re-layouts: none -> 1.66 us  [_call(): pl.pallas_call(kernel, out_shape=outs if several else outs[0], in_specs=[...]
where the time goes in v10:
time: 115 us; the launch traced here: 114 us
  waiting for transfers between devices  49.8 us (43%)
  starting transfers between devices  41.6 us (36%)
  Pallas kernels  12.1 us (11%)
  local copies, waits for them, and re-layouts  5.42 us (5%)
  other arithmetic  4.12 us (4%)
    ppermute x2, waiting for transfers between devices, body(): received.append(lax.ppermute(send, ('src', 'rcv'), perm))  37.5 us
    ppermute x2, starting transfers between devices, swap(): lax.ppermute(head, axis_name, [(i + 1, i) for i in range(count - 1)])  22 us
    ppermute x2, starting transfers between devices, body(): received.append(lax.ppermute(send, ('src', 'rcv'), perm))  15.8 us
    pallas_call x2, Pallas kernels, _call(): pl.pallas_call(kernel, out_shape=outs if several else outs[0], in_specs=[...  12.1 us
    ppermute x2, waiting for transfers between devices, swap(): lax.ppermute(tail, axis_name, [(i, i + 1) for i in range(count - 1)])  8.75 us
    ppermute x2, starting transfers between devices, swap(): lax.ppermute(tail, axis_name, [(i, i + 1) for i in range(count - 1)])  3.84 us
    ppermute x2, waiting for transfers between devices, swap(): lax.ppermute(head, axis_name, [(i + 1, i) for i in range(count - 1)])  3.54 us
  transfers between devices with their start and end apart: 6, of which 4 were waited for; matrix products, arithmetic and copies ran while one was open for 3% of the time, Pallas kernels for 0%

profile of v10, /device:TPU:31, one launch (start us, length us, event | category | flops | bytes accessed | tf_op | source)
XLA Modules:
  0.0 114.4 jit_solution(3051318276651954016)
XLA Ops:
  0.0 0.9 fusion.6
  0.9 0.2 fusion.8
  1.2 1.5 %fusion.1.merged_ref = bf16[64,32,64]{2,1,0:T(8,128)(2,1)S(1)} fusion(bf16[64,32,64]{2,1,0:T(8,128)(2,1)} %param.6, bf16[64,32,64]{2,1,0:T(8,128)(2,1)} %param.5, f32[64,32]{1,0:T(8,128)S(1)} %fusion.8), kind=kLoop, calls=%fused_computation.3 | loop fusion | flops 786432 | bytes 794624 | tf_op jit(solution)/shard_map/convert_element_type | solution.py:181
  2.7 0.0 copy-start
  2.8 0.1 copy.20
  2.9 13.8 %collective-permute-start = (bf16[32,32,64]{2,0,1:T(8,128)(2,1)S(1)}, bf16[32,32,64]{2,0,1:T(8,128)(2,1)S(1)}, u32[]{:S(2)}, u32[]{:S(2)}) collective-permute-start(bf16[32,32,64]{2,0,1:T(8,128)(2,1)S(1)} %bitcast.35), channel_id=1, source_target_pairs={{0,0},{1,1},{2,32},{3,33},{4,64},{5,65},{6,96},{7,97},{8,128},{9,1... | collective-permute-start | bytes 393224 | tf_op jit(solution)/shard_map/ppermute | solution.py:194
  16.7 0.1 copy.19
  16.8 1.9 %collective-permute-start.1 = (bf16[32,32,64]{2,0,1:T(8,128)(2,1)S(1)}, bf16[32,32,64]{2,0,1:T(8,128)(2,1)S(1)}, u32[]{:S(2)}, u32[]{:S(2)}) collective-permute-start(bf16[32,32,64]{2,0,1:T(8,128)(2,1)S(1)} %bitcast.36), channel_id=1, source_target_pairs={{0,1},{1,0},{2,33},{3,32},{4,65},{5,64},{6,97},{7,96},{8,129},{9,1... | collective-permute-start | bytes 393224 | tf_op jit(solution)/shard_map/ppermute | solution.py:194
  18.8 21.9 %collective-permute-done = bf16[32,32,64]{2,0,1:T(8,128)(2,1)S(1)} collective-permute-done((bf16[32,32,64]{2,0,1:T(8,128)(2,1)S(1)}, bf16[32,32,64]{2,0,1:T(8,128)(2,1)S(1)}, u32[]{:S(2)}, u32[]{:S(2)}) %collective-permute-start) | collective-permute-done | bytes 131104 | tf_op jit(solution)/shard_map/ppermute | solution.py:194
  40.7 15.6 %collective-permute-done.1 = bf16[32,32,64]{2,0,1:T(8,128)(2,1)S(1)} collective-permute-done((bf16[32,32,64]{2,0,1:T(8,128)(2,1)S(1)}, bf16[32,32,64]{2,0,1:T(8,128)(2,1)S(1)}, u32[]{:S(2)}, u32[]{:S(2)}) %collective-permute-start.1) | collective-permute-done | bytes 131104 | tf_op jit(solution)/shard_map/ppermute | solution.py:194
  56.3 0.3 fusion.5
  56.6 0.9 pad_maximum_fusion
  57.5 0.0 copy-start.4
  57.5 0.0 copy-done
  57.6 0.1 pad_maximum_fusion.1
  57.6 1.9 %collective-permute-start.2 = (bf16[14,2,32,64]{3,2,1,0:T(8,128)(2,1)S(1)}, bf16[14,2,32,64]{3,2,1,0:T(8,128)(2,1)S(1)}, u32[]{:S(2)}, u32[]{:S(2)}) collective-permute-start(bf16[14,2,32,64]{3,2,1,0:T(8,128)(2,1)S(1)} %pad_maximum_fusion.2), channel_id=1, source_target_pairs={{0,32},{32,64},{64,96},{96,128},{128,160},{160,192},{192,224},{224... | collective-permute-start | bytes 344072 | tf_op jit(solution)/shard_map/ppermute | solution.py:157
  59.5 8.9 %collective-permute-start.3 = (bf16[15,2,32,64]{3,2,1,0:T(8,128)(2,1)S(1)}, bf16[15,2,32,64]{3,2,1,0:T(8,128)(2,1)S(1)}, u32[]{:S(2)}, u32[]{:S(2)}) collective-permute-start(bf16[15,2,32,64]{3,2,1,0:T(8,128)(2,1)S(1)} %pad_maximum_fusion.1), channel_id=1, source_target_pairs={{32,0},{64,32},{96,64},{128,96},{160,128},{192,160},{224,192},{256... | collective-permute-start | bytes 368648 | tf_op jit(solution)/shard_map/ppermute | solution.py:158
  68.4 0.0 copy-done.4
  68.4 0.5 slice_bitcast_fusion
  69.0 0.6 add_convert_fusion.1.ends_ref.src_ends_ref
  69.6 0.0 collective-permute-done.2.left_ref
  69.6 0.0 copy-start.3
  69.6 3.5 %collective-permute-done.3.right_ref = bf16[15,2,32,64]{3,2,1,0:T(8,128)(2,1)S(1)} collective-permute-done((bf16[15,2,32,64]{3,2,1,0:T(8,128)(2,1)S(1)}, bf16[15,2,32,64]{3,2,1,0:T(8,128)(2,1)S(1)}, u32[]{:S(2)}, u32[]{:S(2)}) %collective-permute-start.3) | collective-permute-done | bytes 122912 | tf_op jit(solution)/shard_map/ppermute | solution.py:158
  73.2 0.0 copy-start.2
  73.2 0.0 copy-done.3
  73.2 0.7 copy-done.2
  73.9 3.8 %shard_map.55 = (f32[73,32,64]{2,1,0:T(8,128)}, f32[73,14,64]{2,1,0:T(8,128)}, f32[73,15,64]{2,1,0:T(8,128)}) custom-call(s32[2]{0:T(128)} %add_convert_fusion.1.ends_ref.src_ends_ref, s32[1,1,64]{2,1,0:T(1,128)} %get-tuple-element.17.depth_ref.src_depth_ref, bf16[14,2,32,64]{3,2,1,0:T(8,128)(2,1)} %copy-done.3, bf16[64,32,64]{2,1,0:T(8,128)(2,1)} %copy-done, ...), custom_call_target="tpu_custom_call" | custom-call | tf_op jit(solution)/shard_map/pallas_call | solution.py:139
  77.7 0.0 copy-start.1
  77.7 1.4 %copy.13 = f32[73,15,64]{0,2,1:T(8,128)S(1)} copy(f32[73,15,64]{2,1,0:T(8,128)} %get-tuple-element.10) | data formatting | bytes 560640 | tf_op jit(solution)/shard_map/pallas_call | solution.py:139
  79.1 13.1 %collective-permute-start.5 = (f32[73,15,64]{0,2,1:T(8,128)S(1)}, f32[73,15,64]{0,2,1:T(8,128)S(1)}, u32[]{:S(2)}, u32[]{:S(2)}) collective-permute-start(f32[73,15,64]{0,2,1:T(8,128)S(1)} %copy.13), channel_id=1, source_target_pairs={{1,0},{2,1},{3,2},{4,3},{5,4},{6,5},{7,6},{8,7},{9,8},{10,9},{11,1... | collective-permute-start | bytes 840968 | tf_op jit(solution)/shard_map/ppermute | solution.py:158
  92.3 0.0 copy-done.1
  92.3 0.3 copy.12
  92.6 1.9 %collective-permute-start.4 = (f32[73,14,64]{0,2,1:T(8,128)S(1)}, f32[73,14,64]{0,2,1:T(8,128)S(1)}, u32[]{:S(2)}, u32[]{:S(2)}) collective-permute-start(f32[73,14,64]{0,2,1:T(8,128)S(1)} %copy.12), channel_id=1, source_target_pairs={{0,1},{1,2},{2,3},{3,4},{4,5},{5,6},{6,7},{7,8},{8,9},{9,10},{10,1... | collective-permute-start | bytes 784904 | tf_op jit(solution)/shard_map/ppermute | solution.py:157
  94.5 0.6 add_convert_fusion.rcv_ends_ref
  95.1 8.8 %collective-permute-done.4 = f32[73,14,64]{0,2,1:T(8,128)S(1)} collective-permute-done((f32[73,14,64]{0,2,1:T(8,128)S(1)}, f32[73,14,64]{0,2,1:T(8,128)S(1)}, u32[]{:S(2)}, u32[]{:S(2)}) %collective-permute-start.4) | collective-permute-done | bytes 261664 | tf_op jit(solution)/shard_map/ppermute | solution.py:157
  103.9 1.1 copy.14.left_ref
  105.0 0.0 collective-permute-done.5
  105.0 1.1 copy.15.right_ref
  106.1 8.3 %shard_map.56 = f32[64,32,64]{2,1,0:T(8,128)} custom-call(s32[2]{0:T(128)} %add_convert_fusion.rcv_ends_ref, s32[2]{0:T(128)} %add_convert_fusion.1.ends_ref.src_ends_ref, s32[1,1,64]{2,1,0:T(1,128)} %get-tuple-element.18.rcv_depth_ref, s32[1,1,64]{2,1,0:T(1,128)} %get-tuple-element.17.depth_ref.src_depth_ref, f32[1,1,64]{2,1,0:T(1,128)} %bitcast.37, ...), custom_call_target="tpu_custom_call" | custom-call | tf_op jit(solution)/shard_map/pallas_call | solution.py:139
  (4 shorter events, 0.1 us)
Async XLA Ops:
  2.7 54.8 %copy-start = (bf16[64,32,64]{2,1,0:T(8,128)(2,1)}, bf16[64,32,64]{2,1,0:T(8,128)(2,1)S(1)}, u32[]{:S(2)}) copy-start(bf16[64,32,64]{2,1,0:T(8,128)(2,1)S(1)} %fusion.1.merged_ref) | copy-start | bytes 786436
  2.9 37.8 %collective-permute-start = (bf16[32,32,64]{2,0,1:T(8,128)(2,1)S(1)}, bf16[32,32,64]{2,0,1:T(8,128)(2,1)S(1)}, u32[]{:S(2)}, u32[]{:S(2)}) collective-permute-start(bf16[32,32,64]{2,0,1:T(8,128)(2,1)S(1)} %bitcast.35), channel_id=1, source_target_pairs={{0,0},{1,1},{2,32},{3,33},{4,64},{5,65},{6,96},{7,97},{8,128},{9,1... | collective-permute-start | bytes 393224 | tf_op jit(solution)/shard_map/ppermute | solution.py:194
  16.8 39.5 %collective-permute-start.1 = (bf16[32,32,64]{2,0,1:T(8,128)(2,1)S(1)}, bf16[32,32,64]{2,0,1:T(8,128)(2,1)S(1)}, u32[]{:S(2)}, u32[]{:S(2)}) collective-permute-start(bf16[32,32,64]{2,0,1:T(8,128)(2,1)S(1)} %bitcast.36), channel_id=1, source_target_pairs={{0,1},{1,0},{2,33},{3,32},{4,65},{5,64},{6,97},{7,96},{8,129},{9,1... | collective-permute-start | bytes 393224 | tf_op jit(solution)/shard_map/ppermute | solution.py:194
  57.5 10.9 %copy-start.4 = (s32[2,64]{1,0:T(2,128)S(1)}, s32[2,64]{1,0:T(2,128)}, u32[]{:S(2)}) copy-start(s32[2,64]{1,0:T(2,128)} %param.8) | copy-start | bytes 1540
  57.6 12.0 %collective-permute-start.2 = (bf16[14,2,32,64]{3,2,1,0:T(8,128)(2,1)S(1)}, bf16[14,2,32,64]{3,2,1,0:T(8,128)(2,1)S(1)}, u32[]{:S(2)}, u32[]{:S(2)}) collective-permute-start(bf16[14,2,32,64]{3,2,1,0:T(8,128)(2,1)S(1)} %pad_maximum_fusion.2), channel_id=1, source_target_pairs={{0,32},{32,64},{64,96},{96,128},{128,160},{160,192},{192,224},{224... | collective-permute-start | bytes 344072 | tf_op jit(solution)/shard_map/ppermute | solution.py:157
  59.5 13.6 %collective-permute-start.3 = (bf16[15,2,32,64]{3,2,1,0:T(8,128)(2,1)S(1)}, bf16[15,2,32,64]{3,2,1,0:T(8,128)(2,1)S(1)}, u32[]{:S(2)}, u32[]{:S(2)}) collective-permute-start(bf16[15,2,32,64]{3,2,1,0:T(8,128)(2,1)S(1)} %pad_maximum_fusion.1), channel_id=1, source_target_pairs={{32,0},{64,32},{96,64},{128,96},{160,128},{192,160},{224,192},{256... | collective-permute-start | bytes 368648 | tf_op jit(solution)/shard_map/ppermute | solution.py:158
  69.6 3.5 %copy-start.3 = (bf16[14,2,32,64]{3,2,1,0:T(8,128)(2,1)}, bf16[14,2,32,64]{3,2,1,0:T(8,128)(2,1)S(1)}, u32[]{:S(2)}) copy-start(bf16[14,2,32,64]{3,2,1,0:T(8,128)(2,1)S(1)} %collective-permute-done.2.left_ref) | copy-start | bytes 344068
  73.2 0.7 copy-start.2
  77.7 14.5 %copy-start.1 = (f32[73,14,64]{2,1,0:T(8,128)S(1)}, f32[73,14,64]{2,1,0:T(8,128)}, u32[]{:S(2)}) copy-start(f32[73,14,64]{2,1,0:T(8,128)} %get-tuple-element.8) | copy-start | bytes 784900
  79.1 25.9 %collective-permute-start.5 = (f32[73,15,64]{0,2,1:T(8,128)S(1)}, f32[73,15,64]{0,2,1:T(8,128)S(1)}, u32[]{:S(2)}, u32[]{:S(2)}) collective-permute-start(f32[73,15,64]{0,2,1:T(8,128)S(1)} %copy.13), channel_id=1, source_target_pairs={{1,0},{2,1},{3,2},{4,3},{5,4},{6,5},{7,6},{8,7},{9,8},{10,9},{11,1... | collective-permute-start | bytes 840968 | tf_op jit(solution)/shard_map/ppermute | solution.py:158
  92.6 11.3 %collective-permute-start.4 = (f32[73,14,64]{0,2,1:T(8,128)S(1)}, f32[73,14,64]{0,2,1:T(8,128)S(1)}, u32[]{:S(2)}, u32[]{:S(2)}) collective-permute-start(f32[73,14,64]{0,2,1:T(8,128)S(1)} %copy.12), channel_id=1, source_target_pairs={{0,1},{1,2},{2,3},{3,4},{4,5},{5,6},{6,7},{7,8},{8,9},{9,10},{10,1... | collective-permute-start | bytes 784904 | tf_op jit(solution)/shard_map/ppermute | solution.py:157

commit v11 on v10

--- a/solution.py
+++ b/solution.py
@@ -23,8 +23,8 @@
     shape = list(work.shape)
     shape[axis] = pairs
     pair_ids = lax.broadcasted_iota(jnp.int32, tuple(shape), axis)
-    first = (pair_ids == width // step) & (ends[0] != 0)
-    last = (pair_ids == (width + length) // step - 1) & (ends[1] != 0)
+    first = (pair_ids == width // step) & ends[0]
+    last = (pair_ids == (width + length) // step - 1) & ends[1]
 
     def at(start):
         window = pl.ds(start, pairs, stride=step)
@@ -54,6 +54,11 @@
         work[odds] = jnp.where(enabled, odd_part, detail)
 
 
+def _ends(axis_name):
+    index = lax.axis_index(axis_name)
+    return (index == 0, index == lax.axis_size(axis_name) - 1)
+
+
 def _fill(work, axis, parts, total):
     def span(lo, hi):
         return (slice(lo, hi),) if axis == 0 else (slice(None), slice(lo, hi))
@@ -74,11 +79,11 @@
 
 
 def _src_forward_kernel(
-    ends_ref, depth_ref, left_ref, merged_ref, mirror_ref, right_ref, out_ref, tail_ref, head_ref, work,
+    depth_ref, left_ref, merged_ref, mirror_ref, right_ref, out_ref, tail_ref, head_ref, work,
     *, width, out_from,
 ):
     length = merged_ref.shape[0]
-    ends = (ends_ref[0], ends_ref[1])
+    ends = _ends("src")
     depth = depth_ref[...]
 
     def half_sum(ref):
@@ -100,11 +105,11 @@
 
 
 def _rcv_kernel(
-    rcv_ends_ref, src_ends_ref, rcv_depth_ref, src_depth_ref, thr_ref, left_ref, mid_ref, right_ref,
+    rcv_depth_ref, src_depth_ref, thr_ref, left_ref, mid_ref, right_ref,
     out_ref, work, rows_work, *, width, src_width, in_from,
 ):
     length = mid_ref.shape[1]
-    ends = (rcv_ends_ref[0], rcv_ends_ref[1])
+    ends = _ends("rcv")
     depth = rcv_depth_ref[...]
     parts = [
         (PAD + width - left_ref.shape[1], left_ref[...]),
@@ -121,7 +126,7 @@
         _lift_level(work, 2**depth_index, depth > depth_index, False, width, length, ends, axis=1)
 
     row_count = out_ref.shape[0]
-    ends = (src_ends_ref[0], src_ends_ref[1])
+    ends = _ends("src")
     depth = src_depth_ref[...]
     block = work[:, PAD + width : PAD + width + length]
     _fill(rows_work, 0, [(PAD + src_width - in_from, block)], rows_work.shape[0])
@@ -201,8 +206,6 @@
     samples_shape = (1, 1, samples)
     src_depth = levels[0].reshape(samples_shape)
     rcv_depth = levels[1].reshape(samples_shape)
-    src_ends = jnp.stack([src_index == 0, src_index == src_count - 1]).astype(jnp.int32)
-    rcv_ends = jnp.stack([rcv_index == 0, rcv_index == rcv_count - 1]).astype(jnp.int32)
 
     left_src, right_src = halos(jnp.stack([merged, mirror], axis=1), "src", 0, FAR_LEFT, FAR_RIGHT)
     coeff, tail, head = _call(
@@ -213,8 +216,8 @@
             (NEAR_LEFT + row_count + NEAR_RIGHT, FAR_RIGHT, samples),
         ],
         [(row_count + 2 * SLOT + 2 * PAD, col_count, samples)],
-        1,
-        src_ends, src_depth, left_src, merged, mirror, right_src,
+        0,
+        src_depth, left_src, merged, mirror, right_src,
     )
     left_rcv, right_rcv = swap(tail, head, "rcv")
     return _call(
@@ -224,8 +227,8 @@
             (coeff.shape[0], col_count + 2 * SLOT + 2 * PAD, samples),
             (row_count + 2 * NEAR_SLOT + 2 * PAD, col_count, samples),
         ],
-        2,
-        rcv_ends, src_ends, rcv_depth, src_depth, thresholds.reshape(samples_shape),
+        0,
+        rcv_depth, src_depth, thresholds.reshape(samples_shape),
         left_rcv, coeff, right_rcv,
     )
 

time: 115 us -> 115 us (level)
  waiting for transfers between devices: 49.8 us -> 51.1 us
  other arithmetic: 4.12 us -> 2.83 us
    convert_element_type x2 -> x0, other arithmetic: 1.29 us -> none  [the longest x1 0.65 us: body(): jnp.stack([rcv_index == 0, rcv_index == rcv_count - 1]).astype(jnp.int32)]
  transfers between devices with their start and end apart: 6 -> 6, of which waited for: 4 -> 4; matrix products, arithmetic and copies ran while one was open for 3% -> 2% of each run, Pallas kernels for 0% -> 0%
where the time goes in v11:
time: 115 us; the launch traced here: 114 us
  waiting for transfers between devices  51.1 us (44%)
  starting transfers between devices  41.6 us (36%)
  Pallas kernels  12.1 us (11%)
  local copies, waits for them, and re-layouts  5.42 us (5%)
  other arithmetic  2.83 us (2%)
    ppermute x2, waiting for transfers between devices, body(): received.append(lax.ppermute(send, ('src', 'rcv'), perm))  37.5 us
    ppermute x2, starting transfers between devices, swap(): lax.ppermute(head, axis_name, [(i + 1, i) for i in range(count - 1)])  22.1 us
    ppermute x2, starting transfers between devices, body(): received.append(lax.ppermute(send, ('src', 'rcv'), perm))  15.8 us
    pallas_call x2, Pallas kernels, _call(): pl.pallas_call(kernel, out_shape=outs if several else outs[0], in_specs=[...  12.1 us
    ppermute x2, waiting for transfers between devices, swap(): lax.ppermute(tail, axis_name, [(i, i + 1) for i in range(count - 1)])  9.41 us
    ppermute x2, waiting for transfers between devices, swap(): lax.ppermute(head, axis_name, [(i + 1, i) for i in range(count - 1)])  4.17 us
    ppermute x2, starting transfers between devices, swap(): lax.ppermute(tail, axis_name, [(i, i + 1) for i in range(count - 1)])  3.84 us
  transfers between devices with their start and end apart: 6, of which 4 were waited for; matrix products, arithmetic and copies ran while one was open for 2% of the time, Pallas kernels for 0%

profile of v11, /device:TPU:31, one launch (start us, length us, event | category | flops | bytes accessed | tf_op | source)
XLA Modules:
  0.0 114.4 jit_solution(18233776516756075033)
XLA Ops:
  0.0 0.9 fusion.6
  0.9 0.2 fusion.8
  1.2 1.5 %fusion.1.merged_ref = bf16[64,32,64]{2,1,0:T(8,128)(2,1)S(1)} fusion(bf16[64,32,64]{2,1,0:T(8,128)(2,1)} %param.6, bf16[64,32,64]{2,1,0:T(8,128)(2,1)} %param.5, f32[64,32]{1,0:T(8,128)S(1)} %fusion.8), kind=kLoop, calls=%fused_computation.3 | loop fusion | flops 786432 | bytes 794624 | tf_op jit(solution)/shard_map/convert_element_type | solution.py:186
  2.7 0.0 copy-start
  2.8 0.1 copy.20
  2.9 13.8 %collective-permute-start = (bf16[32,32,64]{2,0,1:T(8,128)(2,1)S(1)}, bf16[32,32,64]{2,0,1:T(8,128)(2,1)S(1)}, u32[]{:S(2)}, u32[]{:S(2)}) collective-permute-start(bf16[32,32,64]{2,0,1:T(8,128)(2,1)S(1)} %bitcast.31), channel_id=1, source_target_pairs={{0,0},{1,1},{2,32},{3,33},{4,64},{5,65},{6,96},{7,97},{8,128},{9,1... | collective-permute-start | bytes 393224 | tf_op jit(solution)/shard_map/ppermute | solution.py:199
  16.7 0.1 copy.19
  16.8 1.9 %collective-permute-start.1 = (bf16[32,32,64]{2,0,1:T(8,128)(2,1)S(1)}, bf16[32,32,64]{2,0,1:T(8,128)(2,1)S(1)}, u32[]{:S(2)}, u32[]{:S(2)}) collective-permute-start(bf16[32,32,64]{2,0,1:T(8,128)(2,1)S(1)} %bitcast.32), channel_id=1, source_target_pairs={{0,1},{1,0},{2,33},{3,32},{4,65},{5,64},{6,97},{7,96},{8,129},{9,1... | collective-permute-start | bytes 393224 | tf_op jit(solution)/shard_map/ppermute | solution.py:199
  18.8 21.9 %collective-permute-done = bf16[32,32,64]{2,0,1:T(8,128)(2,1)S(1)} collective-permute-done((bf16[32,32,64]{2,0,1:T(8,128)(2,1)S(1)}, bf16[32,32,64]{2,0,1:T(8,128)(2,1)S(1)}, u32[]{:S(2)}, u32[]{:S(2)}) %collective-permute-start) | collective-permute-done | bytes 131104 | tf_op jit(solution)/shard_map/ppermute | solution.py:199
  40.7 15.6 %collective-permute-done.1 = bf16[32,32,64]{2,0,1:T(8,128)(2,1)S(1)} collective-permute-done((bf16[32,32,64]{2,0,1:T(8,128)(2,1)S(1)}, bf16[32,32,64]{2,0,1:T(8,128)(2,1)S(1)}, u32[]{:S(2)}, u32[]{:S(2)}) %collective-permute-start.1) | collective-permute-done | bytes 131104 | tf_op jit(solution)/shard_map/ppermute | solution.py:199
  56.3 0.3 fusion.5
  56.6 0.9 pad_maximum_fusion
  57.5 0.0 copy-start.4
  57.5 0.0 copy-done
  57.6 0.1 pad_maximum_fusion.1
  57.6 1.9 %collective-permute-start.2 = (bf16[14,2,32,64]{3,2,1,0:T(8,128)(2,1)S(1)}, bf16[14,2,32,64]{3,2,1,0:T(8,128)(2,1)S(1)}, u32[]{:S(2)}, u32[]{:S(2)}) collective-permute-start(bf16[14,2,32,64]{3,2,1,0:T(8,128)(2,1)S(1)} %pad_maximum_fusion.2), channel_id=1, source_target_pairs={{0,32},{32,64},{64,96},{96,128},{128,160},{160,192},{192,224},{224... | collective-permute-start | bytes 344072 | tf_op jit(solution)/shard_map/ppermute | solution.py:162
  59.5 8.9 %collective-permute-start.3 = (bf16[15,2,32,64]{3,2,1,0:T(8,128)(2,1)S(1)}, bf16[15,2,32,64]{3,2,1,0:T(8,128)(2,1)S(1)}, u32[]{:S(2)}, u32[]{:S(2)}) collective-permute-start(bf16[15,2,32,64]{3,2,1,0:T(8,128)(2,1)S(1)} %pad_maximum_fusion.1), channel_id=1, source_target_pairs={{32,0},{64,32},{96,64},{128,96},{160,128},{192,160},{224,192},{256... | collective-permute-start | bytes 368648 | tf_op jit(solution)/shard_map/ppermute | solution.py:163
  68.5 0.0 copy-done.4
  68.5 0.5 slice_bitcast_fusion
  69.0 0.0 collective-permute-done.2.left_ref
  69.0 0.0 copy-start.3
  69.0 4.2 %collective-permute-done.3.right_ref = bf16[15,2,32,64]{3,2,1,0:T(8,128)(2,1)S(1)} collective-permute-done((bf16[15,2,32,64]{3,2,1,0:T(8,128)(2,1)S(1)}, bf16[15,2,32,64]{3,2,1,0:T(8,128)(2,1)S(1)}, u32[]{:S(2)}, u32[]{:S(2)}) %collective-permute-start.3) | collective-permute-done | bytes 122912 | tf_op jit(solution)/shard_map/ppermute | solution.py:163
  73.2 0.0 copy-start.2
  73.2 0.0 copy-done.3
  73.2 0.7 copy-done.2
  73.9 3.8 %shard_map.55 = (f32[73,32,64]{2,1,0:T(8,128)}, f32[73,14,64]{2,1,0:T(8,128)}, f32[73,15,64]{2,1,0:T(8,128)}) custom-call(s32[1,1,64]{2,1,0:T(1,128)} %get-tuple-element.17.depth_ref.src_depth_ref, bf16[14,2,32,64]{3,2,1,0:T(8,128)(2,1)} %copy-done.3, bf16[64,32,64]{2,1,0:T(8,128)(2,1)} %copy-done, bf16[64,32,64]{2,1,0:T(8,128)(2,1)} %get-tuple-element.11.mirror_ref, ...), custom_call_target="tpu_custom_call" | custom-call | tf_op jit(solution)/shard_map/pallas_call | solution.py:144
  77.7 0.0 copy-start.1
  77.7 1.4 %copy.13 = f32[73,15,64]{0,2,1:T(8,128)S(1)} copy(f32[73,15,64]{2,1,0:T(8,128)} %get-tuple-element.10) | data formatting | bytes 560640 | tf_op jit(solution)/shard_map/pallas_call | solution.py:144
  79.1 13.2 %collective-permute-start.5 = (f32[73,15,64]{0,2,1:T(8,128)S(1)}, f32[73,15,64]{0,2,1:T(8,128)S(1)}, u32[]{:S(2)}, u32[]{:S(2)}) collective-permute-start(f32[73,15,64]{0,2,1:T(8,128)S(1)} %copy.13), channel_id=1, source_target_pairs={{1,0},{2,1},{3,2},{4,3},{5,4},{6,5},{7,6},{8,7},{9,8},{10,9},{11,1... | collective-permute-start | bytes 840968 | tf_op jit(solution)/shard_map/ppermute | solution.py:163
  92.3 0.0 copy-done.1
  92.3 0.3 copy.12
  92.6 1.9 %collective-permute-start.4 = (f32[73,14,64]{0,2,1:T(8,128)S(1)}, f32[73,14,64]{0,2,1:T(8,128)S(1)}, u32[]{:S(2)}, u32[]{:S(2)}) collective-permute-start(f32[73,14,64]{0,2,1:T(8,128)S(1)} %copy.12), channel_id=1, source_target_pairs={{0,1},{1,2},{2,3},{3,4},{4,5},{5,6},{6,7},{7,8},{8,9},{9,10},{10,1... | collective-permute-start | bytes 784904 | tf_op jit(solution)/shard_map/ppermute | solution.py:162
  94.5 9.4 %collective-permute-done.4 = f32[73,14,64]{0,2,1:T(8,128)S(1)} collective-permute-done((f32[73,14,64]{0,2,1:T(8,128)S(1)}, f32[73,14,64]{0,2,1:T(8,128)S(1)}, u32[]{:S(2)}, u32[]{:S(2)}) %collective-permute-start.4) | collective-permute-done | bytes 261664 | tf_op jit(solution)/shard_map/ppermute | solution.py:162
  103.9 1.1 copy.14.left_ref
  105.0 0.0 collective-permute-done.5
  105.0 1.1 copy.15.right_ref
  106.1 8.3 %shard_map.56 = f32[64,32,64]{2,1,0:T(8,128)} custom-call(s32[1,1,64]{2,1,0:T(1,128)} %get-tuple-element.18.rcv_depth_ref, s32[1,1,64]{2,1,0:T(1,128)} %get-tuple-element.17.depth_ref.src_depth_ref, f32[1,1,64]{2,1,0:T(1,128)} %bitcast.33, f32[73,14,64]{2,1,0:T(8,128)} %copy.14.left_ref, f32[73,32,64]{2,1,0:T(8,128)} %get-tuple-element.9.mid_ref, ...), custom_call_target="tpu_custom_call" | custom-call | tf_op jit(solution)/shard_map/pallas_call | solution.py:144
  (4 shorter events, 0.1 us)
Async XLA Ops:
  2.7 54.8 %copy-start = (bf16[64,32,64]{2,1,0:T(8,128)(2,1)}, bf16[64,32,64]{2,1,0:T(8,128)(2,1)S(1)}, u32[]{:S(2)}) copy-start(bf16[64,32,64]{2,1,0:T(8,128)(2,1)S(1)} %fusion.1.merged_ref) | copy-start | bytes 786436
  2.9 37.8 %collective-permute-start = (bf16[32,32,64]{2,0,1:T(8,128)(2,1)S(1)}, bf16[32,32,64]{2,0,1:T(8,128)(2,1)S(1)}, u32[]{:S(2)}, u32[]{:S(2)}) collective-permute-start(bf16[32,32,64]{2,0,1:T(8,128)(2,1)S(1)} %bitcast.31), channel_id=1, source_target_pairs={{0,0},{1,1},{2,32},{3,33},{4,64},{5,65},{6,96},{7,97},{8,128},{9,1... | collective-permute-start | bytes 393224 | tf_op jit(solution)/shard_map/ppermute | solution.py:199
  16.8 39.5 %collective-permute-start.1 = (bf16[32,32,64]{2,0,1:T(8,128)(2,1)S(1)}, bf16[32,32,64]{2,0,1:T(8,128)(2,1)S(1)}, u32[]{:S(2)}, u32[]{:S(2)}) collective-permute-start(bf16[32,32,64]{2,0,1:T(8,128)(2,1)S(1)} %bitcast.32), channel_id=1, source_target_pairs={{0,1},{1,0},{2,33},{3,32},{4,65},{5,64},{6,97},{7,96},{8,129},{9,1... | collective-permute-start | bytes 393224 | tf_op jit(solution)/shard_map/ppermute | solution.py:199
  57.5 11.0 %copy-start.4 = (s32[2,64]{1,0:T(2,128)S(1)}, s32[2,64]{1,0:T(2,128)}, u32[]{:S(2)}) copy-start(s32[2,64]{1,0:T(2,128)} %param.8) | copy-start | bytes 1540
  57.6 11.4 %collective-permute-start.2 = (bf16[14,2,32,64]{3,2,1,0:T(8,128)(2,1)S(1)}, bf16[14,2,32,64]{3,2,1,0:T(8,128)(2,1)S(1)}, u32[]{:S(2)}, u32[]{:S(2)}) collective-permute-start(bf16[14,2,32,64]{3,2,1,0:T(8,128)(2,1)S(1)} %pad_maximum_fusion.2), channel_id=1, source_target_pairs={{0,32},{32,64},{64,96},{96,128},{128,160},{160,192},{192,224},{224... | collective-permute-start | bytes 344072 | tf_op jit(solution)/shard_map/ppermute | solution.py:162
  59.5 13.6 %collective-permute-start.3 = (bf16[15,2,32,64]{3,2,1,0:T(8,128)(2,1)S(1)}, bf16[15,2,32,64]{3,2,1,0:T(8,128)(2,1)S(1)}, u32[]{:S(2)}, u32[]{:S(2)}) collective-permute-start(bf16[15,2,32,64]{3,2,1,0:T(8,128)(2,1)S(1)} %pad_maximum_fusion.1), channel_id=1, source_target_pairs={{32,0},{64,32},{96,64},{128,96},{160,128},{192,160},{224,192},{256... | collective-permute-start | bytes 368648 | tf_op jit(solution)/shard_map/ppermute | solution.py:163
  69.0 4.2 %copy-start.3 = (bf16[14,2,32,64]{3,2,1,0:T(8,128)(2,1)}, bf16[14,2,32,64]{3,2,1,0:T(8,128)(2,1)S(1)}, u32[]{:S(2)}) copy-start(bf16[14,2,32,64]{3,2,1,0:T(8,128)(2,1)S(1)} %collective-permute-done.2.left_ref) | copy-start | bytes 344068
  73.2 0.7 copy-start.2
  77.7 14.6 %copy-start.1 = (f32[73,14,64]{2,1,0:T(8,128)S(1)}, f32[73,14,64]{2,1,0:T(8,128)}, u32[]{:S(2)}) copy-start(f32[73,14,64]{2,1,0:T(8,128)} %get-tuple-element.8) | copy-start | bytes 784900
  79.1 25.9 %collective-permute-start.5 = (f32[73,15,64]{0,2,1:T(8,128)S(1)}, f32[73,15,64]{0,2,1:T(8,128)S(1)}, u32[]{:S(2)}, u32[]{:S(2)}) collective-permute-start(f32[73,15,64]{0,2,1:T(8,128)S(1)} %copy.13), channel_id=1, source_target_pairs={{1,0},{2,1},{3,2},{4,3},{5,4},{6,5},{7,6},{8,7},{9,8},{10,9},{11,1... | collective-permute-start | bytes 840968 | tf_op jit(solution)/shard_map/ppermute | solution.py:163
  92.6 11.3 %collective-permute-start.4 = (f32[73,14,64]{0,2,1:T(8,128)S(1)}, f32[73,14,64]{0,2,1:T(8,128)S(1)}, u32[]{:S(2)}, u32[]{:S(2)}) collective-permute-start(f32[73,14,64]{0,2,1:T(8,128)S(1)} %copy.12), channel_id=1, source_target_pairs={{0,1},{1,2},{2,3},{3,4},{4,5},{5,6},{6,7},{7,8},{8,9},{9,10},{10,1... | collective-permute-start | bytes 784904 | tf_op jit(solution)/shard_map/ppermute | solution.py:162
